TPU v7x, 512 devices: a whole 4x8x8 slice. The times are simulated.
512 devices in a mesh: sta: 32 (over z, x), slab: 16 (over y, core).
Axes of the slice: x: 4, y: 8, z: 8, core: 2. Of those that a mesh axis runs over, the one named last changes fastest.
Arguments:
- green_fields: bfloat16 [2, 64, 256, 4096], P(None, 'sta', 'slab'), may hold values from -6 to 6
- pair_list: int32 [256, 2], replicated, may hold values from 0 to 63
- pair_values: float32 [2, 256], replicated, may hold values from -6 to 6
- noise_map: float32 [256, 4096], P('slab'), may hold values from 0.1 to 1
- wave_square: float32 [256, 4096], P('slab'), may hold values from 0.1 to 1.5
- station_cell: int32 [64], P('sta'), may hold values from 0 to 1048575
Outputs:
- adjoint_field: float32 [2, 64, 256, 4096], P(None, 'sta', 'slab')
Inputs may be any that keep to these rules, and one draw needn't show every extreme that they name: `pair_list`: pairs may repeat and may name one station twice; repeated entries add up. `station_cell`: index = depth layer * 64 * 64 + lateral index; stations may share a cell.
All inputs are finite; a program needn't handle non-finite values.
Results may differ from a plain program's by a relative error of at most 0.004.
Values may be sent and summed in bfloat16 or wider, within the bound.
No kernel may reach another device: no remote copies, remote signals or barrier semaphores. Data moves between devices by JAX's collectives and lax.ppermute only.
A program may use at most 64 MiB of HBM per device.

v0:
```python
import jax
import jax.numpy as jnp
from jax import lax
from jax.sharding import PartitionSpec as P

GY = 64
SWEEPS = 6


damping = 0.3
relaxation = 0.8
point_size = 2.0


def extended(block, sides, width):
    for axis, dim in sides:
        count = lax.axis_size(axis)
        forward = [(i, i + 1) for i in range(count - 1)]
        backward = [(target, source) for source, target in forward]
        low = lax.ppermute(
            lax.slice_in_dim(block, block.shape[dim] - width, None, axis=dim), axis, forward
        )
        high = lax.ppermute(lax.slice_in_dim(block, 0, width, axis=dim), axis, backward)
        block = jnp.concatenate([low, block, high], axis=dim)
    return block


def build_resid(pair_list, pair_values, count):
    labels = jnp.arange(count, dtype=jnp.int32)
    first = (pair_list[:, 0:1] == labels[None, :]).astype(jnp.float32)
    second = (pair_list[:, 1:2] == labels[None, :]).astype(jnp.float32)
    real_w = pair_values[0][:, None]
    imag_w = pair_values[1][:, None]
    highest = lax.Precision.HIGHEST
    resid_real = jnp.dot(
        first.T, real_w * second, precision=highest, preferred_element_type=jnp.float32
    ) + jnp.dot(second.T, real_w * first, precision=highest, preferred_element_type=jnp.float32)
    resid_imag = jnp.dot(
        first.T, imag_w * second, precision=highest, preferred_element_type=jnp.float32
    ) - jnp.dot(second.T, imag_w * first, precision=highest, preferred_element_type=jnp.float32)
    resid_real = resid_real.astype(jnp.bfloat16)
    resid_imag = resid_imag.astype(jnp.bfloat16)
    upper = jnp.concatenate([resid_real, -resid_imag], axis=1)
    lower = jnp.concatenate([resid_imag, resid_real], axis=1)
    return jnp.concatenate([upper, lower], axis=0)


def lateral(field, width_y):
    width = field.shape[-1]
    zeros_pad = [(0, 0)] * (field.ndim - 1)
    padded = jnp.pad(field, zeros_pad + [(width_y, width_y)])
    along_x = padded[..., :width] + padded[..., 2 * width_y :]
    column = jnp.arange(width, dtype=jnp.int32) % width_y
    stepped = jnp.pad(field, zeros_pad + [(1, 1)])
    left = stepped[..., :width] * (column != 0).astype(jnp.float32)
    right = stepped[..., 2:] * (column != width_y - 1).astype(jnp.float32)
    return along_x + left + right


def scales_from(wave):
    diag_real = 6.0 - wave
    denom = diag_real * diag_real + damping * wave * (damping * wave)
    return (relaxation * diag_real / denom, relaxation * damping * wave / denom)


def relax(padded, source, wave, scale_real, scale_imag, width_y):
    inner = padded[:, :, 1:-1]
    near = lateral(inner, width_y) + padded[:, :, :-2] + padded[:, :, 2:]
    real_in = inner[0]
    imag_in = inner[1]
    applied_real = 6.0 * real_in - near[0] - wave * (real_in - damping * imag_in)
    applied_imag = 6.0 * imag_in - near[1] - wave * (damping * real_in + imag_in)
    rest_real = source[0] - applied_real
    rest_imag = source[1] - applied_imag
    return jnp.stack(
        [
            real_in + scale_real * rest_real - scale_imag * rest_imag,
            imag_in + scale_real * rest_imag + scale_imag * rest_real,
        ]
    )


def local(green_fields, pair_list, pair_values, noise_map, wave_square, station_cell):
    owned = green_fields.shape[1]
    depth = green_fields.shape[2]
    cells = green_fields.shape[3]
    count = owned * lax.axis_size("sta")
    big = build_resid(pair_list, pair_values, count)
    pieces = lax.all_to_all(green_fields, "sta", split_axis=3, concat_axis=1, tiled=True)
    layout = pieces.shape
    flat = pieces.reshape(2 * layout[1], layout[2] * layout[3])
    mixed = jnp.dot(big, flat, preferred_element_type=jnp.float32).astype(jnp.bfloat16)
    moved = mixed.reshape(layout)
    adjoint = lax.all_to_all(moved, "sta", split_axis=1, concat_axis=3, tiled=True)
    offset = lax.axis_index("slab") * (depth * cells)
    flat_cells = jnp.arange(depth * cells, dtype=jnp.int32) + offset
    spot = (flat_cells[None, :] == station_cell[:, None]).astype(jnp.float32).reshape(
        owned, depth, cells
    ) * point_size
    source = noise_map[None, None] * adjoint.astype(jnp.float32)
    source = jnp.stack([source[0] + spot, source[1]])
    field = jnp.zeros((2, owned, depth, cells), jnp.float32)
    scale_real, scale_imag = scales_from(wave_square)
    for repeat in range(SWEEPS):
        padded = extended(field, (("slab", 2),), 1)
        field = relax(padded, source, wave_square, scale_real, scale_imag, GY)
    return field


def solution(mesh):
    placed = (P(None, "sta", "slab", None), P(), P(), P("slab", None), P("slab", None), P("sta"))
    return jax.shard_map(
        local, mesh=mesh, in_specs=placed, out_specs=P(None, "sta", "slab", None), check_vma=False
    )
```

profile of v0, /device:TPU:25, one launch (start us, length us, event | category | flops | bytes accessed | tf_op | source)
XLA Modules:
  0.0 151.4 jit_solution(14406352399546489876)
XLA Ops:
  0.0 5.0 %collective-permute-start = (f32[2,2,1,4096]{3,2,1,0:T(1,128)S(1)}, f32[2,2,1,4096]{3,2,1,0:T(1,128)S(1)}, u32[]{:S(2)}, u32[]{:S(2)}) collective-permute-start(f32[2,2,1,4096]{3,2,1,0:T(1,128)S(1)} %broadcast.574), channel_id=1, source_target_pairs={{0,1},{1,2},{2,3},{3,4},{4,5},{5,6},{6,7},{7,8},{8,9},{9,10},{10,1... | collective-permute-start | bytes 196616 | tf_op jit(solution)/shard_map/ppermute | solution.py:20
  5.0 1.9 %collective-permute-start.1 = (f32[2,2,1,4096]{3,2,1,0:T(1,128)S(1)}, f32[2,2,1,4096]{3,2,1,0:T(1,128)S(1)}, u32[]{:S(2)}, u32[]{:S(2)}) collective-permute-start(f32[2,2,1,4096]{3,2,1,0:T(1,128)S(1)} %broadcast.574), channel_id=1, source_target_pairs={{1,0},{2,1},{3,2},{4,3},{5,4},{6,5},{7,6},{8,7},{9,8},{10,9},{11,1... | collective-permute-start | bytes 196616 | tf_op jit(solution)/shard_map/ppermute | solution.py:23
  7.0 9.1 %copy.10 = bf16[2,2,16,4096]{2,1,0,3:T(2,128)(2,1)} copy(bf16[2,2,16,4096]{3,2,1,0:T(8,128)(2,1)} %param.6) | data formatting | bytes 1048576 | tf_op args[0]
  16.1 12.9 %reshape.92 = bf16[32,2,4096]{2,1,0:T(2,128)(2,1)} reshape(bf16[4096,2,2,16]{3,2,1,0:T(2,128)(2,1)} %bitcast.24) | data formatting | bytes 1048576
  29.0 13.0 %all-to-all-start = ((bf16[32,2,4096]{2,1,0:T(2,128)(2,1)}), bf16[32,2,4096]{2,1,0:T(2,128)(2,1)S(1)}, u32[]{:S(2)}, u32[]{:S(2)}) async-start(bf16[32,2,4096]{2,1,0:T(2,128)(2,1)} %reshape.92), calls=%async_computation | async-start | bytes 1048576 | tf_op jit(solution)/shard_map/all_to_all | solution.py:89
  43.8 15.6 %all-to-all-done = bf16[32,2,4096]{2,1,0:T(2,128)(2,1)S(1)} async-done(((bf16[32,2,4096]{2,1,0:T(2,128)(2,1)}), bf16[32,2,4096]{2,1,0:T(2,128)(2,1)S(1)}, u32[]{:S(2)}, u32[]{:S(2)}) %all-to-all-start) | async-done | bytes 524320 | tf_op jit(solution)/shard_map/all_to_all | solution.py:89
  59.4 4.1 %reshape.93 = bf16[4096,2,2,16]{3,2,1,0:T(2,128)(2,1)} reshape(bf16[32,2,4096]{2,1,0:T(2,128)(2,1)S(1)} %all-to-all-done) | data formatting | bytes 1048576
  63.5 8.3 %copy.11 = bf16[2,2,16,32,128]{4,2,1,3,0:T(8,128)(2,1)S(1)} copy(bf16[2,2,16,32,128]{2,1,0,4,3:T(2,128)(2,1)} %bitcast.23) | data formatting | bytes 1048576 | tf_op jit(solution)/shard_map/all_to_all | solution.py:89
  73.1 4.9 %all-to-all-start.1 = ((bf16[2,64,16,128]{3,2,0,1:T(8,128)(2,1)}), bf16[2,64,16,128]{3,2,0,1:T(8,128)(2,1)S(1)}, u32[]{:S(2)}, u32[]{:S(2)}) async-start(bf16[2,64,16,128]{3,2,0,1:T(8,128)(2,1)} %copy.12), calls=%async_computation.1 | async-start | bytes 1048576 | tf_op jit(solution)/shard_map/all_to_all | solution.py:94
  79.3 14.3 %all-to-all-done.1 = bf16[2,64,16,128]{3,2,0,1:T(8,128)(2,1)S(1)} async-done(((bf16[2,64,16,128]{3,2,0,1:T(8,128)(2,1)}), bf16[2,64,16,128]{3,2,0,1:T(8,128)(2,1)S(1)}, u32[]{:S(2)}, u32[]{:S(2)}) %all-to-all-start.1) | async-done | bytes 524320 | tf_op jit(solution)/shard_map/all_to_all | solution.py:94
  97.4 3.1 %collective-permute-start.2 = (f32[2,2,1,4096]{3,2,1,0:T(1,128)S(1)}, f32[2,2,1,4096]{3,2,1,0:T(1,128)S(1)}, u32[]{:S(2)}, u32[]{:S(2)}) collective-permute-start(f32[2,2,1,4096]{3,2,1,0:T(1,128)S(1)} %get-tuple-element.25), channel_id=1, source_target_pairs={{0,1},{1,2},{2,3},{3,4},{4,5},{5,6},{6,7},{7,8},{8,9},{9,10},{10,1... | collective-permute-start | bytes 196616 | tf_op jit(solution)/shard_map/ppermute | solution.py:20
  100.5 4.0 %collective-permute-start.3 = (f32[2,2,1,4096]{3,2,1,0:T(1,128)S(1)}, f32[2,2,1,4096]{3,2,1,0:T(1,128)S(1)}, u32[]{:S(2)}, u32[]{:S(2)}) collective-permute-start(f32[2,2,1,4096]{3,2,1,0:T(1,128)S(1)} %get-tuple-element.26), channel_id=1, source_target_pairs={{1,0},{2,1},{3,2},{4,3},{5,4},{6,5},{7,6},{8,7},{9,8},{10,9},{11,1... | collective-permute-start | bytes 196616 | tf_op jit(solution)/shard_map/ppermute | solution.py:23
  104.6 2.7 %collective-permute-done.3 = f32[2,2,1,4096]{3,2,1,0:T(1,128)S(1)} collective-permute-done((f32[2,2,1,4096]{3,2,1,0:T(1,128)S(1)}, f32[2,2,1,4096]{3,2,1,0:T(1,128)S(1)}, u32[]{:S(2)}, u32[]{:S(2)}) %collective-permute-start.3) | collective-permute-done | bytes 65568 | tf_op jit(solution)/shard_map/ppermute | solution.py:23
  109.0 1.9 %collective-permute-start.4 = (f32[2,2,1,4096]{3,2,1,0:T(1,128)S(1)}, f32[2,2,1,4096]{3,2,1,0:T(1,128)S(1)}, u32[]{:S(2)}, u32[]{:S(2)}) collective-permute-start(f32[2,2,1,4096]{3,2,1,0:T(1,128)S(1)} %get-tuple-element.23), channel_id=1, source_target_pairs={{0,1},{1,2},{2,3},{3,4},{4,5},{5,6},{6,7},{7,8},{8,9},{9,10},{10,1... | collective-permute-start | bytes 196616 | tf_op jit(solution)/shard_map/ppermute | solution.py:20
  110.9 2.5 %collective-permute-start.5 = (f32[2,2,1,4096]{3,2,1,0:T(1,128)S(1)}, f32[2,2,1,4096]{3,2,1,0:T(1,128)S(1)}, u32[]{:S(2)}, u32[]{:S(2)}) collective-permute-start(f32[2,2,1,4096]{3,2,1,0:T(1,128)S(1)} %get-tuple-element.24), channel_id=1, source_target_pairs={{1,0},{2,1},{3,2},{4,3},{5,4},{6,5},{7,6},{8,7},{9,8},{10,9},{11,1... | collective-permute-start | bytes 196616 | tf_op jit(solution)/shard_map/ppermute | solution.py:23
  113.6 4.2 %collective-permute-done.5 = f32[2,2,1,4096]{3,2,1,0:T(1,128)S(1)} collective-permute-done((f32[2,2,1,4096]{3,2,1,0:T(1,128)S(1)}, f32[2,2,1,4096]{3,2,1,0:T(1,128)S(1)}, u32[]{:S(2)}, u32[]{:S(2)}) %collective-permute-start.5) | collective-permute-done | bytes 65568 | tf_op jit(solution)/shard_map/ppermute | solution.py:23
  119.4 1.9 %collective-permute-start.6 = (f32[2,2,1,4096]{3,2,1,0:T(1,128)S(1)}, f32[2,2,1,4096]{3,2,1,0:T(1,128)S(1)}, u32[]{:S(2)}, u32[]{:S(2)}) collective-permute-start(f32[2,2,1,4096]{3,2,1,0:T(1,128)S(1)} %get-tuple-element.21), channel_id=1, source_target_pairs={{0,1},{1,2},{2,3},{3,4},{4,5},{5,6},{6,7},{7,8},{8,9},{9,10},{10,1... | collective-permute-start | bytes 196616 | tf_op jit(solution)/shard_map/ppermute | solution.py:20
  121.3 2.4 %collective-permute-start.7 = (f32[2,2,1,4096]{3,2,1,0:T(1,128)S(1)}, f32[2,2,1,4096]{3,2,1,0:T(1,128)S(1)}, u32[]{:S(2)}, u32[]{:S(2)}) collective-permute-start(f32[2,2,1,4096]{3,2,1,0:T(1,128)S(1)} %get-tuple-element.22), channel_id=1, source_target_pairs={{1,0},{2,1},{3,2},{4,3},{5,4},{6,5},{7,6},{8,7},{9,8},{10,9},{11,1... | collective-permute-start | bytes 196616 | tf_op jit(solution)/shard_map/ppermute | solution.py:23
  123.8 4.3 %collective-permute-done.7 = f32[2,2,1,4096]{3,2,1,0:T(1,128)S(1)} collective-permute-done((f32[2,2,1,4096]{3,2,1,0:T(1,128)S(1)}, f32[2,2,1,4096]{3,2,1,0:T(1,128)S(1)}, u32[]{:S(2)}, u32[]{:S(2)}) %collective-permute-start.7) | collective-permute-done | bytes 65568 | tf_op jit(solution)/shard_map/ppermute | solution.py:23
  131.6 2.4 %collective-permute-start.9 = (f32[2,2,1,4096]{3,2,1,0:T(1,128)S(1)}, f32[2,2,1,4096]{3,2,1,0:T(1,128)S(1)}, u32[]{:S(2)}, u32[]{:S(2)}) collective-permute-start(f32[2,2,1,4096]{3,2,1,0:T(1,128)S(1)} %get-tuple-element.20), channel_id=1, source_target_pairs={{1,0},{2,1},{3,2},{4,3},{5,4},{6,5},{7,6},{8,7},{9,8},{10,9},{11,1... | collective-permute-start | bytes 196616 | tf_op jit(solution)/shard_map/ppermute | solution.py:23
  134.2 4.3 %collective-permute-done.9 = f32[2,2,1,4096]{3,2,1,0:T(1,128)S(1)} collective-permute-done((f32[2,2,1,4096]{3,2,1,0:T(1,128)S(1)}, f32[2,2,1,4096]{3,2,1,0:T(1,128)S(1)}, u32[]{:S(2)}, u32[]{:S(2)}) %collective-permute-start.9) | collective-permute-done | bytes 65568 | tf_op jit(solution)/shard_map/ppermute | solution.py:23
  140.1 1.9 %collective-permute-start.10 = (f32[2,2,1,4096]{3,2,1,0:T(1,128)S(1)}, f32[2,2,1,4096]{3,2,1,0:T(1,128)S(1)}, u32[]{:S(2)}, u32[]{:S(2)}) collective-permute-start(f32[2,2,1,4096]{3,2,1,0:T(1,128)S(1)} %get-tuple-element.17), channel_id=1, source_target_pairs={{0,1},{1,2},{2,3},{3,4},{4,5},{5,6},{6,7},{7,8},{8,9},{9,10},{10,1... | collective-permute-start | bytes 196616 | tf_op jit(solution)/shard_map/ppermute | solution.py:20
  142.0 2.4 %collective-permute-start.11 = (f32[2,2,1,4096]{3,2,1,0:T(1,128)S(1)}, f32[2,2,1,4096]{3,2,1,0:T(1,128)S(1)}, u32[]{:S(2)}, u32[]{:S(2)}) collective-permute-start(f32[2,2,1,4096]{3,2,1,0:T(1,128)S(1)} %get-tuple-element.18), channel_id=1, source_target_pairs={{1,0},{2,1},{3,2},{4,3},{5,4},{6,5},{7,6},{8,7},{9,8},{10,9},{11,1... | collective-permute-start | bytes 196616 | tf_op jit(solution)/shard_map/ppermute | solution.py:23
  144.5 4.3 %collective-permute-done.11 = f32[2,2,1,4096]{3,2,1,0:T(1,128)S(1)} collective-permute-done((f32[2,2,1,4096]{3,2,1,0:T(1,128)S(1)}, f32[2,2,1,4096]{3,2,1,0:T(1,128)S(1)}, u32[]{:S(2)}, u32[]{:S(2)}) %collective-permute-start.11) | collective-permute-done | bytes 65568 | tf_op jit(solution)/shard_map/ppermute | solution.py:23
  (58 shorter events, 19.4 us)
Async XLA Ops:
  0.0 78.0 %collective-permute-start = (f32[2,2,1,4096]{3,2,1,0:T(1,128)S(1)}, f32[2,2,1,4096]{3,2,1,0:T(1,128)S(1)}, u32[]{:S(2)}, u32[]{:S(2)}) collective-permute-start(f32[2,2,1,4096]{3,2,1,0:T(1,128)S(1)} %broadcast.574), channel_id=1, source_target_pairs={{0,1},{1,2},{2,3},{3,4},{4,5},{5,6},{6,7},{7,8},{8,9},{9,10},{10,1... | collective-permute-start | bytes 196616 | tf_op jit(solution)/shard_map/ppermute | solution.py:20
  5.0 73.0 %collective-permute-start.1 = (f32[2,2,1,4096]{3,2,1,0:T(1,128)S(1)}, f32[2,2,1,4096]{3,2,1,0:T(1,128)S(1)}, u32[]{:S(2)}, u32[]{:S(2)}) collective-permute-start(f32[2,2,1,4096]{3,2,1,0:T(1,128)S(1)} %broadcast.574), channel_id=1, source_target_pairs={{1,0},{2,1},{3,2},{4,3},{5,4},{6,5},{7,6},{8,7},{9,8},{10,9},{11,1... | collective-permute-start | bytes 196616 | tf_op jit(solution)/shard_map/ppermute | solution.py:23
  16.1 26.0 %copy-start.1 = (s32[256,2]{0,1:T(2,128)S(1)}, s32[256,2]{0,1:T(2,128)}, u32[]{:S(2)}) copy-start(s32[256,2]{0,1:T(2,128)} %param.7) | copy-start | bytes 6148
  16.1 26.0 %copy-start.2 = (f32[2,256]{1,0:T(2,128)S(1)}, f32[2,256]{1,0:T(2,128)}, u32[]{:S(2)}) copy-start(f32[2,256]{1,0:T(2,128)} %param.8) | copy-start | bytes 6148
  29.0 14.7 %copy-start = (f32[16,4096]{1,0:T(8,128)S(1)}, f32[16,4096]{1,0:T(8,128)}, u32[]{:S(2)}) copy-start(f32[16,4096]{1,0:T(8,128)} %param.10) | copy-start | bytes 786436
  29.0 30.4 %all-to-all-start = ((bf16[32,2,4096]{2,1,0:T(2,128)(2,1)}), bf16[32,2,4096]{2,1,0:T(2,128)(2,1)S(1)}, u32[]{:S(2)}, u32[]{:S(2)}) async-start(bf16[32,2,4096]{2,1,0:T(2,128)(2,1)} %reshape.92), calls=%async_computation | async-start | bytes 1048576 | tf_op jit(solution)/shard_map/all_to_all | solution.py:89
  73.1 20.5 %all-to-all-start.1 = ((bf16[2,64,16,128]{3,2,0,1:T(8,128)(2,1)}), bf16[2,64,16,128]{3,2,0,1:T(8,128)(2,1)S(1)}, u32[]{:S(2)}, u32[]{:S(2)}) async-start(bf16[2,64,16,128]{3,2,0,1:T(8,128)(2,1)} %copy.12), calls=%async_computation.1 | async-start | bytes 1048576 | tf_op jit(solution)/shard_map/all_to_all | solution.py:94
  95.5 1.4 copy-start.3
  97.4 7.2 %collective-permute-start.2 = (f32[2,2,1,4096]{3,2,1,0:T(1,128)S(1)}, f32[2,2,1,4096]{3,2,1,0:T(1,128)S(1)}, u32[]{:S(2)}, u32[]{:S(2)}) collective-permute-start(f32[2,2,1,4096]{3,2,1,0:T(1,128)S(1)} %get-tuple-element.25), channel_id=1, source_target_pairs={{0,1},{1,2},{2,3},{3,4},{4,5},{5,6},{6,7},{7,8},{8,9},{9,10},{10,1... | collective-permute-start | bytes 196616 | tf_op jit(solution)/shard_map/ppermute | solution.py:20
  100.5 6.8 %collective-permute-start.3 = (f32[2,2,1,4096]{3,2,1,0:T(1,128)S(1)}, f32[2,2,1,4096]{3,2,1,0:T(1,128)S(1)}, u32[]{:S(2)}, u32[]{:S(2)}) collective-permute-start(f32[2,2,1,4096]{3,2,1,0:T(1,128)S(1)} %get-tuple-element.26), channel_id=1, source_target_pairs={{1,0},{2,1},{3,2},{4,3},{5,4},{6,5},{7,6},{8,7},{9,8},{10,9},{11,1... | collective-permute-start | bytes 196616 | tf_op jit(solution)/shard_map/ppermute | solution.py:23
  109.0 4.6 %collective-permute-start.4 = (f32[2,2,1,4096]{3,2,1,0:T(1,128)S(1)}, f32[2,2,1,4096]{3,2,1,0:T(1,128)S(1)}, u32[]{:S(2)}, u32[]{:S(2)}) collective-permute-start(f32[2,2,1,4096]{3,2,1,0:T(1,128)S(1)} %get-tuple-element.23), channel_id=1, source_target_pairs={{0,1},{1,2},{2,3},{3,4},{4,5},{5,6},{6,7},{7,8},{8,9},{9,10},{10,1... | collective-permute-start | bytes 196616 | tf_op jit(solution)/shard_map/ppermute | solution.py:20
  110.9 6.8 %collective-permute-start.5 = (f32[2,2,1,4096]{3,2,1,0:T(1,128)S(1)}, f32[2,2,1,4096]{3,2,1,0:T(1,128)S(1)}, u32[]{:S(2)}, u32[]{:S(2)}) collective-permute-start(f32[2,2,1,4096]{3,2,1,0:T(1,128)S(1)} %get-tuple-element.24), channel_id=1, source_target_pairs={{1,0},{2,1},{3,2},{4,3},{5,4},{6,5},{7,6},{8,7},{9,8},{10,9},{11,1... | collective-permute-start | bytes 196616 | tf_op jit(solution)/shard_map/ppermute | solution.py:23
  119.4 4.4 %collective-permute-start.6 = (f32[2,2,1,4096]{3,2,1,0:T(1,128)S(1)}, f32[2,2,1,4096]{3,2,1,0:T(1,128)S(1)}, u32[]{:S(2)}, u32[]{:S(2)}) collective-permute-start(f32[2,2,1,4096]{3,2,1,0:T(1,128)S(1)} %get-tuple-element.21), channel_id=1, source_target_pairs={{0,1},{1,2},{2,3},{3,4},{4,5},{5,6},{6,7},{7,8},{8,9},{9,10},{10,1... | collective-permute-start | bytes 196616 | tf_op jit(solution)/shard_map/ppermute | solution.py:20
  121.3 6.8 %collective-permute-start.7 = (f32[2,2,1,4096]{3,2,1,0:T(1,128)S(1)}, f32[2,2,1,4096]{3,2,1,0:T(1,128)S(1)}, u32[]{:S(2)}, u32[]{:S(2)}) collective-permute-start(f32[2,2,1,4096]{3,2,1,0:T(1,128)S(1)} %get-tuple-element.22), channel_id=1, source_target_pairs={{1,0},{2,1},{3,2},{4,3},{5,4},{6,5},{7,6},{8,7},{9,8},{10,9},{11,1... | collective-permute-start | bytes 196616 | tf_op jit(solution)/shard_map/ppermute | solution.py:23
  129.7 4.4 %collective-permute-start.8 = (f32[2,2,1,4096]{3,2,1,0:T(1,128)S(1)}, f32[2,2,1,4096]{3,2,1,0:T(1,128)S(1)}, u32[]{:S(2)}, u32[]{:S(2)}) collective-permute-start(f32[2,2,1,4096]{3,2,1,0:T(1,128)S(1)} %get-tuple-element.19), channel_id=1, source_target_pairs={{0,1},{1,2},{2,3},{3,4},{4,5},{5,6},{6,7},{7,8},{8,9},{9,10},{10,1... | collective-permute-start | bytes 196616 | tf_op jit(solution)/shard_map/ppermute | solution.py:20
  131.6 6.8 %collective-permute-start.9 = (f32[2,2,1,4096]{3,2,1,0:T(1,128)S(1)}, f32[2,2,1,4096]{3,2,1,0:T(1,128)S(1)}, u32[]{:S(2)}, u32[]{:S(2)}) collective-permute-start(f32[2,2,1,4096]{3,2,1,0:T(1,128)S(1)} %get-tuple-element.20), channel_id=1, source_target_pairs={{1,0},{2,1},{3,2},{4,3},{5,4},{6,5},{7,6},{8,7},{9,8},{10,9},{11,1... | collective-permute-start | bytes 196616 | tf_op jit(solution)/shard_map/ppermute | solution.py:23
  140.1 4.4 %collective-permute-start.10 = (f32[2,2,1,4096]{3,2,1,0:T(1,128)S(1)}, f32[2,2,1,4096]{3,2,1,0:T(1,128)S(1)}, u32[]{:S(2)}, u32[]{:S(2)}) collective-permute-start(f32[2,2,1,4096]{3,2,1,0:T(1,128)S(1)} %get-tuple-element.17), channel_id=1, source_target_pairs={{0,1},{1,2},{2,3},{3,4},{4,5},{5,6},{6,7},{7,8},{8,9},{9,10},{10,1... | collective-permute-start | bytes 196616 | tf_op jit(solution)/shard_map/ppermute | solution.py:20
  142.0 6.8 %collective-permute-start.11 = (f32[2,2,1,4096]{3,2,1,0:T(1,128)S(1)}, f32[2,2,1,4096]{3,2,1,0:T(1,128)S(1)}, u32[]{:S(2)}, u32[]{:S(2)}) collective-permute-start(f32[2,2,1,4096]{3,2,1,0:T(1,128)S(1)} %get-tuple-element.18), channel_id=1, source_target_pairs={{1,0},{2,1},{3,2},{4,3},{5,4},{6,5},{7,6},{8,7},{9,8},{10,9},{11,1... | collective-permute-start | bytes 196616 | tf_op jit(solution)/shard_map/ppermute | solution.py:23
where the time goes:
time: 153 us; the launch traced here: 151 us
  waiting for transfers between devices  49.7 us (32%)
  starting transfers between devices  49.4 us (32%)
  local copies, waits for them, and re-layouts  37.3 us (24%)
  other arithmetic  12.7 us (8%)
  matrix products  1.88 us (1%)
    unnamed x12, local copies, waits for them, and re-layouts  26.2 us
    ppermute x6, waiting for transfers between devices, extended(): lax.ppermute(lax.slice_in_dim(block, 0, width, axis=dim), axis, backward)  19.7 us
    ppermute x6, starting transfers between devices, extended(): lax.ppermute(lax.slice_in_dim(block, block.shape[dim] - width, None, axis...  15.8 us
    ppermute x6, starting transfers between devices, extended(): lax.ppermute(lax.slice_in_dim(block, 0, width, axis=dim), axis, backward)  15.7 us
    all_to_all x1, waiting for transfers between devices, local(): lax.all_to_all(green_fields, 'sta', split_axis=3, concat_axis=1, tiled=True)  15.6 us
    all_to_all x1, waiting for transfers between devices, local(): lax.all_to_all(moved, 'sta', split_axis=1, concat_axis=3, tiled=True)  14.3 us
    all_to_all x1, starting transfers between devices, local(): lax.all_to_all(green_fields, 'sta', split_axis=3, concat_axis=1, tiled=True)  13 us
    all_to_all x1, local copies, waits for them, and re-layouts, local(): lax.all_to_all(green_fields, 'sta', split_axis=3, concat_axis=1, tiled=True)  8.35 us
  transfers between devices with their start and end apart: 14, of which 7 were waited for; matrix products, arithmetic and copies ran while one was open for 26% of the time, Pallas kernels for 0%

commit v1 on v0

v1 whole, which is shorter than its diff:
```python
import functools

import jax
import jax.numpy as jnp
from jax import lax
from jax.experimental import pallas as pl
from jax.experimental.pallas import tpu as pltpu
from jax.sharding import PartitionSpec as P

GY = 64
SWEEPS = 6
HALO = 8

damping = 0.3
relaxation = 0.8
point_size = 2.0


def build_resid(pair_list, pair_values, count):
    labels = jnp.arange(count, dtype=jnp.int32)
    first = (pair_list[:, 0:1] == labels[None, :]).astype(jnp.float32)
    second = (pair_list[:, 1:2] == labels[None, :]).astype(jnp.float32)
    real_w = pair_values[0][:, None]
    imag_w = pair_values[1][:, None]
    highest = lax.Precision.HIGHEST
    resid_real = jnp.dot(
        first.T, real_w * second, precision=highest, preferred_element_type=jnp.float32
    ) + jnp.dot(second.T, real_w * first, precision=highest, preferred_element_type=jnp.float32)
    resid_imag = jnp.dot(
        first.T, imag_w * second, precision=highest, preferred_element_type=jnp.float32
    ) - jnp.dot(second.T, imag_w * first, precision=highest, preferred_element_type=jnp.float32)
    resid_real = resid_real.astype(jnp.bfloat16)
    resid_imag = resid_imag.astype(jnp.bfloat16)
    upper = jnp.concatenate([resid_real, -resid_imag], axis=1)
    lower = jnp.concatenate([resid_imag, resid_real], axis=1)
    return jnp.concatenate([upper, lower], axis=0)


def mix_kernel(depth, big_ref, recv_ref, out_ref, wide_ref, acc_ref):
    wide_ref[...] = recv_ref[...].astype(jnp.float32)
    big = big_ref[...]
    rows = big.shape[0]
    for r in range(depth):
        rhs = wide_ref[pl.ds(r, rows, stride=depth), :].astype(jnp.bfloat16)
        acc_ref[pl.ds(r, rows, stride=depth), :] = jnp.dot(
            big, rhs, preferred_element_type=jnp.float32
        )
    out_ref[...] = acc_ref[...].astype(out_ref.dtype)


def mix(big, recv, depth):
    total, lanes = recv.shape
    return pl.pallas_call(
        functools.partial(mix_kernel, depth),
        out_shape=jax.ShapeDtypeStruct((total, lanes), jnp.bfloat16),
        scratch_shapes=[
            pltpu.VMEM((total, lanes), jnp.float32),
            pltpu.VMEM((total, lanes), jnp.float32),
        ],
        cost_estimate=pl.CostEstimate(
            flops=2 * big.shape[0] * big.shape[1] * depth * lanes,
            bytes_accessed=4 * total * lanes,
            transcendentals=0,
        ),
    )(big, recv)


def source_kernel(owned, depth, meta_ref, recv_ref, noise_ref, lo_ref, hi_ref):
    pieces, _, lanes = recv_ref.shape
    half = depth // 2
    slab = meta_ref[0]
    row = lax.broadcasted_iota(jnp.int32, (depth, lanes), 0)
    lane = lax.broadcasted_iota(jnp.int32, (depth, lanes), 1)
    base = (slab * depth + row) * (pieces * lanes) + lane
    for b in range(owned):
        spot_at = meta_ref[2 + b]
        for part in range(2):
            start = (b * 2 + part) * depth
            for ct in range(pieces):
                cols = slice(ct * lanes, (ct + 1) * lanes)
                tile = recv_ref[ct, start : start + depth, :].astype(jnp.float32)
                value = noise_ref[:, cols] * tile
                if part == 0:
                    hit = base + ct * lanes == spot_at
                    value = value + jnp.where(hit, point_size, 0.0)
                lo_ref[b, part, :, cols] = value[:half]
                hi_ref[b, part, :, cols] = value[half:]


def sweep_kernel(depth, meta_ref, lo_ref, hi_ref, below_ref, above_ref, wave_ref, wbelow_ref,
                 wabove_ref, out_ref, re_ref, im_ref, sre_ref, sim_ref, w_ref, sr_ref, si_ref):
    half = depth // 2
    rows, cells = re_ref.shape
    slab = meta_ref[0]
    nslab = meta_ref[1]
    w_ref[0:HALO] = wbelow_ref[...]
    w_ref[HALO : HALO + depth] = wave_ref[...]
    w_ref[HALO + depth :] = wabove_ref[...]
    for part, dst in ((0, sre_ref), (1, sim_ref)):
        dst[0:HALO] = below_ref[0, part]
        dst[HALO : HALO + half] = lo_ref[0, part]
        dst[HALO + half : HALO + depth] = hi_ref[0, part]
        dst[HALO + depth :] = above_ref[0, part]
    wave = w_ref[...]
    row = lax.broadcasted_iota(jnp.int32, (rows, cells), 0)
    inside = jnp.logical_and(
        jnp.logical_or(row >= HALO, slab > 0),
        jnp.logical_or(row < HALO + depth, slab < nslab - 1),
    )
    diag_real = 6.0 - wave
    denom = diag_real * diag_real + damping * wave * (damping * wave)
    sr_ref[...] = jnp.where(inside, relaxation * diag_real / denom, 0.0)
    si_ref[...] = jnp.where(inside, relaxation * damping * wave / denom, 0.0)
    sr = sr_ref[...]
    si = si_ref[...]
    src_re = sre_ref[...]
    src_im = sim_ref[...]
    re_ref[...] = sr * src_re - si * src_im
    im_ref[...] = sr * src_im + si * src_re

    def near(f, lane):
        col = lane % GY
        xm = jnp.where(lane >= GY, pltpu.roll(f, GY, 1), 0.0)
        xp = jnp.where(lane < cells - GY, pltpu.roll(f, cells - GY, 1), 0.0)
        ym = jnp.where(col != 0, pltpu.roll(f, 1, 1), 0.0)
        yp = jnp.where(col != GY - 1, pltpu.roll(f, cells - 1, 1), 0.0)
        dn = pltpu.roll(f, 1, 0)
        up = pltpu.roll(f, rows - 1, 0)
        return xm + xp + ym + yp + dn + up

    def body(_, carry):
        lane = lax.broadcasted_iota(jnp.int32, (rows, cells), 1)
        re = re_ref[...]
        im = im_ref[...]
        w = w_ref[...]
        near_re = near(re, lane)
        near_im = near(im, lane)
        applied_re = 6.0 * re - near_re - w * (re - damping * im)
        applied_im = 6.0 * im - near_im - w * (damping * re + im)
        rest_re = sre_ref[...] - applied_re
        rest_im = sim_ref[...] - applied_im
        s_r = sr_ref[...]
        s_i = si_ref[...]
        re_ref[...] = re + s_r * rest_re - s_i * rest_im
        im_ref[...] = im + s_r * rest_im + s_i * rest_re
        return carry

    lax.fori_loop(0, SWEEPS - 1, body, 0)
    out_ref[0, 0] = re_ref[HALO : HALO + depth]
    out_ref[1, 0] = im_ref[HALO : HALO + depth]


def sweeps(meta, lo, hi, below, above, wave, wbelow, wabove):
    owned, _, half, cells = lo.shape
    depth = 2 * half
    rows = depth + 2 * HALO
    piece = pl.BlockSpec((1, 2, half, cells), lambda b, *_: (b, 0, 0, 0))
    halo = pl.BlockSpec((1, 2, HALO, cells), lambda b, *_: (b, 0, 0, 0))
    whole = lambda shape: pl.BlockSpec(shape, lambda b, *_: (0,) * len(shape))
    grid_spec = pltpu.PrefetchScalarGridSpec(
        num_scalar_prefetch=1,
        grid=(owned,),
        in_specs=[piece, piece, halo, halo, whole((depth, cells)), whole((HALO, cells)),
                  whole((HALO, cells))],
        out_specs=pl.BlockSpec((2, 1, depth, cells), lambda b, *_: (0, b, 0, 0)),
        scratch_shapes=[pltpu.VMEM((rows, cells), jnp.float32) for _ in range(7)],
    )
    return pl.pallas_call(
        functools.partial(sweep_kernel, depth),
        out_shape=jax.ShapeDtypeStruct((2, owned, depth, cells), jnp.float32),
        grid_spec=grid_spec,
        cost_estimate=pl.CostEstimate(
            flops=owned * SWEEPS * 90 * rows * cells,
            bytes_accessed=owned * 4 * cells * (6 * depth),
            transcendentals=0,
        ),
    )(meta, lo, hi, below, above, wave, wbelow, wabove)


def local(green_fields, pair_list, pair_values, noise_map, wave_square, station_cell):
    parts, owned, depth, cells = green_fields.shape
    nsta = lax.axis_size("sta")
    nslab = lax.axis_size("slab")
    count = owned * nsta
    lanes = cells // nsta
    slab = lax.axis_index("slab")
    up_pairs = [(i, i + 1) for i in range(nslab - 1)]
    down_pairs = [(i + 1, i) for i in range(nslab - 1)]
    half = depth // 2

    wbelow = lax.ppermute(wave_square[depth - HALO :], "slab", up_pairs)
    wabove = lax.ppermute(wave_square[:HALO], "slab", down_pairs)

    send = green_fields.reshape(parts, owned, depth, nsta, lanes)
    send = send.transpose(3, 0, 1, 2, 4).reshape(nsta, parts * owned * depth, lanes)
    recv = lax.all_to_all(send, "sta", 0, 0, tiled=True)

    big = build_resid(pair_list, pair_values, count)
    big = big.reshape(2, count, 2, nsta, owned).transpose(1, 0, 3, 2, 4)
    big = big.reshape(2 * count, 2 * count)
    mixed = mix(big, recv.reshape(nsta * parts * owned * depth, lanes), depth)
    back = lax.all_to_all(mixed.reshape(nsta, owned * parts * depth, lanes), "sta", 0, 0,
                          tiled=True)

    meta = jnp.concatenate(
        [jnp.stack([slab, jnp.int32(nslab)]).astype(jnp.int32), station_cell.astype(jnp.int32)]
    )
    lo, hi = pl.pallas_call(
        functools.partial(source_kernel, owned, depth),
        out_shape=[jax.ShapeDtypeStruct((owned, 2, half, cells), jnp.float32)] * 2,
        in_specs=[
            pl.BlockSpec(memory_space=pltpu.SMEM),
            pl.BlockSpec(memory_space=pltpu.VMEM),
            pl.BlockSpec(memory_space=pltpu.VMEM),
        ],
    )(meta, back, noise_map)
    below = lax.ppermute(hi, "slab", up_pairs)
    above = lax.ppermute(lo, "slab", down_pairs)
    return sweeps(meta, lo, hi, below, above, wave_square, wbelow, wabove)


def solution(mesh):
    placed = (P(None, "sta", "slab", None), P(), P(), P("slab", None), P("slab", None), P("sta"))
    return jax.shard_map(
        local, mesh=mesh, in_specs=placed, out_specs=P(None, "sta", "slab", None), check_vma=False
    )
```

time: 153 us -> 96.9 us (0.63)
  the two profiles are of different devices: /device:TPU:25 before, /device:TPU:32 now
where the time goes in v1:
time: 96.9 us; the launch traced here: 96.4 us
  waiting for transfers between devices  31.4 us (32%)
  starting transfers between devices  28.4 us (29%)
  Pallas kernels  22.2 us (23%)
  local copies, waits for them, and re-layouts  11.9 us (12%)
  matrix products  1.54 us (2%)
    pallas_call x1, Pallas kernels, sweeps(): pl.pallas_call(functools.partial(sweep_kernel, depth), out_shape=jax.Shap...  17.2 us
    all_to_all x1, waiting for transfers between devices, local(): lax.all_to_all(mixed.reshape(nsta, owned * parts * depth, lanes), 'sta',...  16.3 us
    all_to_all x1, starting transfers between devices, local(): recv = lax.all_to_all(send, 'sta', 0, 0, tiled=True)  13.2 us
    all_to_all x1, waiting for transfers between devices, local(): recv = lax.all_to_all(send, 'sta', 0, 0, tiled=True)  9.49 us
    reshape x2, local copies, waits for them, and re-layouts, local(): big = big.reshape(2 * count, 2 * count)  6.31 us
    ppermute x1, waiting for transfers between devices, local(): wbelow = lax.ppermute(wave_square[depth - HALO:], 'slab', up_pairs)  5 us
    all_to_all x1, starting transfers between devices, local(): lax.all_to_all(mixed.reshape(nsta, owned * parts * depth, lanes), 'sta',...  4.64 us
    unnamed x21, local copies, waits for them, and re-layouts  4.39 us
  transfers between devices with their start and end apart: 6, of which 4 were waited for; matrix products, arithmetic and copies ran while one was open for 9% of the time, Pallas kernels for 0%

profile of v1, /device:TPU:32, one launch (start us, length us, event | category | flops | bytes accessed | tf_op | source)
XLA Modules:
  0.0 96.4 jit_solution(1165680941098339807)
XLA Ops:
  0.0 1.2 %copy.15 = bf16[8,8,32,128]{3,2,1,0:T(8,128)(2,1)S(1)} copy(bf16[8,8,32,128]{3,1,2,0:T(8,128)(2,1)} %bitcast.21) | data formatting | bytes 1048576
  1.2 1.0 %copy.11 = bf16[32,2,2,16,128]{4,3,2,1,0:T(8,128)(2,1)} copy(bf16[32,2,2,16,128]{4,0,3,2,1:T(8,128)(2,1)S(1)} %bitcast.20) | data formatting | bytes 1048576 | tf_op jit(solution)/shard_map/transpose | solution.py:195
  2.2 13.2 %all-to-all-start = ((bf16[32,64,128]{2,1,0:T(8,128)(2,1)}), bf16[32,64,128]{2,1,0:T(8,128)(2,1)S(1)}, u32[]{:S(2)}, u32[]{:S(2)}) async-start(bf16[32,64,128]{2,1,0:T(8,128)(2,1)} %bitcast.7), calls=%async_computation | async-start | bytes 1048576 | tf_op jit(solution)/shard_map/all_to_all | solution.py:196
  16.2 0.4 fusion
  16.6 0.4 fusion.31
  17.3 2.6 %copy.13 = bf16[64,2,32,2,2]{4,3,2,1,0:T(2,128)(2,1)S(1)} copy(bf16[64,2,32,2,2]{0,1,4,2,3:T(2,128)(2,1)S(1)} %bitcast.22) | data formatting | bytes 65536 | tf_op jit(solution)/shard_map/reshape | solution.py:200
  19.9 3.8 %reshape.26.big_ref = bf16[128,128]{1,0:T(8,128)(2,1)} reshape(bf16[64,2,32,2,2]{4,3,2,1,0:T(2,128)(2,1)S(1)} %copy.13) | data formatting | bytes 65536 | tf_op jit(solution)/shard_map/reshape | solution.py:200
  23.6 9.5 %all-to-all-done = bf16[32,64,128]{2,1,0:T(8,128)(2,1)S(1)} async-done(((bf16[32,64,128]{2,1,0:T(8,128)(2,1)}), bf16[32,64,128]{2,1,0:T(8,128)(2,1)S(1)}, u32[]{:S(2)}, u32[]{:S(2)}) %all-to-all-start) | async-done | bytes 524320 | tf_op jit(solution)/shard_map/all_to_all | solution.py:196
  33.1 0.8 copy-done
  33.9 2.7 %shard_map.64 = bf16[2048,128]{1,0:T(8,128)(2,1)} custom-call(bf16[128,128]{1,0:T(8,128)(2,1)} %reshape.26.big_ref, bf16[2048,128]{1,0:T(8,128)(2,1)} %bitcast.18), custom_call_target="tpu_custom_call" | custom-call | flops 67108864 | bytes 1048576 | tf_op jit(solution)/shard_map/pallas_call | solution.py:53
  36.6 4.6 %all-to-all-start.1 = ((bf16[32,64,128]{2,1,0:T(8,128)(2,1)}), bf16[32,64,128]{2,1,0:T(8,128)(2,1)S(1)}, u32[]{:S(2)}, u32[]{:S(2)}) async-start(bf16[32,64,128]{2,1,0:T(8,128)(2,1)} %bitcast.19), calls=%async_computation.1 | async-start | bytes 1048576 | tf_op jit(solution)/shard_map/all_to_all | solution.py:202
  41.3 0.7 pad_add_fusion.meta_ref
  42.0 16.3 %all-to-all-done.1.recv_ref = bf16[32,64,128]{2,1,0:T(8,128)(2,1)S(1)} async-done(((bf16[32,64,128]{2,1,0:T(8,128)(2,1)}), bf16[32,64,128]{2,1,0:T(8,128)(2,1)S(1)}, u32[]{:S(2)}, u32[]{:S(2)}) %all-to-all-start.1) | async-done | bytes 524320 | tf_op jit(solution)/shard_map/all_to_all | solution.py:202
  58.3 0.8 copy-done.1
  59.1 2.3 %shard_map.65 = (f32[2,2,8,4096]{3,2,1,0:T(8,128)}, f32[2,2,8,4096]{3,2,1,0:T(8,128)}) custom-call(s32[4]{0:T(128)} %pad_add_fusion.meta_ref, bf16[32,64,128]{2,1,0:T(8,128)(2,1)} %copy-done.1, f32[16,4096]{1,0:T(8,128)} %noise_ref.1), custom_call_target="tpu_custom_call" | custom-call | tf_op jit(solution)/shard_map/pallas_call | solution.py:208
  61.3 1.9 %collective-permute-start.1 = (f32[2,2,8,4096]{3,2,1,0:T(8,128)}, f32[2,2,8,4096]{3,2,1,0:T(8,128)S(1)}, u32[]{:S(2)}, u32[]{:S(2)}) collective-permute-start(f32[2,2,8,4096]{3,2,1,0:T(8,128)} %get-tuple-element.7.lo_ref), channel_id=1, source_target_pairs={{1,0},{2,1},{3,2},{4,3},{5,4},{6,5},{7,6},{8,7},{9,8},{10,9},{11,1... | collective-permute-start | bytes 1572872 | tf_op jit(solution)/shard_map/ppermute | solution.py:218
  63.2 2.4 %collective-permute-start = (f32[2,2,8,4096]{3,2,1,0:T(8,128)}, f32[2,2,8,4096]{3,2,1,0:T(8,128)S(1)}, u32[]{:S(2)}, u32[]{:S(2)}) collective-permute-start(f32[2,2,8,4096]{3,2,1,0:T(8,128)} %get-tuple-element.8.hi_ref), channel_id=1, source_target_pairs={{0,1},{1,2},{2,3},{3,4},{4,5},{5,6},{6,7},{7,8},{8,9},{9,10},{10,1... | collective-permute-start | bytes 1572872 | tf_op jit(solution)/shard_map/ppermute | solution.py:217
  65.7 4.4 %collective-permute-start.3 = (f32[8,4096]{1,0:T(8,128)S(1)}, f32[8,4096]{1,0:T(8,128)S(1)}, u32[]{:S(2)}, u32[]{:S(2)}) collective-permute-start(f32[8,4096]{1,0:T(8,128)S(1)} %get-tuple-element.9), channel_id=1, source_target_pairs={{1,0},{2,1},{3,2},{4,3},{5,4},{6,5},{7,6},{8,7},{9,8},{10,9},{11,1... | collective-permute-start | bytes 393224 | tf_op jit(solution)/shard_map/ppermute | solution.py:192
  70.1 1.9 %collective-permute-start.2 = (f32[8,4096]{1,0:T(8,128)S(1)}, f32[8,4096]{1,0:T(8,128)S(1)}, u32[]{:S(2)}, u32[]{:S(2)}) collective-permute-start(f32[8,4096]{1,0:T(8,128)S(1)} %get-tuple-element.10), channel_id=1, source_target_pairs={{0,1},{1,2},{2,3},{3,4},{4,5},{5,6},{6,7},{7,8},{8,9},{9,10},{10,1... | collective-permute-start | bytes 393224 | tf_op jit(solution)/shard_map/ppermute | solution.py:191
  72.0 0.6 collective-permute-done.3.wabove_ref
  72.6 5.0 %collective-permute-done.2.wbelow_ref = f32[8,4096]{1,0:T(8,128)S(1)} collective-permute-done((f32[8,4096]{1,0:T(8,128)S(1)}, f32[8,4096]{1,0:T(8,128)S(1)}, u32[]{:S(2)}, u32[]{:S(2)}) %collective-permute-start.2) | collective-permute-done | bytes 131104 | tf_op jit(solution)/shard_map/ppermute | solution.py:191
  77.6 0.6 copy-done.6
  78.4 0.8 copy-done.4
  79.2 17.2 %shard_map.66 = f32[2,2,16,4096]{3,2,1,0:T(8,128)} custom-call(s32[4]{0:T(128)} %pad_add_fusion.meta_ref, f32[2,2,8,4096]{3,2,1,0:T(8,128)} %get-tuple-element.7.lo_ref, f32[2,2,8,4096]{3,2,1,0:T(8,128)} %get-tuple-element.8.hi_ref, f32[2,2,8,4096]{3,2,1,0:T(8,128)} %copy-done.4, f32[2,2,8,4096]{3,2,1,0:T(8,128)} %copy-done.3, f32[16,4096]{1,0:T(8,128)} %wave_ref.1, ...), custom_call_target="tpu_custom_call" | custom-call | flops 141557760 | bytes 3145728 | tf_op jit(solution)/shard_map/pallas_call | solution.py:168
  (26 shorter events, 1.3 us)
Async XLA Ops:
  0.0 15.4 %copy-start.7 = (s32[256,2]{0,1:T(2,128)S(1)}, s32[256,2]{0,1:T(2,128)}, u32[]{:S(2)}) copy-start(s32[256,2]{0,1:T(2,128)} %param.7) | copy-start | bytes 6148
  0.0 15.4 %copy-start.8 = (f32[2,256]{1,0:T(2,128)S(1)}, f32[2,256]{1,0:T(2,128)}, u32[]{:S(2)}) copy-start(f32[2,256]{1,0:T(2,128)} %param.8) | copy-start | bytes 6148
  2.2 30.9 %all-to-all-start = ((bf16[32,64,128]{2,1,0:T(8,128)(2,1)}), bf16[32,64,128]{2,1,0:T(8,128)(2,1)S(1)}, u32[]{:S(2)}, u32[]{:S(2)}) async-start(bf16[32,64,128]{2,1,0:T(8,128)(2,1)} %bitcast.7), calls=%async_computation | async-start | bytes 1048576 | tf_op jit(solution)/shard_map/all_to_all | solution.py:196
  19.8 21.4 %copy-start.9 = (s32[2]{0:T(128)S(1)}, s32[2]{0:T(128)}, u32[]{:S(2)}) copy-start(s32[2]{0:T(128)} %param.11) | copy-start | bytes 28
  19.9 45.8 %copy-start.2 = (f32[16,4096]{1,0:T(8,128)S(1)}, f32[16,4096]{1,0:T(8,128)}, u32[]{:S(2)}) copy-start(f32[16,4096]{1,0:T(8,128)} %wave_ref.1) | copy-start | bytes 786436
  33.1 0.8 copy-start
  36.6 21.6 %all-to-all-start.1 = ((bf16[32,64,128]{2,1,0:T(8,128)(2,1)}), bf16[32,64,128]{2,1,0:T(8,128)(2,1)S(1)}, u32[]{:S(2)}, u32[]{:S(2)}) async-start(bf16[32,64,128]{2,1,0:T(8,128)(2,1)} %bitcast.19), calls=%async_computation.1 | async-start | bytes 1048576 | tf_op jit(solution)/shard_map/all_to_all | solution.py:202
  58.3 0.8 copy-start.1
  61.3 16.2 %collective-permute-start.1 = (f32[2,2,8,4096]{3,2,1,0:T(8,128)}, f32[2,2,8,4096]{3,2,1,0:T(8,128)S(1)}, u32[]{:S(2)}, u32[]{:S(2)}) collective-permute-start(f32[2,2,8,4096]{3,2,1,0:T(8,128)} %get-tuple-element.7.lo_ref), channel_id=1, source_target_pairs={{1,0},{2,1},{3,2},{4,3},{5,4},{6,5},{7,6},{8,7},{9,8},{10,9},{11,1... | collective-permute-start | bytes 1572872 | tf_op jit(solution)/shard_map/ppermute | solution.py:218
  63.2 14.3 %collective-permute-start = (f32[2,2,8,4096]{3,2,1,0:T(8,128)}, f32[2,2,8,4096]{3,2,1,0:T(8,128)S(1)}, u32[]{:S(2)}, u32[]{:S(2)}) collective-permute-start(f32[2,2,8,4096]{3,2,1,0:T(8,128)} %get-tuple-element.8.hi_ref), channel_id=1, source_target_pairs={{0,1},{1,2},{2,3},{3,4},{4,5},{5,6},{6,7},{7,8},{8,9},{9,10},{10,1... | collective-permute-start | bytes 1572872 | tf_op jit(solution)/shard_map/ppermute | solution.py:217
  65.7 6.9 %collective-permute-start.3 = (f32[8,4096]{1,0:T(8,128)S(1)}, f32[8,4096]{1,0:T(8,128)S(1)}, u32[]{:S(2)}, u32[]{:S(2)}) collective-permute-start(f32[8,4096]{1,0:T(8,128)S(1)} %get-tuple-element.9), channel_id=1, source_target_pairs={{1,0},{2,1},{3,2},{4,3},{5,4},{6,5},{7,6},{8,7},{9,8},{10,9},{11,1... | collective-permute-start | bytes 393224 | tf_op jit(solution)/shard_map/ppermute | solution.py:192
  70.1 7.5 %collective-permute-start.2 = (f32[8,4096]{1,0:T(8,128)S(1)}, f32[8,4096]{1,0:T(8,128)S(1)}, u32[]{:S(2)}, u32[]{:S(2)}) collective-permute-start(f32[8,4096]{1,0:T(8,128)S(1)} %get-tuple-element.10), channel_id=1, source_target_pairs={{0,1},{1,2},{2,3},{3,4},{4,5},{5,6},{6,7},{7,8},{8,9},{9,10},{10,1... | collective-permute-start | bytes 393224 | tf_op jit(solution)/shard_map/ppermute | solution.py:191
  72.6 5.0 %copy-start.5 = (f32[8,4096]{1,0:T(8,128)}, f32[8,4096]{1,0:T(8,128)S(1)}, u32[]{:S(2)}) copy-start(f32[8,4096]{1,0:T(8,128)S(1)} %collective-permute-done.3.wabove_ref) | copy-start | bytes 393220
  77.6 0.7 copy-start.6
  77.6 0.8 copy-start.3
  78.4 0.8 copy-start.4

commit v2 on v1

--- a/solution.py
+++ b/solution.py
@@ -118,31 +118,34 @@
     re_ref[...] = sr * src_re - si * src_im
     im_ref[...] = sr * src_im + si * src_re
 
-    def near(f, lane):
-        col = lane % GY
-        xm = jnp.where(lane >= GY, pltpu.roll(f, GY, 1), 0.0)
-        xp = jnp.where(lane < cells - GY, pltpu.roll(f, cells - GY, 1), 0.0)
-        ym = jnp.where(col != 0, pltpu.roll(f, 1, 1), 0.0)
-        yp = jnp.where(col != GY - 1, pltpu.roll(f, cells - 1, 1), 0.0)
-        dn = pltpu.roll(f, 1, 0)
-        up = pltpu.roll(f, rows - 1, 0)
-        return xm + xp + ym + yp + dn + up
+    keep = 1.0 - relaxation
 
     def body(_, carry):
         lane = lax.broadcasted_iota(jnp.int32, (rows, cells), 1)
+        col = jnp.bitwise_and(lane, GY - 1)
+        has_xm = lane >= GY
+        has_xp = lane < cells - GY
+        has_ym = col != 0
+        has_yp = col != GY - 1
+
+        def total(f, src):
+            shifted = pltpu.roll(f, GY, 1)
+            xm = jnp.where(has_xm, shifted, 0.0)
+            xp = jnp.where(has_xp, pltpu.roll(shifted, cells - 2 * GY, 1), 0.0)
+            ym = jnp.where(has_ym, pltpu.roll(f, 1, 1), 0.0)
+            yp = jnp.where(has_yp, pltpu.roll(f, cells - 1, 1), 0.0)
+            dn = pltpu.roll(f, 1, 0)
+            up = pltpu.roll(f, rows - 1, 0)
+            return src + (xm + xp + ym + yp + dn + up)
+
         re = re_ref[...]
         im = im_ref[...]
-        w = w_ref[...]
-        near_re = near(re, lane)
-        near_im = near(im, lane)
-        applied_re = 6.0 * re - near_re - w * (re - damping * im)
-        applied_im = 6.0 * im - near_im - w * (damping * re + im)
-        rest_re = sre_ref[...] - applied_re
-        rest_im = sim_ref[...] - applied_im
+        t_re = total(re, sre_ref[...])
+        t_im = total(im, sim_ref[...])
         s_r = sr_ref[...]
         s_i = si_ref[...]
-        re_ref[...] = re + s_r * rest_re - s_i * rest_im
-        im_ref[...] = im + s_r * rest_im + s_i * rest_re
+        re_ref[...] = keep * re + (s_r * t_re - s_i * t_im)
+        im_ref[...] = keep * im + (s_r * t_im + s_i * t_re)
         return carry
 
     lax.fori_loop(0, SWEEPS - 1, body, 0)
@@ -198,6 +201,7 @@
     big = build_resid(pair_list, pair_values, count)
     big = big.reshape(2, count, 2, nsta, owned).transpose(1, 0, 3, 2, 4)
     big = big.reshape(2 * count, 2 * count)
+    big, wbelow, wabove = lax.optimization_barrier((big, wbelow, wabove))
     mixed = mix(big, recv.reshape(nsta * parts * owned * depth, lanes), depth)
     back = lax.all_to_all(mixed.reshape(nsta, owned * parts * depth, lanes), "sta", 0, 0,
                           tiled=True)

time: 96.9 us -> 99.6 us (1.028)
  waiting for transfers between devices: 31.4 us -> 37.5 us
  Pallas kernels: 22.2 us -> 21 us
  local copies, waits for them, and re-layouts: 11.9 us -> 10.8 us
  starting transfers between devices: 28.4 us -> 27.3 us
    ppermute x1, waiting for transfers between devices: 5 us -> 0.01 us  [local(): wbelow = lax.ppermute(wave_square[depth - HALO:], 'slab', up_pairs)]
    ppermute x1, waiting for transfers between devices: 0.01 us -> 4.92 us  [local(): below = lax.ppermute(hi, 'slab', up_pairs)]
    ppermute x1, waiting for transfers between devices: 0.01 us -> 4.58 us  [local(): above = lax.ppermute(lo, 'slab', down_pairs)]
    reshape x2 -> x1, local copies, waits for them, and re-layouts: 6.31 us -> 3.16 us  [local(): big = big.reshape(2 * count, 2 * count)]
    ppermute x1, starting transfers between devices: 4.37 us -> 1.92 us  [local(): wabove = lax.ppermute(wave_square[:HALO], 'slab', down_pairs)]
    all_to_all x1, waiting for transfers between devices: 9.49 us -> 11.2 us  [local(): recv = lax.all_to_all(send, 'sta', 0, 0, tiled=True)]
    pallas_call x1, Pallas kernels: 17.2 us -> 16.1 us  [sweeps(): pl.pallas_call(functools.partial(sweep_kernel, depth), out_shape=jax.Shap...]
    transpose x0 -> x1, local copies, waits for them, and re-layouts: none -> 1.11 us  [local(): big = big.reshape(2, count, 2, nsta, owned).transpose(1, 0, 3, 2, 4)]
  transfers between devices with their start and end apart: 6 -> 6, of which waited for: 4 -> 4; matrix products, arithmetic and copies ran while one was open for 9% -> 10% of each run, Pallas kernels for 0% -> 0%
where the time goes in v2:
time: 99.6 us; the launch traced here: 99.1 us
  waiting for transfers between devices  37.5 us (38%)
  starting transfers between devices  27.3 us (27%)
  Pallas kernels  21 us (21%)
  local copies, waits for them, and re-layouts  10.8 us (11%)
  matrix products  1.54 us (2%)
    all_to_all x1, waiting for transfers between devices, local(): lax.all_to_all(mixed.reshape(nsta, owned * parts * depth, lanes), 'sta',...  16.9 us
    pallas_call x1, Pallas kernels, sweeps(): pl.pallas_call(functools.partial(sweep_kernel, depth), out_shape=jax.Shap...  16.1 us
    all_to_all x1, starting transfers between devices, local(): recv = lax.all_to_all(send, 'sta', 0, 0, tiled=True)  13.2 us
    all_to_all x1, waiting for transfers between devices, local(): recv = lax.all_to_all(send, 'sta', 0, 0, tiled=True)  11.2 us
    all_to_all x1, starting transfers between devices, local(): lax.all_to_all(mixed.reshape(nsta, owned * parts * depth, lanes), 'sta',...  5.5 us
    ppermute x1, waiting for transfers between devices, local(): below = lax.ppermute(hi, 'slab', up_pairs)  4.92 us
    ppermute x1, waiting for transfers between devices, local(): above = lax.ppermute(lo, 'slab', down_pairs)  4.58 us
    unnamed x19, local copies, waits for them, and re-layouts  3.54 us
  transfers between devices with their start and end apart: 6, of which 4 were waited for; matrix products, arithmetic and copies ran while one was open for 10% of the time, Pallas kernels for 0%

profile of v2, /device:TPU:32, one launch (start us, length us, event | category | flops | bytes accessed | tf_op | source)
XLA Modules:
  0.0 99.1 jit_solution(6112624247804306957)
XLA Ops:
  0.0 1.0 %fusion.28 = (f32[8,4096]{1,0:T(8,128)S(1)}, f32[8,4096]{1,0:T(8,128)S(1)}) fusion(f32[16,4096]{1,0:T(8,128)} %wave_ref.1), kind=kLoop, calls=%fused_computation.34 | loop fusion | bytes 524288 | tf_op jit(solution)/shard_map/slice | solution.py:195
  1.0 1.9 %collective-permute-start.1 = (f32[8,4096]{1,0:T(8,128)S(1)}, f32[8,4096]{1,0:T(8,128)S(1)}, u32[]{:S(2)}, u32[]{:S(2)}) collective-permute-start(f32[8,4096]{1,0:T(8,128)S(1)} %get-tuple-element.15), channel_id=1, source_target_pairs={{1,0},{2,1},{3,2},{4,3},{5,4},{6,5},{7,6},{8,7},{9,8},{10,9},{11,1... | collective-permute-start | bytes 393224 | tf_op jit(solution)/shard_map/ppermute | solution.py:195
  2.9 2.4 %collective-permute-start = (f32[8,4096]{1,0:T(8,128)S(1)}, f32[8,4096]{1,0:T(8,128)S(1)}, u32[]{:S(2)}, u32[]{:S(2)}) collective-permute-start(f32[8,4096]{1,0:T(8,128)S(1)} %get-tuple-element.16), channel_id=1, source_target_pairs={{0,1},{1,2},{2,3},{3,4},{4,5},{5,6},{6,7},{7,8},{8,9},{9,10},{10,1... | collective-permute-start | bytes 393224 | tf_op jit(solution)/shard_map/ppermute | solution.py:194
  5.4 1.1 %copy.13 = bf16[8,8,32,128]{3,2,1,0:T(8,128)(2,1)S(1)} copy(bf16[8,8,32,128]{3,1,2,0:T(8,128)(2,1)} %bitcast.25) | data formatting | bytes 1048576
  6.5 1.0 %copy.11 = bf16[32,2,2,16,128]{4,3,2,1,0:T(8,128)(2,1)} copy(bf16[32,2,2,16,128]{4,0,3,2,1:T(8,128)(2,1)S(1)} %bitcast.24) | data formatting | bytes 1048576 | tf_op jit(solution)/shard_map/transpose | solution.py:198
  7.5 13.2 %all-to-all-start = ((bf16[32,64,128]{2,1,0:T(8,128)(2,1)}), bf16[32,64,128]{2,1,0:T(8,128)(2,1)S(1)}, u32[]{:S(2)}, u32[]{:S(2)}) async-start(bf16[32,64,128]{2,1,0:T(8,128)(2,1)} %bitcast.7), calls=%async_computation | async-start | bytes 1048576 | tf_op jit(solution)/shard_map/all_to_all | solution.py:199
  21.5 0.4 fusion.31
  22.6 1.1 %copy.10 = bf16[64,2,32,2,2]{1,0,4,3,2:T(8,128)(2,1)S(1)} copy(bf16[64,2,32,2,2]{0,1,4,2,3:T(2,128)(2,1)S(1)} %bitcast.26) | data formatting | bytes 65536 | tf_op jit(solution)/shard_map/transpose | solution.py:202
  23.7 3.2 %reshape.21 = bf16[128,128]{0,1:T(8,128)(2,1)S(1)} reshape(bf16[64,2,32,2,2]{1,0,4,3,2:T(8,128)(2,1)S(1)} %copy.10) | data formatting | bytes 65536 | tf_op jit(solution)/shard_map/reshape | solution.py:203
  26.9 0.7 copy.12.big_ref
  27.7 11.2 %all-to-all-done = bf16[32,64,128]{2,1,0:T(8,128)(2,1)S(1)} async-done(((bf16[32,64,128]{2,1,0:T(8,128)(2,1)}), bf16[32,64,128]{2,1,0:T(8,128)(2,1)S(1)}, u32[]{:S(2)}, u32[]{:S(2)}) %all-to-all-start) | async-done | bytes 524320 | tf_op jit(solution)/shard_map/all_to_all | solution.py:199
  38.8 0.8 copy-done
  39.6 2.7 %shard_map.64 = bf16[2048,128]{1,0:T(8,128)(2,1)} custom-call(bf16[128,128]{1,0:T(8,128)(2,1)} %copy.12.big_ref, bf16[2048,128]{1,0:T(8,128)(2,1)} %bitcast.22), custom_call_target="tpu_custom_call" | custom-call | flops 67108864 | bytes 1048576 | tf_op jit(solution)/shard_map/pallas_call | solution.py:53
  42.3 5.5 %all-to-all-start.1 = ((bf16[32,64,128]{2,1,0:T(8,128)(2,1)}), bf16[32,64,128]{2,1,0:T(8,128)(2,1)S(1)}, u32[]{:S(2)}, u32[]{:S(2)}) async-start(bf16[32,64,128]{2,1,0:T(8,128)(2,1)} %bitcast.23), calls=%async_computation.1 | async-start | bytes 1048576 | tf_op jit(solution)/shard_map/all_to_all | solution.py:206
  47.9 0.7 pad_add_fusion.meta_ref
  48.5 16.9 %all-to-all-done.1.recv_ref = bf16[32,64,128]{2,1,0:T(8,128)(2,1)S(1)} async-done(((bf16[32,64,128]{2,1,0:T(8,128)(2,1)}), bf16[32,64,128]{2,1,0:T(8,128)(2,1)S(1)}, u32[]{:S(2)}, u32[]{:S(2)}) %all-to-all-start.1) | async-done | bytes 524320 | tf_op jit(solution)/shard_map/all_to_all | solution.py:206
  65.4 0.8 copy-done.1
  66.2 2.2 %shard_map.65 = (f32[2,2,8,4096]{3,2,1,0:T(8,128)}, f32[2,2,8,4096]{3,2,1,0:T(8,128)}) custom-call(s32[4]{0:T(128)} %pad_add_fusion.meta_ref, bf16[32,64,128]{2,1,0:T(8,128)(2,1)} %copy-done.1, f32[16,4096]{1,0:T(8,128)} %noise_ref.1), custom_call_target="tpu_custom_call" | custom-call | tf_op jit(solution)/shard_map/pallas_call | solution.py:212
  68.4 1.9 %collective-permute-start.3 = (f32[2,2,8,4096]{3,2,1,0:T(8,128)}, f32[2,2,8,4096]{3,2,1,0:T(8,128)S(1)}, u32[]{:S(2)}, u32[]{:S(2)}) collective-permute-start(f32[2,2,8,4096]{3,2,1,0:T(8,128)} %get-tuple-element.11.lo_ref), channel_id=1, source_target_pairs={{1,0},{2,1},{3,2},{4,3},{5,4},{6,5},{7,6},{8,7},{9,8},{10,9},{11,1... | collective-permute-start | bytes 1572872 | tf_op jit(solution)/shard_map/ppermute | solution.py:222
  70.3 2.4 %collective-permute-start.2 = (f32[2,2,8,4096]{3,2,1,0:T(8,128)}, f32[2,2,8,4096]{3,2,1,0:T(8,128)S(1)}, u32[]{:S(2)}, u32[]{:S(2)}) collective-permute-start(f32[2,2,8,4096]{3,2,1,0:T(8,128)} %get-tuple-element.12.hi_ref), channel_id=1, source_target_pairs={{0,1},{1,2},{2,3},{3,4},{4,5},{5,6},{6,7},{7,8},{8,9},{9,10},{10,1... | collective-permute-start | bytes 1572872 | tf_op jit(solution)/shard_map/ppermute | solution.py:221
  72.7 4.6 %collective-permute-done.3.above_ref = f32[2,2,8,4096]{3,2,1,0:T(8,128)S(1)} collective-permute-done((f32[2,2,8,4096]{3,2,1,0:T(8,128)}, f32[2,2,8,4096]{3,2,1,0:T(8,128)S(1)}, u32[]{:S(2)}, u32[]{:S(2)}) %collective-permute-start.3) | collective-permute-done | bytes 524320 | tf_op jit(solution)/shard_map/ppermute | solution.py:222
  77.3 4.9 %collective-permute-done.2.below_ref = f32[2,2,8,4096]{3,2,1,0:T(8,128)S(1)} collective-permute-done((f32[2,2,8,4096]{3,2,1,0:T(8,128)}, f32[2,2,8,4096]{3,2,1,0:T(8,128)S(1)}, u32[]{:S(2)}, u32[]{:S(2)}) %collective-permute-start.2) | collective-permute-done | bytes 524320 | tf_op jit(solution)/shard_map/ppermute | solution.py:221
  82.3 0.8 copy-done.3
  83.0 16.1 %shard_map.66 = f32[2,2,16,4096]{3,2,1,0:T(8,128)} custom-call(s32[4]{0:T(128)} %pad_add_fusion.meta_ref, f32[2,2,8,4096]{3,2,1,0:T(8,128)} %get-tuple-element.11.lo_ref, f32[2,2,8,4096]{3,2,1,0:T(8,128)} %get-tuple-element.12.hi_ref, f32[2,2,8,4096]{3,2,1,0:T(8,128)} %copy-done.3, f32[2,2,8,4096]{3,2,1,0:T(8,128)} %copy-done.2, f32[16,4096]{1,0:T(8,128)} %wave_ref.1, ...), custom_call_target="tpu_custom_call" | custom-call | flops 141557760 | bytes 3145728 | tf_op jit(solution)/shard_map/pallas_call | solution.py:171
  (25 shorter events, 1.5 us)
Async XLA Ops:
  0.0 20.7 %copy-start.6 = (s32[256,2]{0,1:T(2,128)S(1)}, s32[256,2]{0,1:T(2,128)}, u32[]{:S(2)}) copy-start(s32[256,2]{0,1:T(2,128)} %param.7) | copy-start | bytes 6148
  0.0 20.7 %copy-start.7 = (f32[2,256]{1,0:T(2,128)S(1)}, f32[2,256]{1,0:T(2,128)}, u32[]{:S(2)}) copy-start(f32[2,256]{1,0:T(2,128)} %param.8) | copy-start | bytes 6148
  1.0 25.9 %collective-permute-start.1 = (f32[8,4096]{1,0:T(8,128)S(1)}, f32[8,4096]{1,0:T(8,128)S(1)}, u32[]{:S(2)}, u32[]{:S(2)}) collective-permute-start(f32[8,4096]{1,0:T(8,128)S(1)} %get-tuple-element.15), channel_id=1, source_target_pairs={{1,0},{2,1},{3,2},{4,3},{5,4},{6,5},{7,6},{8,7},{9,8},{10,9},{11,1... | collective-permute-start | bytes 393224 | tf_op jit(solution)/shard_map/ppermute | solution.py:195
  2.9 24.0 %collective-permute-start = (f32[8,4096]{1,0:T(8,128)S(1)}, f32[8,4096]{1,0:T(8,128)S(1)}, u32[]{:S(2)}, u32[]{:S(2)}) collective-permute-start(f32[8,4096]{1,0:T(8,128)S(1)} %get-tuple-element.16), channel_id=1, source_target_pairs={{0,1},{1,2},{2,3},{3,4},{4,5},{5,6},{6,7},{7,8},{8,9},{9,10},{10,1... | collective-permute-start | bytes 393224 | tf_op jit(solution)/shard_map/ppermute | solution.py:194
  7.5 31.3 %all-to-all-start = ((bf16[32,64,128]{2,1,0:T(8,128)(2,1)}), bf16[32,64,128]{2,1,0:T(8,128)(2,1)S(1)}, u32[]{:S(2)}, u32[]{:S(2)}) async-start(bf16[32,64,128]{2,1,0:T(8,128)(2,1)} %bitcast.7), calls=%async_computation | async-start | bytes 1048576 | tf_op jit(solution)/shard_map/all_to_all | solution.py:199
  23.7 24.1 %copy-start.8 = (s32[2]{0:T(128)S(1)}, s32[2]{0:T(128)}, u32[]{:S(2)}) copy-start(s32[2]{0:T(128)} %param.11) | copy-start | bytes 28
  26.9 55.3 %copy-start.4 = (f32[8,4096]{1,0:T(8,128)}, f32[8,4096]{1,0:T(8,128)S(1)}, u32[]{:S(2)}) copy-start(f32[8,4096]{1,0:T(8,128)S(1)} %collective-permute-done.1.wabove_ref) | copy-start | bytes 393220
  26.9 55.3 %copy-start.5 = (f32[8,4096]{1,0:T(8,128)}, f32[8,4096]{1,0:T(8,128)S(1)}, u32[]{:S(2)}) copy-start(f32[8,4096]{1,0:T(8,128)S(1)} %collective-permute-done.wbelow_ref) | copy-start | bytes 393220
  38.8 0.8 copy-start
  42.3 23.0 %all-to-all-start.1 = ((bf16[32,64,128]{2,1,0:T(8,128)(2,1)}), bf16[32,64,128]{2,1,0:T(8,128)(2,1)S(1)}, u32[]{:S(2)}, u32[]{:S(2)}) async-start(bf16[32,64,128]{2,1,0:T(8,128)(2,1)} %bitcast.23), calls=%async_computation.1 | async-start | bytes 1048576 | tf_op jit(solution)/shard_map/all_to_all | solution.py:206
  65.4 0.8 copy-start.1
  68.4 8.9 %collective-permute-start.3 = (f32[2,2,8,4096]{3,2,1,0:T(8,128)}, f32[2,2,8,4096]{3,2,1,0:T(8,128)S(1)}, u32[]{:S(2)}, u32[]{:S(2)}) collective-permute-start(f32[2,2,8,4096]{3,2,1,0:T(8,128)} %get-tuple-element.11.lo_ref), channel_id=1, source_target_pairs={{1,0},{2,1},{3,2},{4,3},{5,4},{6,5},{7,6},{8,7},{9,8},{10,9},{11,1... | collective-permute-start | bytes 1572872 | tf_op jit(solution)/shard_map/ppermute | solution.py:222
  70.3 11.9 %collective-permute-start.2 = (f32[2,2,8,4096]{3,2,1,0:T(8,128)}, f32[2,2,8,4096]{3,2,1,0:T(8,128)S(1)}, u32[]{:S(2)}, u32[]{:S(2)}) collective-permute-start(f32[2,2,8,4096]{3,2,1,0:T(8,128)} %get-tuple-element.12.hi_ref), channel_id=1, source_target_pairs={{0,1},{1,2},{2,3},{3,4},{4,5},{5,6},{6,7},{7,8},{8,9},{9,10},{10,1... | collective-permute-start | bytes 1572872 | tf_op jit(solution)/shard_map/ppermute | solution.py:221
  77.3 4.9 %copy-start.2 = (f32[2,2,8,4096]{3,2,1,0:T(8,128)}, f32[2,2,8,4096]{3,2,1,0:T(8,128)S(1)}, u32[]{:S(2)}) copy-start(f32[2,2,8,4096]{3,2,1,0:T(8,128)S(1)} %collective-permute-done.3.above_ref) | copy-start | bytes 1572868
  82.2 0.8 copy-start.3

commit v3 on v2

--- a/solution.py
+++ b/solution.py
@@ -10,6 +10,8 @@
 GY = 64
 SWEEPS = 6
 HALO = 8
+LANES = 128
+PAD = 128
 
 damping = 0.3
 relaxation = 0.8
@@ -88,9 +90,12 @@
 
 
 def sweep_kernel(depth, meta_ref, lo_ref, hi_ref, below_ref, above_ref, wave_ref, wbelow_ref,
-                 wabove_ref, out_ref, re_ref, im_ref, sre_ref, sim_ref, w_ref, sr_ref, si_ref):
+                 wabove_ref, out_ref, are_ref, aim_ref, bre_ref, bim_ref, sre_ref, sim_ref, w_ref,
+                 sr_ref, si_ref):
     half = depth // 2
-    rows, cells = re_ref.shape
+    rows, cells = sre_ref.shape
+    width = LANES
+    chunks = cells // width
     slab = meta_ref[0]
     nslab = meta_ref[1]
     w_ref[0:HALO] = wbelow_ref[...]
@@ -101,56 +106,77 @@
         dst[HALO : HALO + half] = lo_ref[0, part]
         dst[HALO + half : HALO + depth] = hi_ref[0, part]
         dst[HALO + depth :] = above_ref[0, part]
-    wave = w_ref[...]
-    row = lax.broadcasted_iota(jnp.int32, (rows, cells), 0)
+    zeros = jnp.zeros((rows, PAD), jnp.float32)
+    for ref in (are_ref, aim_ref, bre_ref, bim_ref):
+        ref[:, 0:PAD] = zeros
+        ref[:, PAD + cells :] = zeros
+    row = lax.broadcasted_iota(jnp.int32, (rows, width), 0)
     inside = jnp.logical_and(
         jnp.logical_or(row >= HALO, slab > 0),
         jnp.logical_or(row < HALO + depth, slab < nslab - 1),
     )
-    diag_real = 6.0 - wave
-    denom = diag_real * diag_real + damping * wave * (damping * wave)
-    sr_ref[...] = jnp.where(inside, relaxation * diag_real / denom, 0.0)
-    si_ref[...] = jnp.where(inside, relaxation * damping * wave / denom, 0.0)
-    sr = sr_ref[...]
-    si = si_ref[...]
-    src_re = sre_ref[...]
-    src_im = sim_ref[...]
-    re_ref[...] = sr * src_re - si * src_im
-    im_ref[...] = sr * src_im + si * src_re
+
+    def first(j, carry):
+        c0 = pl.multiple_of(j * width, width)
+        cols = pl.ds(c0, width)
+        wave = w_ref[:, cols]
+        diag_real = 6.0 - wave
+        denom = diag_real * diag_real + damping * wave * (damping * wave)
+        sr = jnp.where(inside, relaxation * diag_real / denom, 0.0)
+        si = jnp.where(inside, relaxation * damping * wave / denom, 0.0)
+        sr_ref[:, cols] = sr
+        si_ref[:, cols] = si
+        src_re = sre_ref[:, cols]
+        src_im = sim_ref[:, cols]
+        out = pl.ds(PAD + c0, width)
+        are_ref[:, out] = sr * src_re - si * src_im
+        aim_ref[:, out] = sr * src_im + si * src_re
+        return carry
+
+    lax.fori_loop(0, chunks, first, 0)
 
     keep = 1.0 - relaxation
-
-    def body(_, carry):
-        lane = lax.broadcasted_iota(jnp.int32, (rows, cells), 1)
-        col = jnp.bitwise_and(lane, GY - 1)
-        has_xm = lane >= GY
-        has_xp = lane < cells - GY
-        has_ym = col != 0
-        has_yp = col != GY - 1
-
-        def total(f, src):
-            shifted = pltpu.roll(f, GY, 1)
-            xm = jnp.where(has_xm, shifted, 0.0)
-            xp = jnp.where(has_xp, pltpu.roll(shifted, cells - 2 * GY, 1), 0.0)
-            ym = jnp.where(has_ym, pltpu.roll(f, 1, 1), 0.0)
-            yp = jnp.where(has_yp, pltpu.roll(f, cells - 1, 1), 0.0)
-            dn = pltpu.roll(f, 1, 0)
-            up = pltpu.roll(f, rows - 1, 0)
-            return src + (xm + xp + ym + yp + dn + up)
-
-        re = re_ref[...]
-        im = im_ref[...]
-        t_re = total(re, sre_ref[...])
-        t_im = total(im, sim_ref[...])
-        s_r = sr_ref[...]
-        s_i = si_ref[...]
-        re_ref[...] = keep * re + (s_r * t_re - s_i * t_im)
-        im_ref[...] = keep * im + (s_r * t_im + s_i * t_re)
-        return carry
-
-    lax.fori_loop(0, SWEEPS - 1, body, 0)
-    out_ref[0, 0] = re_ref[HALO : HALO + depth]
-    out_ref[1, 0] = im_ref[HALO : HALO + depth]
+    lane = lax.broadcasted_iota(jnp.int32, (rows, width), 1)
+    col = jnp.bitwise_and(lane, GY - 1)
+    has_ym = col != 0
+    has_yp = col != GY - 1
+
+    def sweep(src_pair, dst_pair, last):
+        def chunk(j, carry):
+            c0 = pl.multiple_of(j * width, width)
+            cols = pl.ds(c0, width)
+
+            def total(ref, src):
+                ext = ref[:, pl.ds(c0, width + 2 * PAD)]
+                rot = pltpu.roll(ext, GY, 1)
+                mid = ext[:, PAD : PAD + width]
+                xm = rot[:, PAD : PAD + width]
+                xp = rot[:, 2 * PAD : 2 * PAD + width]
+                ym = jnp.where(has_ym, pltpu.roll(mid, 1, 1), 0.0)
+                yp = jnp.where(has_yp, pltpu.roll(mid, width - 1, 1), 0.0)
+                dn = pltpu.roll(mid, 1, 0)
+                up = pltpu.roll(mid, rows - 1, 0)
+                return mid, src + (xm + xp + ym + yp + dn + up)
+
+            re, t_re = total(src_pair[0], sre_ref[:, cols])
+            im, t_im = total(src_pair[1], sim_ref[:, cols])
+            s_r = sr_ref[:, cols]
+            s_i = si_ref[:, cols]
+            new_re = keep * re + (s_r * t_re - s_i * t_im)
+            new_im = keep * im + (s_r * t_im + s_i * t_re)
+            if last:
+                out_ref[0, 0, :, cols] = new_re[HALO : HALO + depth]
+                out_ref[1, 0, :, cols] = new_im[HALO : HALO + depth]
+            else:
+                dst_pair[0][:, pl.ds(PAD + c0, width)] = new_re
+                dst_pair[1][:, pl.ds(PAD + c0, width)] = new_im
+            return carry
+
+        lax.fori_loop(0, chunks, chunk, 0)
+
+    pairs = ((are_ref, aim_ref), (bre_ref, bim_ref))
+    for k in range(SWEEPS - 1):
+        sweep(pairs[k % 2], pairs[(k + 1) % 2], k == SWEEPS - 2)
 
 
 def sweeps(meta, lo, hi, below, above, wave, wbelow, wabove):
@@ -166,14 +192,15 @@
         in_specs=[piece, piece, halo, halo, whole((depth, cells)), whole((HALO, cells)),
                   whole((HALO, cells))],
         out_specs=pl.BlockSpec((2, 1, depth, cells), lambda b, *_: (0, b, 0, 0)),
-        scratch_shapes=[pltpu.VMEM((rows, cells), jnp.float32) for _ in range(7)],
+        scratch_shapes=[pltpu.VMEM((rows, cells + 2 * PAD), jnp.float32) for _ in range(4)]
+        + [pltpu.VMEM((rows, cells), jnp.float32) for _ in range(5)],
     )
     return pl.pallas_call(
         functools.partial(sweep_kernel, depth),
         out_shape=jax.ShapeDtypeStruct((2, owned, depth, cells), jnp.float32),
         grid_spec=grid_spec,
         cost_estimate=pl.CostEstimate(
-            flops=owned * SWEEPS * 90 * rows * cells,
+            flops=owned * SWEEPS * 60 * rows * cells,
             bytes_accessed=owned * 4 * cells * (6 * depth),
             transcendentals=0,
         ),
@@ -191,9 +218,6 @@
     down_pairs = [(i + 1, i) for i in range(nslab - 1)]
     half = depth // 2
 
-    wbelow = lax.ppermute(wave_square[depth - HALO :], "slab", up_pairs)
-    wabove = lax.ppermute(wave_square[:HALO], "slab", down_pairs)
-
     send = green_fields.reshape(parts, owned, depth, nsta, lanes)
     send = send.transpose(3, 0, 1, 2, 4).reshape(nsta, parts * owned * depth, lanes)
     recv = lax.all_to_all(send, "sta", 0, 0, tiled=True)
@@ -201,6 +225,11 @@
     big = build_resid(pair_list, pair_values, count)
     big = big.reshape(2, count, 2, nsta, owned).transpose(1, 0, 3, 2, 4)
     big = big.reshape(2 * count, 2 * count)
+    big, wave_hi, wave_lo = lax.optimization_barrier(
+        (big, wave_square[depth - HALO :], wave_square[:HALO])
+    )
+    wbelow = lax.ppermute(wave_hi, "slab", up_pairs)
+    wabove = lax.ppermute(wave_lo, "slab", down_pairs)
     big, wbelow, wabove = lax.optimization_barrier((big, wbelow, wabove))
     mixed = mix(big, recv.reshape(nsta * parts * owned * depth, lanes), depth)
     back = lax.all_to_all(mixed.reshape(nsta, owned * parts * depth, lanes), "sta", 0, 0,

time: 99.6 us -> 122 us (1.22)
  Pallas kernels: 21 us -> 45.6 us
  waiting for transfers between devices: 37.5 us -> 30.8 us
  starting transfers between devices: 27.3 us -> 32.5 us
    pallas_call x1, Pallas kernels: 16.1 us -> 40.7 us  [sweeps(): pl.pallas_call(functools.partial(sweep_kernel, depth), out_shape=jax.Shap...]
    all_to_all x1, waiting for transfers between devices: 11.2 us -> 1.48 us  [local(): recv = lax.all_to_all(send, 'sta', 0, 0, tiled=True)]
    all_to_all x1, starting transfers between devices: 5.5 us -> 8.3 us  [local(): lax.all_to_all(mixed.reshape(nsta, owned * parts * depth, lanes), 'sta',...]
    ppermute x2, waiting for transfers between devices: 0.01 us -> 2.5 us  [the longest x1 1.79 us: local(): wabove = lax.ppermute(wave_lo, 'slab', down_pairs)]
    ppermute x2, starting transfers between devices: 4.33 us -> 6.77 us  [the longest x1 4.85 us: local(): wabove = lax.ppermute(wave_lo, 'slab', down_pairs)]
    unnamed x19 -> x21, local copies, waits for them, and re-layouts: 3.54 us -> 3.56 us
  transfers between devices with their start and end apart: 6 -> 6, of which waited for: 4 -> 6; matrix products, arithmetic and copies ran while one was open for 10% -> 6% of each run, Pallas kernels for 0% -> 0%
where the time goes in v3:
time: 122 us; the launch traced here: 121 us
  Pallas kernels  45.6 us (37%)
  starting transfers between devices  32.5 us (27%)
  waiting for transfers between devices  30.8 us (25%)
  local copies, waits for them, and re-layouts  9.79 us (8%)
  matrix products  1.54 us (1%)
    pallas_call x1, Pallas kernels, sweeps(): pl.pallas_call(functools.partial(sweep_kernel, depth), out_shape=jax.Shap...  40.7 us
    all_to_all x1, waiting for transfers between devices, local(): lax.all_to_all(mixed.reshape(nsta, owned * parts * depth, lanes), 'sta',...  16.9 us
    all_to_all x1, starting transfers between devices, local(): recv = lax.all_to_all(send, 'sta', 0, 0, tiled=True)  13.2 us
    all_to_all x1, starting transfers between devices, local(): lax.all_to_all(mixed.reshape(nsta, owned * parts * depth, lanes), 'sta',...  8.3 us
    ppermute x1, waiting for transfers between devices, local(): above = lax.ppermute(lo, 'slab', down_pairs)  5.06 us
    ppermute x1, waiting for transfers between devices, local(): below = lax.ppermute(hi, 'slab', up_pairs)  4.92 us
    ppermute x1, starting transfers between devices, local(): wabove = lax.ppermute(wave_lo, 'slab', down_pairs)  4.85 us
    unnamed x21, local copies, waits for them, and re-layouts  3.56 us
  transfers between devices with their start and end apart: 6, of which 6 were waited for; matrix products, arithmetic and copies ran while one was open for 6% of the time, Pallas kernels for 0%

profile of v3, /device:TPU:32, one launch (start us, length us, event | category | flops | bytes accessed | tf_op | source)
XLA Modules:
  0.0 121.3 jit_solution(3987486082911517975)
XLA Ops:
  0.0 1.2 copy.13
  1.2 1.0 copy.11
  2.2 13.2 %all-to-all-start = ((bf16[32,64,128]{2,1,0:T(8,128)(2,1)}), bf16[32,64,128]{2,1,0:T(8,128)(2,1)S(1)}, u32[]{:S(2)}, u32[]{:S(2)}) async-start(bf16[32,64,128]{2,1,0:T(8,128)(2,1)} %bitcast.7), calls=%async_computation | async-start | bytes 1048576 | tf_op jit(solution)/shard_map/all_to_all | solution.py:223
  17.3 1.1 copy.10
  18.4 3.2 %reshape.21 = bf16[128,128]{0,1:T(8,128)(2,1)S(1)} reshape(bf16[64,2,32,2,2]{1,0,4,3,2:T(8,128)(2,1)S(1)} %copy.10) | data formatting | bytes 65536 | tf_op jit(solution)/shard_map/reshape | solution.py:227
  21.6 1.9 %collective-permute-start = (f32[8,4096]{1,0:T(8,128)S(1)}, f32[8,4096]{1,0:T(8,128)S(1)}, u32[]{:S(2)}, u32[]{:S(2)}) collective-permute-start(f32[8,4096]{1,0:T(8,128)S(1)} %get-tuple-element.14), channel_id=1, source_target_pairs={{0,1},{1,2},{2,3},{3,4},{4,5},{5,6},{6,7},{7,8},{8,9},{9,10},{10,1... | collective-permute-start | bytes 393224 | tf_op jit(solution)/shard_map/ppermute | solution.py:231
  23.5 4.9 %collective-permute-start.1 = (f32[8,4096]{1,0:T(8,128)S(1)}, f32[8,4096]{1,0:T(8,128)S(1)}, u32[]{:S(2)}, u32[]{:S(2)}) collective-permute-start(f32[8,4096]{1,0:T(8,128)S(1)} %get-tuple-element.15), channel_id=1, source_target_pairs={{1,0},{2,1},{3,2},{4,3},{5,4},{6,5},{7,6},{8,7},{9,8},{10,9},{11,1... | collective-permute-start | bytes 393224 | tf_op jit(solution)/shard_map/ppermute | solution.py:232
  28.4 0.7 collective-permute-done.wbelow_ref
  29.1 1.8 %collective-permute-done.1.wabove_ref = f32[8,4096]{1,0:T(8,128)S(1)} collective-permute-done((f32[8,4096]{1,0:T(8,128)S(1)}, f32[8,4096]{1,0:T(8,128)S(1)}, u32[]{:S(2)}, u32[]{:S(2)}) %collective-permute-start.1) | collective-permute-done | bytes 131104 | tf_op jit(solution)/shard_map/ppermute | solution.py:232
  30.9 0.7 copy.12.big_ref
  31.6 1.5 %all-to-all-done = bf16[32,64,128]{2,1,0:T(8,128)(2,1)S(1)} async-done(((bf16[32,64,128]{2,1,0:T(8,128)(2,1)}), bf16[32,64,128]{2,1,0:T(8,128)(2,1)S(1)}, u32[]{:S(2)}, u32[]{:S(2)}) %all-to-all-start) | async-done | bytes 524320 | tf_op jit(solution)/shard_map/all_to_all | solution.py:223
  33.1 0.8 copy-done
  33.9 2.7 %shard_map.64 = bf16[2048,128]{1,0:T(8,128)(2,1)} custom-call(bf16[128,128]{1,0:T(8,128)(2,1)} %copy.12.big_ref, bf16[2048,128]{1,0:T(8,128)(2,1)} %bitcast.22), custom_call_target="tpu_custom_call" | custom-call | flops 67108864 | bytes 1048576 | tf_op jit(solution)/shard_map/pallas_call | solution.py:55
  36.6 8.3 %all-to-all-start.1 = ((bf16[32,64,128]{2,1,0:T(8,128)(2,1)}), bf16[32,64,128]{2,1,0:T(8,128)(2,1)S(1)}, u32[]{:S(2)}, u32[]{:S(2)}) async-start(bf16[32,64,128]{2,1,0:T(8,128)(2,1)} %bitcast.23), calls=%async_computation.1 | async-start | bytes 1048576 | tf_op jit(solution)/shard_map/all_to_all | solution.py:235
  44.9 0.7 pad_add_fusion.meta_ref
  45.6 16.9 %all-to-all-done.1.recv_ref = bf16[32,64,128]{2,1,0:T(8,128)(2,1)S(1)} async-done(((bf16[32,64,128]{2,1,0:T(8,128)(2,1)}), bf16[32,64,128]{2,1,0:T(8,128)(2,1)S(1)}, u32[]{:S(2)}, u32[]{:S(2)}) %all-to-all-start.1) | async-done | bytes 524320 | tf_op jit(solution)/shard_map/all_to_all | solution.py:235
  62.5 0.8 copy-done.1
  63.3 2.3 %shard_map.65 = (f32[2,2,8,4096]{3,2,1,0:T(8,128)}, f32[2,2,8,4096]{3,2,1,0:T(8,128)}) custom-call(s32[4]{0:T(128)} %pad_add_fusion.meta_ref, bf16[32,64,128]{2,1,0:T(8,128)(2,1)} %copy-done.1, f32[16,4096]{1,0:T(8,128)} %noise_ref.1), custom_call_target="tpu_custom_call" | custom-call | tf_op jit(solution)/shard_map/pallas_call | solution.py:241
  65.6 2.4 %collective-permute-start.3 = (f32[2,2,8,4096]{3,2,1,0:T(8,128)}, f32[2,2,8,4096]{3,2,1,0:T(8,128)S(1)}, u32[]{:S(2)}, u32[]{:S(2)}) collective-permute-start(f32[2,2,8,4096]{3,2,1,0:T(8,128)} %get-tuple-element.17.lo_ref), channel_id=1, source_target_pairs={{1,0},{2,1},{3,2},{4,3},{5,4},{6,5},{7,6},{8,7},{9,8},{10,9},{11,1... | collective-permute-start | bytes 1572872 | tf_op jit(solution)/shard_map/ppermute | solution.py:251
  67.9 1.9 %collective-permute-start.2 = (f32[2,2,8,4096]{3,2,1,0:T(8,128)}, f32[2,2,8,4096]{3,2,1,0:T(8,128)S(1)}, u32[]{:S(2)}, u32[]{:S(2)}) collective-permute-start(f32[2,2,8,4096]{3,2,1,0:T(8,128)} %get-tuple-element.18.hi_ref), channel_id=1, source_target_pairs={{0,1},{1,2},{2,3},{3,4},{4,5},{5,6},{6,7},{7,8},{8,9},{9,10},{10,1... | collective-permute-start | bytes 1572872 | tf_op jit(solution)/shard_map/ppermute | solution.py:250
  69.9 5.1 %collective-permute-done.3.above_ref = f32[2,2,8,4096]{3,2,1,0:T(8,128)S(1)} collective-permute-done((f32[2,2,8,4096]{3,2,1,0:T(8,128)}, f32[2,2,8,4096]{3,2,1,0:T(8,128)S(1)}, u32[]{:S(2)}, u32[]{:S(2)}) %collective-permute-start.3) | collective-permute-done | bytes 524320 | tf_op jit(solution)/shard_map/ppermute | solution.py:251
  74.9 4.9 %collective-permute-done.2.below_ref = f32[2,2,8,4096]{3,2,1,0:T(8,128)S(1)} collective-permute-done((f32[2,2,8,4096]{3,2,1,0:T(8,128)}, f32[2,2,8,4096]{3,2,1,0:T(8,128)S(1)}, u32[]{:S(2)}, u32[]{:S(2)}) %collective-permute-start.2) | collective-permute-done | bytes 524320 | tf_op jit(solution)/shard_map/ppermute | solution.py:250
  79.9 0.8 copy-done.4
  80.7 40.7 %shard_map.66 = f32[2,2,16,4096]{3,2,1,0:T(8,128)} custom-call(s32[4]{0:T(128)} %pad_add_fusion.meta_ref, f32[2,2,8,4096]{3,2,1,0:T(8,128)} %get-tuple-element.17.lo_ref, f32[2,2,8,4096]{3,2,1,0:T(8,128)} %get-tuple-element.18.hi_ref, f32[2,2,8,4096]{3,2,1,0:T(8,128)} %copy-done.4, f32[2,2,8,4096]{3,2,1,0:T(8,128)} %copy-done.3, f32[16,4096]{1,0:T(8,128)} %wave_ref.1, ...), custom_call_target="tpu_custom_call" | custom-call | flops 94371840 | bytes 3145728 | tf_op jit(solution)/shard_map/pallas_call | solution.py:198
  (27 shorter events, 1.9 us)
Async XLA Ops:
  0.0 15.4 %copy-start.7 = (s32[256,2]{0,1:T(2,128)S(1)}, s32[256,2]{0,1:T(2,128)}, u32[]{:S(2)}) copy-start(s32[256,2]{0,1:T(2,128)} %param.7) | copy-start | bytes 6148
  0.0 15.4 %copy-start.8 = (f32[2,256]{1,0:T(2,128)S(1)}, f32[2,256]{1,0:T(2,128)}, u32[]{:S(2)}) copy-start(f32[2,256]{1,0:T(2,128)} %param.8) | copy-start | bytes 6148
  2.2 30.9 %all-to-all-start = ((bf16[32,64,128]{2,1,0:T(8,128)(2,1)}), bf16[32,64,128]{2,1,0:T(8,128)(2,1)S(1)}, u32[]{:S(2)}, u32[]{:S(2)}) async-start(bf16[32,64,128]{2,1,0:T(8,128)(2,1)} %bitcast.7), calls=%async_computation | async-start | bytes 1048576 | tf_op jit(solution)/shard_map/all_to_all | solution.py:223
  17.3 4.3 %copy-start.2 = (f32[16,4096]{1,0:T(8,128)S(1)}, f32[16,4096]{1,0:T(8,128)}, u32[]{:S(2)}) copy-start(f32[16,4096]{1,0:T(8,128)} %wave_ref.1) | copy-start | bytes 786436
  18.4 26.5 %copy-start.9 = (s32[2]{0:T(128)S(1)}, s32[2]{0:T(128)}, u32[]{:S(2)}) copy-start(s32[2]{0:T(128)} %param.11) | copy-start | bytes 28
  21.6 7.5 %collective-permute-start = (f32[8,4096]{1,0:T(8,128)S(1)}, f32[8,4096]{1,0:T(8,128)S(1)}, u32[]{:S(2)}, u32[]{:S(2)}) collective-permute-start(f32[8,4096]{1,0:T(8,128)S(1)} %get-tuple-element.14), channel_id=1, source_target_pairs={{0,1},{1,2},{2,3},{3,4},{4,5},{5,6},{6,7},{7,8},{8,9},{9,10},{10,1... | collective-permute-start | bytes 393224 | tf_op jit(solution)/shard_map/ppermute | solution.py:231
  23.5 7.4 %collective-permute-start.1 = (f32[8,4096]{1,0:T(8,128)S(1)}, f32[8,4096]{1,0:T(8,128)S(1)}, u32[]{:S(2)}, u32[]{:S(2)}) collective-permute-start(f32[8,4096]{1,0:T(8,128)S(1)} %get-tuple-element.15), channel_id=1, source_target_pairs={{1,0},{2,1},{3,2},{4,3},{5,4},{6,5},{7,6},{8,7},{9,8},{10,9},{11,1... | collective-permute-start | bytes 393224 | tf_op jit(solution)/shard_map/ppermute | solution.py:232
  29.1 50.8 %copy-start.5 = (f32[8,4096]{1,0:T(8,128)}, f32[8,4096]{1,0:T(8,128)S(1)}, u32[]{:S(2)}) copy-start(f32[8,4096]{1,0:T(8,128)S(1)} %collective-permute-done.wbelow_ref) | copy-start | bytes 393220
  30.9 49.0 %copy-start.6 = (f32[8,4096]{1,0:T(8,128)}, f32[8,4096]{1,0:T(8,128)S(1)}, u32[]{:S(2)}) copy-start(f32[8,4096]{1,0:T(8,128)S(1)} %collective-permute-done.1.wabove_ref) | copy-start | bytes 393220
  33.1 0.8 copy-start
  36.6 25.9 %all-to-all-start.1 = ((bf16[32,64,128]{2,1,0:T(8,128)(2,1)}), bf16[32,64,128]{2,1,0:T(8,128)(2,1)S(1)}, u32[]{:S(2)}, u32[]{:S(2)}) async-start(bf16[32,64,128]{2,1,0:T(8,128)(2,1)} %bitcast.23), calls=%async_computation.1 | async-start | bytes 1048576 | tf_op jit(solution)/shard_map/all_to_all | solution.py:235
  62.5 0.8 copy-start.1
  65.6 9.4 %collective-permute-start.3 = (f32[2,2,8,4096]{3,2,1,0:T(8,128)}, f32[2,2,8,4096]{3,2,1,0:T(8,128)S(1)}, u32[]{:S(2)}, u32[]{:S(2)}) collective-permute-start(f32[2,2,8,4096]{3,2,1,0:T(8,128)} %get-tuple-element.17.lo_ref), channel_id=1, source_target_pairs={{1,0},{2,1},{3,2},{4,3},{5,4},{6,5},{7,6},{8,7},{9,8},{10,9},{11,1... | collective-permute-start | bytes 1572872 | tf_op jit(solution)/shard_map/ppermute | solution.py:251
  67.9 11.9 %collective-permute-start.2 = (f32[2,2,8,4096]{3,2,1,0:T(8,128)}, f32[2,2,8,4096]{3,2,1,0:T(8,128)S(1)}, u32[]{:S(2)}, u32[]{:S(2)}) collective-permute-start(f32[2,2,8,4096]{3,2,1,0:T(8,128)} %get-tuple-element.18.hi_ref), channel_id=1, source_target_pairs={{0,1},{1,2},{2,3},{3,4},{4,5},{5,6},{6,7},{7,8},{8,9},{9,10},{10,1... | collective-permute-start | bytes 1572872 | tf_op jit(solution)/shard_map/ppermute | solution.py:250
  74.9 4.9 %copy-start.3 = (f32[2,2,8,4096]{3,2,1,0:T(8,128)}, f32[2,2,8,4096]{3,2,1,0:T(8,128)S(1)}, u32[]{:S(2)}) copy-start(f32[2,2,8,4096]{3,2,1,0:T(8,128)S(1)} %collective-permute-done.3.above_ref) | copy-start | bytes 1572868
  79.9 0.8 copy-start.4

commit v4 on v2

--- a/solution.py
+++ b/solution.py
@@ -191,9 +191,6 @@
     down_pairs = [(i + 1, i) for i in range(nslab - 1)]
     half = depth // 2
 
-    wbelow = lax.ppermute(wave_square[depth - HALO :], "slab", up_pairs)
-    wabove = lax.ppermute(wave_square[:HALO], "slab", down_pairs)
-
     send = green_fields.reshape(parts, owned, depth, nsta, lanes)
     send = send.transpose(3, 0, 1, 2, 4).reshape(nsta, parts * owned * depth, lanes)
     recv = lax.all_to_all(send, "sta", 0, 0, tiled=True)
@@ -201,6 +198,11 @@
     big = build_resid(pair_list, pair_values, count)
     big = big.reshape(2, count, 2, nsta, owned).transpose(1, 0, 3, 2, 4)
     big = big.reshape(2 * count, 2 * count)
+    big, wave_hi, wave_lo = lax.optimization_barrier(
+        (big, wave_square[depth - HALO :], wave_square[:HALO])
+    )
+    wbelow = lax.ppermute(wave_hi, "slab", up_pairs)
+    wabove = lax.ppermute(wave_lo, "slab", down_pairs)
     big, wbelow, wabove = lax.optimization_barrier((big, wbelow, wabove))
     mixed = mix(big, recv.reshape(nsta * parts * owned * depth, lanes), depth)
     back = lax.all_to_all(mixed.reshape(nsta, owned * parts * depth, lanes), "sta", 0, 0,

time: 99.6 us -> 97.2 us (0.976)
  waiting for transfers between devices: 37.5 us -> 30.8 us
  starting transfers between devices: 27.3 us -> 32.5 us
  local copies, waits for them, and re-layouts: 10.8 us -> 9.79 us
    all_to_all x1, waiting for transfers between devices: 11.2 us -> 1.48 us  [local(): recv = lax.all_to_all(send, 'sta', 0, 0, tiled=True)]
    all_to_all x1, starting transfers between devices: 5.5 us -> 8.3 us  [local(): lax.all_to_all(mixed.reshape(nsta, owned * parts * depth, lanes), 'sta',...]
    ppermute x2, waiting for transfers between devices: 0.01 us -> 2.5 us  [the longest x1 1.79 us: local(): wabove = lax.ppermute(wave_lo, 'slab', down_pairs)]
    ppermute x2, starting transfers between devices: 4.33 us -> 6.77 us  [the longest x1 4.85 us: local(): wabove = lax.ppermute(wave_lo, 'slab', down_pairs)]
    unnamed x19 -> x21, local copies, waits for them, and re-layouts: 3.54 us -> 3.56 us
  transfers between devices with their start and end apart: 6 -> 6, of which waited for: 4 -> 6; matrix products, arithmetic and copies ran while one was open for 10% -> 8% of each run, Pallas kernels for 0% -> 0%
where the time goes in v4:
time: 97.2 us; the launch traced here: 96.7 us
  starting transfers between devices  32.5 us (33%)
  waiting for transfers between devices  30.8 us (32%)
  Pallas kernels  21 us (22%)
  local copies, waits for them, and re-layouts  9.79 us (10%)
  matrix products  1.54 us (2%)
    all_to_all x1, waiting for transfers between devices, local(): lax.all_to_all(mixed.reshape(nsta, owned * parts * depth, lanes), 'sta',...  16.9 us
    pallas_call x1, Pallas kernels, sweeps(): pl.pallas_call(functools.partial(sweep_kernel, depth), out_shape=jax.Shap...  16.1 us
    all_to_all x1, starting transfers between devices, local(): recv = lax.all_to_all(send, 'sta', 0, 0, tiled=True)  13.2 us
    all_to_all x1, starting transfers between devices, local(): lax.all_to_all(mixed.reshape(nsta, owned * parts * depth, lanes), 'sta',...  8.3 us
    ppermute x1, waiting for transfers between devices, local(): above = lax.ppermute(lo, 'slab', down_pairs)  5.06 us
    ppermute x1, waiting for transfers between devices, local(): below = lax.ppermute(hi, 'slab', up_pairs)  4.92 us
    ppermute x1, starting transfers between devices, local(): wabove = lax.ppermute(wave_lo, 'slab', down_pairs)  4.85 us
    unnamed x21, local copies, waits for them, and re-layouts  3.56 us
  transfers between devices with their start and end apart: 6, of which 6 were waited for; matrix products, arithmetic and copies ran while one was open for 8% of the time, Pallas kernels for 0%

profile of v4, /device:TPU:32, one launch (start us, length us, event | category | flops | bytes accessed | tf_op | source)
XLA Modules:
  0.0 96.7 jit_solution(15201097057342026655)
XLA Ops:
  0.0 1.2 %copy.13 = bf16[8,8,32,128]{3,2,1,0:T(8,128)(2,1)S(1)} copy(bf16[8,8,32,128]{3,1,2,0:T(8,128)(2,1)} %bitcast.25) | data formatting | bytes 1048576
  1.2 1.0 %copy.11 = bf16[32,2,2,16,128]{4,3,2,1,0:T(8,128)(2,1)} copy(bf16[32,2,2,16,128]{4,0,3,2,1:T(8,128)(2,1)S(1)} %bitcast.24) | data formatting | bytes 1048576 | tf_op jit(solution)/shard_map/transpose | solution.py:195
  2.2 13.2 %all-to-all-start = ((bf16[32,64,128]{2,1,0:T(8,128)(2,1)}), bf16[32,64,128]{2,1,0:T(8,128)(2,1)S(1)}, u32[]{:S(2)}, u32[]{:S(2)}) async-start(bf16[32,64,128]{2,1,0:T(8,128)(2,1)} %bitcast.7), calls=%async_computation | async-start | bytes 1048576 | tf_op jit(solution)/shard_map/all_to_all | solution.py:196
  17.3 1.1 %copy.10 = bf16[64,2,32,2,2]{1,0,4,3,2:T(8,128)(2,1)S(1)} copy(bf16[64,2,32,2,2]{0,1,4,2,3:T(2,128)(2,1)S(1)} %bitcast.26) | data formatting | bytes 65536 | tf_op jit(solution)/shard_map/transpose | solution.py:199
  18.4 3.2 %reshape.21 = bf16[128,128]{0,1:T(8,128)(2,1)S(1)} reshape(bf16[64,2,32,2,2]{1,0,4,3,2:T(8,128)(2,1)S(1)} %copy.10) | data formatting | bytes 65536 | tf_op jit(solution)/shard_map/reshape | solution.py:200
  21.6 1.9 %collective-permute-start = (f32[8,4096]{1,0:T(8,128)S(1)}, f32[8,4096]{1,0:T(8,128)S(1)}, u32[]{:S(2)}, u32[]{:S(2)}) collective-permute-start(f32[8,4096]{1,0:T(8,128)S(1)} %get-tuple-element.14), channel_id=1, source_target_pairs={{0,1},{1,2},{2,3},{3,4},{4,5},{5,6},{6,7},{7,8},{8,9},{9,10},{10,1... | collective-permute-start | bytes 393224 | tf_op jit(solution)/shard_map/ppermute | solution.py:204
  23.5 4.9 %collective-permute-start.1 = (f32[8,4096]{1,0:T(8,128)S(1)}, f32[8,4096]{1,0:T(8,128)S(1)}, u32[]{:S(2)}, u32[]{:S(2)}) collective-permute-start(f32[8,4096]{1,0:T(8,128)S(1)} %get-tuple-element.15), channel_id=1, source_target_pairs={{1,0},{2,1},{3,2},{4,3},{5,4},{6,5},{7,6},{8,7},{9,8},{10,9},{11,1... | collective-permute-start | bytes 393224 | tf_op jit(solution)/shard_map/ppermute | solution.py:205
  28.4 0.7 collective-permute-done.wbelow_ref
  29.1 1.8 %collective-permute-done.1.wabove_ref = f32[8,4096]{1,0:T(8,128)S(1)} collective-permute-done((f32[8,4096]{1,0:T(8,128)S(1)}, f32[8,4096]{1,0:T(8,128)S(1)}, u32[]{:S(2)}, u32[]{:S(2)}) %collective-permute-start.1) | collective-permute-done | bytes 131104 | tf_op jit(solution)/shard_map/ppermute | solution.py:205
  30.9 0.7 copy.12.big_ref
  31.6 1.5 %all-to-all-done = bf16[32,64,128]{2,1,0:T(8,128)(2,1)S(1)} async-done(((bf16[32,64,128]{2,1,0:T(8,128)(2,1)}), bf16[32,64,128]{2,1,0:T(8,128)(2,1)S(1)}, u32[]{:S(2)}, u32[]{:S(2)}) %all-to-all-start) | async-done | bytes 524320 | tf_op jit(solution)/shard_map/all_to_all | solution.py:196
  33.1 0.8 copy-done
  33.9 2.7 %shard_map.64 = bf16[2048,128]{1,0:T(8,128)(2,1)} custom-call(bf16[128,128]{1,0:T(8,128)(2,1)} %copy.12.big_ref, bf16[2048,128]{1,0:T(8,128)(2,1)} %bitcast.22), custom_call_target="tpu_custom_call" | custom-call | flops 67108864 | bytes 1048576 | tf_op jit(solution)/shard_map/pallas_call | solution.py:53
  36.6 8.3 %all-to-all-start.1 = ((bf16[32,64,128]{2,1,0:T(8,128)(2,1)}), bf16[32,64,128]{2,1,0:T(8,128)(2,1)S(1)}, u32[]{:S(2)}, u32[]{:S(2)}) async-start(bf16[32,64,128]{2,1,0:T(8,128)(2,1)} %bitcast.23), calls=%async_computation.1 | async-start | bytes 1048576 | tf_op jit(solution)/shard_map/all_to_all | solution.py:208
  44.9 0.7 pad_add_fusion.meta_ref
  45.6 16.9 %all-to-all-done.1.recv_ref = bf16[32,64,128]{2,1,0:T(8,128)(2,1)S(1)} async-done(((bf16[32,64,128]{2,1,0:T(8,128)(2,1)}), bf16[32,64,128]{2,1,0:T(8,128)(2,1)S(1)}, u32[]{:S(2)}, u32[]{:S(2)}) %all-to-all-start.1) | async-done | bytes 524320 | tf_op jit(solution)/shard_map/all_to_all | solution.py:208
  62.5 0.8 copy-done.1
  63.3 2.3 %shard_map.65 = (f32[2,2,8,4096]{3,2,1,0:T(8,128)}, f32[2,2,8,4096]{3,2,1,0:T(8,128)}) custom-call(s32[4]{0:T(128)} %pad_add_fusion.meta_ref, bf16[32,64,128]{2,1,0:T(8,128)(2,1)} %copy-done.1, f32[16,4096]{1,0:T(8,128)} %noise_ref.1), custom_call_target="tpu_custom_call" | custom-call | tf_op jit(solution)/shard_map/pallas_call | solution.py:214
  65.6 2.4 %collective-permute-start.3 = (f32[2,2,8,4096]{3,2,1,0:T(8,128)}, f32[2,2,8,4096]{3,2,1,0:T(8,128)S(1)}, u32[]{:S(2)}, u32[]{:S(2)}) collective-permute-start(f32[2,2,8,4096]{3,2,1,0:T(8,128)} %get-tuple-element.17.lo_ref), channel_id=1, source_target_pairs={{1,0},{2,1},{3,2},{4,3},{5,4},{6,5},{7,6},{8,7},{9,8},{10,9},{11,1... | collective-permute-start | bytes 1572872 | tf_op jit(solution)/shard_map/ppermute | solution.py:224
  67.9 1.9 %collective-permute-start.2 = (f32[2,2,8,4096]{3,2,1,0:T(8,128)}, f32[2,2,8,4096]{3,2,1,0:T(8,128)S(1)}, u32[]{:S(2)}, u32[]{:S(2)}) collective-permute-start(f32[2,2,8,4096]{3,2,1,0:T(8,128)} %get-tuple-element.18.hi_ref), channel_id=1, source_target_pairs={{0,1},{1,2},{2,3},{3,4},{4,5},{5,6},{6,7},{7,8},{8,9},{9,10},{10,1... | collective-permute-start | bytes 1572872 | tf_op jit(solution)/shard_map/ppermute | solution.py:223
  69.9 5.1 %collective-permute-done.3.above_ref = f32[2,2,8,4096]{3,2,1,0:T(8,128)S(1)} collective-permute-done((f32[2,2,8,4096]{3,2,1,0:T(8,128)}, f32[2,2,8,4096]{3,2,1,0:T(8,128)S(1)}, u32[]{:S(2)}, u32[]{:S(2)}) %collective-permute-start.3) | collective-permute-done | bytes 524320 | tf_op jit(solution)/shard_map/ppermute | solution.py:224
  74.9 4.9 %collective-permute-done.2.below_ref = f32[2,2,8,4096]{3,2,1,0:T(8,128)S(1)} collective-permute-done((f32[2,2,8,4096]{3,2,1,0:T(8,128)}, f32[2,2,8,4096]{3,2,1,0:T(8,128)S(1)}, u32[]{:S(2)}, u32[]{:S(2)}) %collective-permute-start.2) | collective-permute-done | bytes 524320 | tf_op jit(solution)/shard_map/ppermute | solution.py:223
  79.9 0.8 copy-done.4
  80.7 16.1 %shard_map.66 = f32[2,2,16,4096]{3,2,1,0:T(8,128)} custom-call(s32[4]{0:T(128)} %pad_add_fusion.meta_ref, f32[2,2,8,4096]{3,2,1,0:T(8,128)} %get-tuple-element.17.lo_ref, f32[2,2,8,4096]{3,2,1,0:T(8,128)} %get-tuple-element.18.hi_ref, f32[2,2,8,4096]{3,2,1,0:T(8,128)} %copy-done.4, f32[2,2,8,4096]{3,2,1,0:T(8,128)} %copy-done.3, f32[16,4096]{1,0:T(8,128)} %wave_ref.1, ...), custom_call_target="tpu_custom_call" | custom-call | flops 141557760 | bytes 3145728 | tf_op jit(solution)/shard_map/pallas_call | solution.py:171
  (27 shorter events, 1.9 us)
Async XLA Ops:
  0.0 15.4 %copy-start.7 = (s32[256,2]{0,1:T(2,128)S(1)}, s32[256,2]{0,1:T(2,128)}, u32[]{:S(2)}) copy-start(s32[256,2]{0,1:T(2,128)} %param.7) | copy-start | bytes 6148
  0.0 15.4 %copy-start.8 = (f32[2,256]{1,0:T(2,128)S(1)}, f32[2,256]{1,0:T(2,128)}, u32[]{:S(2)}) copy-start(f32[2,256]{1,0:T(2,128)} %param.8) | copy-start | bytes 6148
  2.2 30.9 %all-to-all-start = ((bf16[32,64,128]{2,1,0:T(8,128)(2,1)}), bf16[32,64,128]{2,1,0:T(8,128)(2,1)S(1)}, u32[]{:S(2)}, u32[]{:S(2)}) async-start(bf16[32,64,128]{2,1,0:T(8,128)(2,1)} %bitcast.7), calls=%async_computation | async-start | bytes 1048576 | tf_op jit(solution)/shard_map/all_to_all | solution.py:196
  17.3 4.3 %copy-start.2 = (f32[16,4096]{1,0:T(8,128)S(1)}, f32[16,4096]{1,0:T(8,128)}, u32[]{:S(2)}) copy-start(f32[16,4096]{1,0:T(8,128)} %wave_ref.1) | copy-start | bytes 786436
  18.4 26.5 %copy-start.9 = (s32[2]{0:T(128)S(1)}, s32[2]{0:T(128)}, u32[]{:S(2)}) copy-start(s32[2]{0:T(128)} %param.11) | copy-start | bytes 28
  21.6 7.5 %collective-permute-start = (f32[8,4096]{1,0:T(8,128)S(1)}, f32[8,4096]{1,0:T(8,128)S(1)}, u32[]{:S(2)}, u32[]{:S(2)}) collective-permute-start(f32[8,4096]{1,0:T(8,128)S(1)} %get-tuple-element.14), channel_id=1, source_target_pairs={{0,1},{1,2},{2,3},{3,4},{4,5},{5,6},{6,7},{7,8},{8,9},{9,10},{10,1... | collective-permute-start | bytes 393224 | tf_op jit(solution)/shard_map/ppermute | solution.py:204
  23.5 7.4 %collective-permute-start.1 = (f32[8,4096]{1,0:T(8,128)S(1)}, f32[8,4096]{1,0:T(8,128)S(1)}, u32[]{:S(2)}, u32[]{:S(2)}) collective-permute-start(f32[8,4096]{1,0:T(8,128)S(1)} %get-tuple-element.15), channel_id=1, source_target_pairs={{1,0},{2,1},{3,2},{4,3},{5,4},{6,5},{7,6},{8,7},{9,8},{10,9},{11,1... | collective-permute-start | bytes 393224 | tf_op jit(solution)/shard_map/ppermute | solution.py:205
  29.1 50.8 %copy-start.5 = (f32[8,4096]{1,0:T(8,128)}, f32[8,4096]{1,0:T(8,128)S(1)}, u32[]{:S(2)}) copy-start(f32[8,4096]{1,0:T(8,128)S(1)} %collective-permute-done.wbelow_ref) | copy-start | bytes 393220
  30.9 49.0 %copy-start.6 = (f32[8,4096]{1,0:T(8,128)}, f32[8,4096]{1,0:T(8,128)S(1)}, u32[]{:S(2)}) copy-start(f32[8,4096]{1,0:T(8,128)S(1)} %collective-permute-done.1.wabove_ref) | copy-start | bytes 393220
  33.1 0.8 copy-start
  36.6 25.9 %all-to-all-start.1 = ((bf16[32,64,128]{2,1,0:T(8,128)(2,1)}), bf16[32,64,128]{2,1,0:T(8,128)(2,1)S(1)}, u32[]{:S(2)}, u32[]{:S(2)}) async-start(bf16[32,64,128]{2,1,0:T(8,128)(2,1)} %bitcast.23), calls=%async_computation.1 | async-start | bytes 1048576 | tf_op jit(solution)/shard_map/all_to_all | solution.py:208
  62.5 0.8 copy-start.1
  65.6 9.4 %collective-permute-start.3 = (f32[2,2,8,4096]{3,2,1,0:T(8,128)}, f32[2,2,8,4096]{3,2,1,0:T(8,128)S(1)}, u32[]{:S(2)}, u32[]{:S(2)}) collective-permute-start(f32[2,2,8,4096]{3,2,1,0:T(8,128)} %get-tuple-element.17.lo_ref), channel_id=1, source_target_pairs={{1,0},{2,1},{3,2},{4,3},{5,4},{6,5},{7,6},{8,7},{9,8},{10,9},{11,1... | collective-permute-start | bytes 1572872 | tf_op jit(solution)/shard_map/ppermute | solution.py:224
  67.9 11.9 %collective-permute-start.2 = (f32[2,2,8,4096]{3,2,1,0:T(8,128)}, f32[2,2,8,4096]{3,2,1,0:T(8,128)S(1)}, u32[]{:S(2)}, u32[]{:S(2)}) collective-permute-start(f32[2,2,8,4096]{3,2,1,0:T(8,128)} %get-tuple-element.18.hi_ref), channel_id=1, source_target_pairs={{0,1},{1,2},{2,3},{3,4},{4,5},{5,6},{6,7},{7,8},{8,9},{9,10},{10,1... | collective-permute-start | bytes 1572872 | tf_op jit(solution)/shard_map/ppermute | solution.py:223
  74.9 4.9 %copy-start.3 = (f32[2,2,8,4096]{3,2,1,0:T(8,128)}, f32[2,2,8,4096]{3,2,1,0:T(8,128)S(1)}, u32[]{:S(2)}) copy-start(f32[2,2,8,4096]{3,2,1,0:T(8,128)S(1)} %collective-permute-done.3.above_ref) | copy-start | bytes 1572868
  79.9 0.8 copy-start.4

commit v5 on v3

--- a/solution.py
+++ b/solution.py
@@ -10,7 +10,7 @@
 GY = 64
 SWEEPS = 6
 HALO = 8
-LANES = 128
+LANES = 512
 PAD = 128
 
 damping = 0.3
@@ -172,7 +172,7 @@
                 dst_pair[1][:, pl.ds(PAD + c0, width)] = new_im
             return carry
 
-        lax.fori_loop(0, chunks, chunk, 0)
+        lax.fori_loop(0, chunks, chunk, 0, unroll=True)
 
     pairs = ((are_ref, aim_ref), (bre_ref, bim_ref))
     for k in range(SWEEPS - 1):

time: 122 us -> 94.6 us (0.78)
  Pallas kernels: 45.6 us -> 18.5 us
    pallas_call x1, Pallas kernels: 40.7 us -> 13.5 us  [sweeps(): pl.pallas_call(functools.partial(sweep_kernel, depth), out_shape=jax.Shap...]
  transfers between devices with their start and end apart: 6 -> 6, of which waited for: 6 -> 6; matrix products, arithmetic and copies ran while one was open for 6% -> 8% of each run, Pallas kernels for 0% -> 0%
where the time goes in v5:
time: 94.6 us; the launch traced here: 94.1 us
  starting transfers between devices  32.5 us (34%)
  waiting for transfers between devices  30.8 us (33%)
  Pallas kernels  18.5 us (20%)
  local copies, waits for them, and re-layouts  9.79 us (10%)
  matrix products  1.54 us (2%)
    all_to_all x1, waiting for transfers between devices, local(): lax.all_to_all(mixed.reshape(nsta, owned * parts * depth, lanes), 'sta',...  16.9 us
    pallas_call x1, Pallas kernels, sweeps(): pl.pallas_call(functools.partial(sweep_kernel, depth), out_shape=jax.Shap...  13.5 us
    all_to_all x1, starting transfers between devices, local(): recv = lax.all_to_all(send, 'sta', 0, 0, tiled=True)  13.2 us
    all_to_all x1, starting transfers between devices, local(): lax.all_to_all(mixed.reshape(nsta, owned * parts * depth, lanes), 'sta',...  8.3 us
    ppermute x1, waiting for transfers between devices, local(): above = lax.ppermute(lo, 'slab', down_pairs)  5.06 us
    ppermute x1, waiting for transfers between devices, local(): below = lax.ppermute(hi, 'slab', up_pairs)  4.92 us
    ppermute x1, starting transfers between devices, local(): wabove = lax.ppermute(wave_lo, 'slab', down_pairs)  4.85 us
    unnamed x21, local copies, waits for them, and re-layouts  3.56 us
  transfers between devices with their start and end apart: 6, of which 6 were waited for; matrix products, arithmetic and copies ran while one was open for 8% of the time, Pallas kernels for 0%

profile of v5, /device:TPU:32, one launch (start us, length us, event | category | flops | bytes accessed | tf_op | source)
XLA Modules:
  0.0 94.1 jit_solution(6217451444724625347)
XLA Ops:
  0.0 1.2 %copy.13 = bf16[8,8,32,128]{3,2,1,0:T(8,128)(2,1)S(1)} copy(bf16[8,8,32,128]{3,1,2,0:T(8,128)(2,1)} %bitcast.25) | data formatting | bytes 1048576
  1.2 1.0 %copy.11 = bf16[32,2,2,16,128]{4,3,2,1,0:T(8,128)(2,1)} copy(bf16[32,2,2,16,128]{4,0,3,2,1:T(8,128)(2,1)S(1)} %bitcast.24) | data formatting | bytes 1048576 | tf_op jit(solution)/shard_map/transpose | solution.py:222
  2.2 13.2 %all-to-all-start = ((bf16[32,64,128]{2,1,0:T(8,128)(2,1)}), bf16[32,64,128]{2,1,0:T(8,128)(2,1)S(1)}, u32[]{:S(2)}, u32[]{:S(2)}) async-start(bf16[32,64,128]{2,1,0:T(8,128)(2,1)} %bitcast.7), calls=%async_computation | async-start | bytes 1048576 | tf_op jit(solution)/shard_map/all_to_all | solution.py:223
  17.3 1.1 %copy.10 = bf16[64,2,32,2,2]{1,0,4,3,2:T(8,128)(2,1)S(1)} copy(bf16[64,2,32,2,2]{0,1,4,2,3:T(2,128)(2,1)S(1)} %bitcast.26) | data formatting | bytes 65536 | tf_op jit(solution)/shard_map/transpose | solution.py:226
  18.4 3.2 %reshape.21 = bf16[128,128]{0,1:T(8,128)(2,1)S(1)} reshape(bf16[64,2,32,2,2]{1,0,4,3,2:T(8,128)(2,1)S(1)} %copy.10) | data formatting | bytes 65536 | tf_op jit(solution)/shard_map/reshape | solution.py:227
  21.6 1.9 %collective-permute-start = (f32[8,4096]{1,0:T(8,128)S(1)}, f32[8,4096]{1,0:T(8,128)S(1)}, u32[]{:S(2)}, u32[]{:S(2)}) collective-permute-start(f32[8,4096]{1,0:T(8,128)S(1)} %get-tuple-element.14), channel_id=1, source_target_pairs={{0,1},{1,2},{2,3},{3,4},{4,5},{5,6},{6,7},{7,8},{8,9},{9,10},{10,1... | collective-permute-start | bytes 393224 | tf_op jit(solution)/shard_map/ppermute | solution.py:231
  23.5 4.9 %collective-permute-start.1 = (f32[8,4096]{1,0:T(8,128)S(1)}, f32[8,4096]{1,0:T(8,128)S(1)}, u32[]{:S(2)}, u32[]{:S(2)}) collective-permute-start(f32[8,4096]{1,0:T(8,128)S(1)} %get-tuple-element.15), channel_id=1, source_target_pairs={{1,0},{2,1},{3,2},{4,3},{5,4},{6,5},{7,6},{8,7},{9,8},{10,9},{11,1... | collective-permute-start | bytes 393224 | tf_op jit(solution)/shard_map/ppermute | solution.py:232
  28.4 0.7 collective-permute-done.wbelow_ref
  29.1 1.8 %collective-permute-done.1.wabove_ref = f32[8,4096]{1,0:T(8,128)S(1)} collective-permute-done((f32[8,4096]{1,0:T(8,128)S(1)}, f32[8,4096]{1,0:T(8,128)S(1)}, u32[]{:S(2)}, u32[]{:S(2)}) %collective-permute-start.1) | collective-permute-done | bytes 131104 | tf_op jit(solution)/shard_map/ppermute | solution.py:232
  30.9 0.7 copy.12.big_ref
  31.6 1.5 %all-to-all-done = bf16[32,64,128]{2,1,0:T(8,128)(2,1)S(1)} async-done(((bf16[32,64,128]{2,1,0:T(8,128)(2,1)}), bf16[32,64,128]{2,1,0:T(8,128)(2,1)S(1)}, u32[]{:S(2)}, u32[]{:S(2)}) %all-to-all-start) | async-done | bytes 524320 | tf_op jit(solution)/shard_map/all_to_all | solution.py:223
  33.1 0.8 copy-done
  33.9 2.7 %shard_map.64 = bf16[2048,128]{1,0:T(8,128)(2,1)} custom-call(bf16[128,128]{1,0:T(8,128)(2,1)} %copy.12.big_ref, bf16[2048,128]{1,0:T(8,128)(2,1)} %bitcast.22), custom_call_target="tpu_custom_call" | custom-call | flops 67108864 | bytes 1048576 | tf_op jit(solution)/shard_map/pallas_call | solution.py:55
  36.6 8.3 %all-to-all-start.1 = ((bf16[32,64,128]{2,1,0:T(8,128)(2,1)}), bf16[32,64,128]{2,1,0:T(8,128)(2,1)S(1)}, u32[]{:S(2)}, u32[]{:S(2)}) async-start(bf16[32,64,128]{2,1,0:T(8,128)(2,1)} %bitcast.23), calls=%async_computation.1 | async-start | bytes 1048576 | tf_op jit(solution)/shard_map/all_to_all | solution.py:235
  44.9 0.7 pad_add_fusion.meta_ref
  45.6 16.9 %all-to-all-done.1.recv_ref = bf16[32,64,128]{2,1,0:T(8,128)(2,1)S(1)} async-done(((bf16[32,64,128]{2,1,0:T(8,128)(2,1)}), bf16[32,64,128]{2,1,0:T(8,128)(2,1)S(1)}, u32[]{:S(2)}, u32[]{:S(2)}) %all-to-all-start.1) | async-done | bytes 524320 | tf_op jit(solution)/shard_map/all_to_all | solution.py:235
  62.5 0.8 copy-done.1
  63.3 2.3 %shard_map.65 = (f32[2,2,8,4096]{3,2,1,0:T(8,128)}, f32[2,2,8,4096]{3,2,1,0:T(8,128)}) custom-call(s32[4]{0:T(128)} %pad_add_fusion.meta_ref, bf16[32,64,128]{2,1,0:T(8,128)(2,1)} %copy-done.1, f32[16,4096]{1,0:T(8,128)} %noise_ref.1), custom_call_target="tpu_custom_call" | custom-call | tf_op jit(solution)/shard_map/pallas_call | solution.py:241
  65.6 2.4 %collective-permute-start.3 = (f32[2,2,8,4096]{3,2,1,0:T(8,128)}, f32[2,2,8,4096]{3,2,1,0:T(8,128)S(1)}, u32[]{:S(2)}, u32[]{:S(2)}) collective-permute-start(f32[2,2,8,4096]{3,2,1,0:T(8,128)} %get-tuple-element.17.lo_ref), channel_id=1, source_target_pairs={{1,0},{2,1},{3,2},{4,3},{5,4},{6,5},{7,6},{8,7},{9,8},{10,9},{11,1... | collective-permute-start | bytes 1572872 | tf_op jit(solution)/shard_map/ppermute | solution.py:251
  67.9 1.9 %collective-permute-start.2 = (f32[2,2,8,4096]{3,2,1,0:T(8,128)}, f32[2,2,8,4096]{3,2,1,0:T(8,128)S(1)}, u32[]{:S(2)}, u32[]{:S(2)}) collective-permute-start(f32[2,2,8,4096]{3,2,1,0:T(8,128)} %get-tuple-element.18.hi_ref), channel_id=1, source_target_pairs={{0,1},{1,2},{2,3},{3,4},{4,5},{5,6},{6,7},{7,8},{8,9},{9,10},{10,1... | collective-permute-start | bytes 1572872 | tf_op jit(solution)/shard_map/ppermute | solution.py:250
  69.9 5.1 %collective-permute-done.3.above_ref = f32[2,2,8,4096]{3,2,1,0:T(8,128)S(1)} collective-permute-done((f32[2,2,8,4096]{3,2,1,0:T(8,128)}, f32[2,2,8,4096]{3,2,1,0:T(8,128)S(1)}, u32[]{:S(2)}, u32[]{:S(2)}) %collective-permute-start.3) | collective-permute-done | bytes 524320 | tf_op jit(solution)/shard_map/ppermute | solution.py:251
  74.9 4.9 %collective-permute-done.2.below_ref = f32[2,2,8,4096]{3,2,1,0:T(8,128)S(1)} collective-permute-done((f32[2,2,8,4096]{3,2,1,0:T(8,128)}, f32[2,2,8,4096]{3,2,1,0:T(8,128)S(1)}, u32[]{:S(2)}, u32[]{:S(2)}) %collective-permute-start.2) | collective-permute-done | bytes 524320 | tf_op jit(solution)/shard_map/ppermute | solution.py:250
  79.9 0.8 copy-done.4
  80.7 13.5 %shard_map.66 = f32[2,2,16,4096]{3,2,1,0:T(8,128)} custom-call(s32[4]{0:T(128)} %pad_add_fusion.meta_ref, f32[2,2,8,4096]{3,2,1,0:T(8,128)} %get-tuple-element.17.lo_ref, f32[2,2,8,4096]{3,2,1,0:T(8,128)} %get-tuple-element.18.hi_ref, f32[2,2,8,4096]{3,2,1,0:T(8,128)} %copy-done.4, f32[2,2,8,4096]{3,2,1,0:T(8,128)} %copy-done.3, f32[16,4096]{1,0:T(8,128)} %wave_ref.1, ...), custom_call_target="tpu_custom_call" | custom-call | flops 94371840 | bytes 3145728 | tf_op jit(solution)/shard_map/pallas_call | solution.py:198
  (27 shorter events, 1.9 us)
Async XLA Ops:
  0.0 15.4 %copy-start.7 = (s32[256,2]{0,1:T(2,128)S(1)}, s32[256,2]{0,1:T(2,128)}, u32[]{:S(2)}) copy-start(s32[256,2]{0,1:T(2,128)} %param.7) | copy-start | bytes 6148
  0.0 15.4 %copy-start.8 = (f32[2,256]{1,0:T(2,128)S(1)}, f32[2,256]{1,0:T(2,128)}, u32[]{:S(2)}) copy-start(f32[2,256]{1,0:T(2,128)} %param.8) | copy-start | bytes 6148
  2.2 30.9 %all-to-all-start = ((bf16[32,64,128]{2,1,0:T(8,128)(2,1)}), bf16[32,64,128]{2,1,0:T(8,128)(2,1)S(1)}, u32[]{:S(2)}, u32[]{:S(2)}) async-start(bf16[32,64,128]{2,1,0:T(8,128)(2,1)} %bitcast.7), calls=%async_computation | async-start | bytes 1048576 | tf_op jit(solution)/shard_map/all_to_all | solution.py:223
  17.3 4.3 %copy-start.2 = (f32[16,4096]{1,0:T(8,128)S(1)}, f32[16,4096]{1,0:T(8,128)}, u32[]{:S(2)}) copy-start(f32[16,4096]{1,0:T(8,128)} %wave_ref.1) | copy-start | bytes 786436
  18.4 26.5 %copy-start.9 = (s32[2]{0:T(128)S(1)}, s32[2]{0:T(128)}, u32[]{:S(2)}) copy-start(s32[2]{0:T(128)} %param.11) | copy-start | bytes 28
  21.6 7.5 %collective-permute-start = (f32[8,4096]{1,0:T(8,128)S(1)}, f32[8,4096]{1,0:T(8,128)S(1)}, u32[]{:S(2)}, u32[]{:S(2)}) collective-permute-start(f32[8,4096]{1,0:T(8,128)S(1)} %get-tuple-element.14), channel_id=1, source_target_pairs={{0,1},{1,2},{2,3},{3,4},{4,5},{5,6},{6,7},{7,8},{8,9},{9,10},{10,1... | collective-permute-start | bytes 393224 | tf_op jit(solution)/shard_map/ppermute | solution.py:231
  23.5 7.4 %collective-permute-start.1 = (f32[8,4096]{1,0:T(8,128)S(1)}, f32[8,4096]{1,0:T(8,128)S(1)}, u32[]{:S(2)}, u32[]{:S(2)}) collective-permute-start(f32[8,4096]{1,0:T(8,128)S(1)} %get-tuple-element.15), channel_id=1, source_target_pairs={{1,0},{2,1},{3,2},{4,3},{5,4},{6,5},{7,6},{8,7},{9,8},{10,9},{11,1... | collective-permute-start | bytes 393224 | tf_op jit(solution)/shard_map/ppermute | solution.py:232
  29.1 50.8 %copy-start.5 = (f32[8,4096]{1,0:T(8,128)}, f32[8,4096]{1,0:T(8,128)S(1)}, u32[]{:S(2)}) copy-start(f32[8,4096]{1,0:T(8,128)S(1)} %collective-permute-done.wbelow_ref) | copy-start | bytes 393220
  30.9 49.0 %copy-start.6 = (f32[8,4096]{1,0:T(8,128)}, f32[8,4096]{1,0:T(8,128)S(1)}, u32[]{:S(2)}) copy-start(f32[8,4096]{1,0:T(8,128)S(1)} %collective-permute-done.1.wabove_ref) | copy-start | bytes 393220
  33.1 0.8 copy-start
  36.6 25.9 %all-to-all-start.1 = ((bf16[32,64,128]{2,1,0:T(8,128)(2,1)}), bf16[32,64,128]{2,1,0:T(8,128)(2,1)S(1)}, u32[]{:S(2)}, u32[]{:S(2)}) async-start(bf16[32,64,128]{2,1,0:T(8,128)(2,1)} %bitcast.23), calls=%async_computation.1 | async-start | bytes 1048576 | tf_op jit(solution)/shard_map/all_to_all | solution.py:235
  62.5 0.8 copy-start.1
  65.6 9.4 %collective-permute-start.3 = (f32[2,2,8,4096]{3,2,1,0:T(8,128)}, f32[2,2,8,4096]{3,2,1,0:T(8,128)S(1)}, u32[]{:S(2)}, u32[]{:S(2)}) collective-permute-start(f32[2,2,8,4096]{3,2,1,0:T(8,128)} %get-tuple-element.17.lo_ref), channel_id=1, source_target_pairs={{1,0},{2,1},{3,2},{4,3},{5,4},{6,5},{7,6},{8,7},{9,8},{10,9},{11,1... | collective-permute-start | bytes 1572872 | tf_op jit(solution)/shard_map/ppermute | solution.py:251
  67.9 11.9 %collective-permute-start.2 = (f32[2,2,8,4096]{3,2,1,0:T(8,128)}, f32[2,2,8,4096]{3,2,1,0:T(8,128)S(1)}, u32[]{:S(2)}, u32[]{:S(2)}) collective-permute-start(f32[2,2,8,4096]{3,2,1,0:T(8,128)} %get-tuple-element.18.hi_ref), channel_id=1, source_target_pairs={{0,1},{1,2},{2,3},{3,4},{4,5},{5,6},{6,7},{7,8},{8,9},{9,10},{10,1... | collective-permute-start | bytes 1572872 | tf_op jit(solution)/shard_map/ppermute | solution.py:250
  74.9 4.9 %copy-start.3 = (f32[2,2,8,4096]{3,2,1,0:T(8,128)}, f32[2,2,8,4096]{3,2,1,0:T(8,128)S(1)}, u32[]{:S(2)}) copy-start(f32[2,2,8,4096]{3,2,1,0:T(8,128)S(1)} %collective-permute-done.3.above_ref) | copy-start | bytes 1572868
  79.9 0.8 copy-start.4

commit v6 on v5

--- a/solution.py
+++ b/solution.py
@@ -67,31 +67,31 @@
     )(big, recv)
 
 
-def source_kernel(owned, depth, meta_ref, recv_ref, noise_ref, lo_ref, hi_ref):
+def source_kernel(depth, b, meta_ref, recv_ref, noise_ref, lo_ref, hi_ref):
     pieces, _, lanes = recv_ref.shape
     half = depth // 2
     slab = meta_ref[0]
+    spot_at = meta_ref[2 + b]
     row = lax.broadcasted_iota(jnp.int32, (depth, lanes), 0)
     lane = lax.broadcasted_iota(jnp.int32, (depth, lanes), 1)
     base = (slab * depth + row) * (pieces * lanes) + lane
-    for b in range(owned):
-        spot_at = meta_ref[2 + b]
-        for part in range(2):
-            start = (b * 2 + part) * depth
-            for ct in range(pieces):
-                cols = slice(ct * lanes, (ct + 1) * lanes)
-                tile = recv_ref[ct, start : start + depth, :].astype(jnp.float32)
-                value = noise_ref[:, cols] * tile
-                if part == 0:
-                    hit = base + ct * lanes == spot_at
-                    value = value + jnp.where(hit, point_size, 0.0)
-                lo_ref[b, part, :, cols] = value[:half]
-                hi_ref[b, part, :, cols] = value[half:]
-
-
-def sweep_kernel(depth, meta_ref, lo_ref, hi_ref, below_ref, above_ref, wave_ref, wbelow_ref,
-                 wabove_ref, out_ref, are_ref, aim_ref, bre_ref, bim_ref, sre_ref, sim_ref, w_ref,
-                 sr_ref, si_ref):
+    for part in range(2):
+        for ct in range(pieces):
+            cols = slice(ct * lanes, (ct + 1) * lanes)
+            tile = recv_ref[ct, part * depth : (part + 1) * depth, :].astype(jnp.float32)
+            value = noise_ref[:, cols] * tile
+            if part == 0:
+                hit = base + ct * lanes == spot_at
+                value = value + jnp.where(hit, point_size, 0.0)
+            lo_ref[0, part, :, cols] = value[:half]
+            hi_ref[0, part, :, cols] = value[half:]
+
+
+def sweep_kernel(depth, aliased, meta_ref, lo_ref, hi_ref, below_ref, above_ref, wave_ref,
+                 wbelow_ref, wabove_ref, *refs):
+    if aliased:
+        refs = refs[1:]
+    out_ref, are_ref, aim_ref, bre_ref, bim_ref, sre_ref, sim_ref, w_ref, sr_ref, si_ref = refs
     half = depth // 2
     rows, cells = sre_ref.shape
     width = LANES
@@ -179,32 +179,40 @@
         sweep(pairs[k % 2], pairs[(k + 1) % 2], k == SWEEPS - 2)
 
 
-def sweeps(meta, lo, hi, below, above, wave, wbelow, wabove):
-    owned, _, half, cells = lo.shape
+def sweeps(meta, lo, hi, below, above, wave, wbelow, wabove, b, owned, prev):
+    _, _, half, cells = lo.shape
     depth = 2 * half
     rows = depth + 2 * HALO
-    piece = pl.BlockSpec((1, 2, half, cells), lambda b, *_: (b, 0, 0, 0))
-    halo = pl.BlockSpec((1, 2, HALO, cells), lambda b, *_: (b, 0, 0, 0))
-    whole = lambda shape: pl.BlockSpec(shape, lambda b, *_: (0,) * len(shape))
+    piece = pl.BlockSpec((1, 2, half, cells), lambda i, *_: (0, 0, 0, 0))
+    halo = pl.BlockSpec((1, 2, HALO, cells), lambda i, *_: (0, 0, 0, 0))
+    whole = lambda shape: pl.BlockSpec(shape, lambda i, *_: (0,) * len(shape))
+    in_specs = [piece, piece, halo, halo, whole((depth, cells)), whole((HALO, cells)),
+                whole((HALO, cells))]
+    operands = [meta, lo, hi, below, above, wave, wbelow, wabove]
+    aliases = {}
+    if prev is not None:
+        in_specs.append(pl.BlockSpec(memory_space=pl.ANY))
+        aliases = {len(operands): 0}
+        operands.append(prev)
     grid_spec = pltpu.PrefetchScalarGridSpec(
         num_scalar_prefetch=1,
-        grid=(owned,),
-        in_specs=[piece, piece, halo, halo, whole((depth, cells)), whole((HALO, cells)),
-                  whole((HALO, cells))],
-        out_specs=pl.BlockSpec((2, 1, depth, cells), lambda b, *_: (0, b, 0, 0)),
+        grid=(1,),
+        in_specs=in_specs,
+        out_specs=pl.BlockSpec((2, 1, depth, cells), lambda i, *_: (0, b, 0, 0)),
         scratch_shapes=[pltpu.VMEM((rows, cells + 2 * PAD), jnp.float32) for _ in range(4)]
         + [pltpu.VMEM((rows, cells), jnp.float32) for _ in range(5)],
     )
     return pl.pallas_call(
-        functools.partial(sweep_kernel, depth),
+        functools.partial(sweep_kernel, depth, prev is not None),
         out_shape=jax.ShapeDtypeStruct((2, owned, depth, cells), jnp.float32),
         grid_spec=grid_spec,
+        input_output_aliases=aliases,
         cost_estimate=pl.CostEstimate(
-            flops=owned * SWEEPS * 60 * rows * cells,
-            bytes_accessed=owned * 4 * cells * (6 * depth),
+            flops=SWEEPS * 60 * rows * cells,
+            bytes_accessed=4 * cells * (6 * depth),
             transcendentals=0,
         ),
-    )(meta, lo, hi, below, above, wave, wbelow, wabove)
+    )(*operands)
 
 
 def local(green_fields, pair_list, pair_values, noise_map, wave_square, station_cell):
@@ -223,7 +231,7 @@
     recv = lax.all_to_all(send, "sta", 0, 0, tiled=True)
 
     big = build_resid(pair_list, pair_values, count)
-    big = big.reshape(2, count, 2, nsta, owned).transpose(1, 0, 3, 2, 4)
+    big = big.reshape(2, nsta, owned, 2, nsta, owned).transpose(2, 1, 0, 4, 3, 5)
     big = big.reshape(2 * count, 2 * count)
     big, wave_hi, wave_lo = lax.optimization_barrier(
         (big, wave_square[depth - HALO :], wave_square[:HALO])
@@ -232,24 +240,26 @@
     wabove = lax.ppermute(wave_lo, "slab", down_pairs)
     big, wbelow, wabove = lax.optimization_barrier((big, wbelow, wabove))
     mixed = mix(big, recv.reshape(nsta * parts * owned * depth, lanes), depth)
-    back = lax.all_to_all(mixed.reshape(nsta, owned * parts * depth, lanes), "sta", 0, 0,
-                          tiled=True)
-
+    mixed = mixed.reshape(owned, nsta, parts * depth, lanes)
     meta = jnp.concatenate(
         [jnp.stack([slab, jnp.int32(nslab)]).astype(jnp.int32), station_cell.astype(jnp.int32)]
     )
-    lo, hi = pl.pallas_call(
-        functools.partial(source_kernel, owned, depth),
-        out_shape=[jax.ShapeDtypeStruct((owned, 2, half, cells), jnp.float32)] * 2,
-        in_specs=[
-            pl.BlockSpec(memory_space=pltpu.SMEM),
-            pl.BlockSpec(memory_space=pltpu.VMEM),
-            pl.BlockSpec(memory_space=pltpu.VMEM),
-        ],
-    )(meta, back, noise_map)
-    below = lax.ppermute(hi, "slab", up_pairs)
-    above = lax.ppermute(lo, "slab", down_pairs)
-    return sweeps(meta, lo, hi, below, above, wave_square, wbelow, wabove)
+    out = None
+    for b in range(owned):
+        back = lax.all_to_all(mixed[b], "sta", 0, 0, tiled=True)
+        lo, hi = pl.pallas_call(
+            functools.partial(source_kernel, depth, b),
+            out_shape=[jax.ShapeDtypeStruct((1, 2, half, cells), jnp.float32)] * 2,
+            in_specs=[
+                pl.BlockSpec(memory_space=pltpu.SMEM),
+                pl.BlockSpec(memory_space=pltpu.VMEM),
+                pl.BlockSpec(memory_space=pltpu.VMEM),
+            ],
+        )(meta, back, noise_map)
+        below = lax.ppermute(hi, "slab", up_pairs)
+        above = lax.ppermute(lo, "slab", down_pairs)
+        out = sweeps(meta, lo, hi, below, above, wave_square, wbelow, wabove, b, owned, out)
+    return out
 
 
 def solution(mesh):

time: 94.6 us -> 137 us (1.45)
  the two profiles are of different devices: /device:TPU:32 before, /device:TPU:1 now
where the time goes in v6:
time: 137 us
  local copies, waits for them, and re-layouts  45.6 us (33%)
  starting transfers between devices  37.8 us (28%)
  Pallas kernels  22.7 us (17%)
  blocking collectives  20.6 us (15%)
  waiting for transfers between devices  7.76 us (6%)
  matrix products  1.54 us (1%)
    transpose x1, local copies, waits for them, and re-layouts, local(): big.reshape(2, nsta, owned, 2, nsta, owned).transpose(2, 1, 0, 4, 3, 5)  27.9 us
    all_to_all x1, blocking collectives, local(): back = lax.all_to_all(mixed[b], 'sta', 0, 0, tiled=True)  20.6 us
    pallas_call x2, Pallas kernels, sweeps(): pl.pallas_call(functools.partial(sweep_kernel, depth, prev is not None),...  16.1 us
    all_to_all x1, starting transfers between devices, local(): recv = lax.all_to_all(send, 'sta', 0, 0, tiled=True)  13.7 us
    ppermute x2, starting transfers between devices, local(): below = lax.ppermute(hi, 'slab', up_pairs)  10.2 us
    unnamed x25, local copies, waits for them, and re-layouts  5.48 us
    reshape x1, local copies, waits for them, and re-layouts, local(): big.reshape(2, nsta, owned, 2, nsta, owned).transpose(2, 1, 0, 4, 3, 5)  4.54 us
    ppermute x1, waiting for transfers between devices, local(): wabove = lax.ppermute(wave_lo, 'slab', down_pairs)  4.34 us
  transfers between devices with their start and end apart: 8, of which 2 were waited for; matrix products, arithmetic and copies ran while one was open for 29% of the time, Pallas kernels for 9%

profile of v6, /device:TPU:1, one launch (start us, length us, event | category | flops | bytes accessed | tf_op | source)
XLA Modules:
  0.0 136.8 jit_solution(4773077566824070836)
XLA Ops:
  0.0 1.2 copy.13
  1.2 1.0 copy.11
  2.2 13.7 %all-to-all-start = ((bf16[32,64,128]{2,1,0:T(8,128)(2,1)}), bf16[32,64,128]{2,1,0:T(8,128)(2,1)S(1)}, u32[]{:S(2)}, u32[]{:S(2)}) async-start(bf16[32,64,128]{2,1,0:T(8,128)(2,1)} %bitcast.7), calls=%async_computation | async-start | bytes 1048576 | tf_op jit(solution)/shard_map/all_to_all | solution.py:231
  17.6 4.5 %reshape.22 = bf16[2,32,2,2,32,2]{5,4,3,2,1,0:T(8,128)(2,1)S(1)} reshape(bf16[128,128]{1,0:T(8,128)(2,1)S(1)} %maximum_maximum_fusion) | data formatting | bytes 65536 | tf_op jit(solution)/shard_map/reshape | solution.py:234
  22.1 27.9 %copy.10 = bf16[2,32,2,32,2,2]{2,1,0,5,4,3:T(8,128)(2,1)} copy(bf16[2,32,2,32,2,2]{5,3,4,0,1,2:T(8,128)(2,1)S(1)} %bitcast.21) | data formatting | bytes 65536 | tf_op jit(solution)/shard_map/transpose | solution.py:234
  50.0 4.2 %reshape.23 = bf16[128,128]{0,1:T(8,128)(2,1)S(1)} reshape(bf16[2,32,2,32,2,2]{2,1,0,5,4,3:T(8,128)(2,1)} %copy.10) | data formatting | bytes 65536 | tf_op jit(solution)/shard_map/reshape | solution.py:235
  54.3 4.0 %collective-permute-start = (f32[8,4096]{1,0:T(8,128)S(1)}, f32[8,4096]{1,0:T(8,128)S(1)}, u32[]{:S(2)}, u32[]{:S(2)}) collective-permute-start(f32[8,4096]{1,0:T(8,128)S(1)} %get-tuple-element.16), channel_id=1, source_target_pairs={{0,1},{1,2},{2,3},{3,4},{4,5},{5,6},{6,7},{7,8},{8,9},{9,10},{10,1... | collective-permute-start | bytes 393224 | tf_op jit(solution)/shard_map/ppermute | solution.py:239
  58.3 1.9 %collective-permute-start.1 = (f32[8,4096]{1,0:T(8,128)S(1)}, f32[8,4096]{1,0:T(8,128)S(1)}, u32[]{:S(2)}, u32[]{:S(2)}) collective-permute-start(f32[8,4096]{1,0:T(8,128)S(1)} %get-tuple-element.17), channel_id=1, source_target_pairs={{1,0},{2,1},{3,2},{4,3},{5,4},{6,5},{7,6},{8,7},{9,8},{10,9},{11,1... | collective-permute-start | bytes 393224 | tf_op jit(solution)/shard_map/ppermute | solution.py:240
  60.3 4.3 %collective-permute-done.1.wabove_ref = f32[8,4096]{1,0:T(8,128)S(1)} collective-permute-done((f32[8,4096]{1,0:T(8,128)S(1)}, f32[8,4096]{1,0:T(8,128)S(1)}, u32[]{:S(2)}, u32[]{:S(2)}) %collective-permute-start.1) | collective-permute-done | bytes 131104 | tf_op jit(solution)/shard_map/ppermute | solution.py:240
  64.6 0.7 copy.12.big_ref
  65.3 0.8 copy-done.1
  66.1 2.7 %shard_map.64 = bf16[2048,128]{1,0:T(8,128)(2,1)} custom-call(bf16[128,128]{1,0:T(8,128)(2,1)} %copy.12.big_ref, bf16[2048,128]{1,0:T(8,128)(2,1)} %bitcast.22), custom_call_target="tpu_custom_call" | custom-call | flops 67108864 | bytes 1048576 | tf_op jit(solution)/shard_map/pallas_call | solution.py:55
  68.9 1.8 %fusion.28 = (bf16[1024,128]{1,0:T(8,128)(2,1)S(1)}, bf16[1024,128]{1,0:T(8,128)(2,1)}) fusion(bf16[2048,128]{1,0:T(8,128)(2,1)} %shard_map.64), kind=kLoop, calls=%fused_computation.34 | loop fusion | bytes 1048576 | tf_op jit(solution)/shard_map/slice | solution.py:249
  70.6 20.6 %all_to_all.15.recv_ref = bf16[32,32,128]{2,1,0:T(8,128)(2,1)} all-to-all(bf16[32,32,128]{2,1,0:T(8,128)(2,1)S(1)} %bitcast.24), channel_id=1, replica_groups=mesh['sta'=32,'slab'=16] {'sta'}, dimensions={0} | all-to-all | bytes 524288 | tf_op jit(solution)/shard_map/all_to_all | solution.py:249
  91.2 3.9 %all-to-all-start.1 = ((bf16[32,32,128]{2,1,0:T(8,128)(2,1)}), bf16[32,32,128]{2,1,0:T(8,128)(2,1)S(1)}, u32[]{:S(2)}, u32[]{:S(2)}) async-start(bf16[32,32,128]{2,1,0:T(8,128)(2,1)} %bitcast.9), calls=%async_computation.1 | async-start | bytes 524288 | tf_op jit(solution)/shard_map/all_to_all | solution.py:249
  95.6 1.9 %shard_map.66 = (f32[1,2,8,4096]{3,2,1,0:T(8,128)}, f32[1,2,8,4096]{3,2,1,0:T(8,128)}) custom-call(s32[4]{0:T(128)} %pad_add_fusion.meta_ref, bf16[32,32,128]{2,1,0:T(8,128)(2,1)} %all_to_all.15.recv_ref, f32[16,4096]{1,0:T(8,128)} %noise_ref.3), custom_call_target="tpu_custom_call" | custom-call | tf_op jit(solution)/shard_map/pallas_call | solution.py:250
  97.6 4.4 %collective-permute-start.4 = (f32[1,2,8,4096]{3,2,1,0:T(8,128)}, f32[1,2,8,4096]{3,2,1,0:T(8,128)S(1)}, u32[]{:S(2)}, u32[]{:S(2)}) collective-permute-start(f32[1,2,8,4096]{3,2,1,0:T(8,128)} %get-tuple-element.24.hi_ref), channel_id=1, source_target_pairs={{0,1},{1,2},{2,3},{3,4},{4,5},{5,6},{6,7},{7,8},{8,9},{9,10},{10,1... | collective-permute-start | bytes 786440 | tf_op jit(solution)/shard_map/ppermute | solution.py:259
  102.0 1.9 %collective-permute-start.5 = (f32[1,2,8,4096]{3,2,1,0:T(8,128)}, f32[1,2,8,4096]{3,2,1,0:T(8,128)S(1)}, u32[]{:S(2)}, u32[]{:S(2)}) collective-permute-start(f32[1,2,8,4096]{3,2,1,0:T(8,128)} %get-tuple-element.23.lo_ref), channel_id=1, source_target_pairs={{1,0},{2,1},{3,2},{4,3},{5,4},{6,5},{7,6},{8,7},{9,8},{10,9},{11,1... | collective-permute-start | bytes 786440 | tf_op jit(solution)/shard_map/ppermute | solution.py:260
  103.9 3.4 %all-to-all-done.1.recv_ref = bf16[32,32,128]{2,1,0:T(8,128)(2,1)S(1)} async-done(((bf16[32,32,128]{2,1,0:T(8,128)(2,1)}), bf16[32,32,128]{2,1,0:T(8,128)(2,1)S(1)}, u32[]{:S(2)}, u32[]{:S(2)}) %all-to-all-start.1) | async-done | bytes 262176 | tf_op jit(solution)/shard_map/all_to_all | solution.py:249
  108.0 1.9 %shard_map.65 = (f32[1,2,8,4096]{3,2,1,0:T(8,128)}, f32[1,2,8,4096]{3,2,1,0:T(8,128)}) custom-call(s32[4]{0:T(128)} %pad_add_fusion.meta_ref, bf16[32,32,128]{2,1,0:T(8,128)(2,1)} %copy-done.2, f32[16,4096]{1,0:T(8,128)} %noise_ref.3), custom_call_target="tpu_custom_call" | custom-call | tf_op jit(solution)/shard_map/pallas_call | solution.py:250
  109.9 5.8 %collective-permute-start.2 = (f32[1,2,8,4096]{3,2,1,0:T(8,128)}, f32[1,2,8,4096]{3,2,1,0:T(8,128)S(1)}, u32[]{:S(2)}, u32[]{:S(2)}) collective-permute-start(f32[1,2,8,4096]{3,2,1,0:T(8,128)} %get-tuple-element.20.hi_ref), channel_id=1, source_target_pairs={{0,1},{1,2},{2,3},{3,4},{4,5},{5,6},{6,7},{7,8},{8,9},{9,10},{10,1... | collective-permute-start | bytes 786440 | tf_op jit(solution)/shard_map/ppermute | solution.py:259
  115.8 2.1 %collective-permute-start.3 = (f32[1,2,8,4096]{3,2,1,0:T(8,128)}, f32[1,2,8,4096]{3,2,1,0:T(8,128)S(1)}, u32[]{:S(2)}, u32[]{:S(2)}) collective-permute-start(f32[1,2,8,4096]{3,2,1,0:T(8,128)} %get-tuple-element.19.lo_ref), channel_id=1, source_target_pairs={{1,0},{2,1},{3,2},{4,3},{5,4},{6,5},{7,6},{8,7},{9,8},{10,9},{11,1... | collective-permute-start | bytes 786440 | tf_op jit(solution)/shard_map/ppermute | solution.py:260
  119.3 8.1 %shard_map.67.refs_0_ = f32[2,2,16,4096]{3,2,1,0:T(8,128)} custom-call(s32[4]{0:T(128)} %pad_add_fusion.meta_ref, f32[1,2,8,4096]{3,2,1,0:T(8,128)} %get-tuple-element.23.lo_ref, f32[1,2,8,4096]{3,2,1,0:T(8,128)} %get-tuple-element.24.hi_ref, f32[1,2,8,4096]{3,2,1,0:T(8,128)} %copy-done.5, f32[1,2,8,4096]{3,2,1,0:T(8,128)} %copy-done.6, ...), custom_call_target="tpu_custom_call" | custom-call | flops 47185920 | bytes 1572864 | tf_op jit(solution)/shard_map/pallas_call | solution.py:205
  128.8 8.1 %shard_map.68 = f32[2,2,16,4096]{3,2,1,0:T(8,128)} custom-call(s32[4]{0:T(128)} %pad_add_fusion.meta_ref, f32[1,2,8,4096]{3,2,1,0:T(8,128)} %get-tuple-element.19.lo_ref, f32[1,2,8,4096]{3,2,1,0:T(8,128)} %get-tuple-element.20.hi_ref, f32[1,2,8,4096]{3,2,1,0:T(8,128)} %copy-done.7, f32[1,2,8,4096]{3,2,1,0:T(8,128)} %copy-done.8, ...), custom_call_target="tpu_custom_call", output_to_operand_aliasing={{}: (8, {})} | custom-call | flops 47185920 | bytes 1572864 | tf_op jit(solution)/shard_map/pallas_call | solution.py:205
  (38 shorter events, 5.8 us)
Async XLA Ops:
  0.0 15.9 %copy-start.9 = (s32[256,2]{0,1:T(2,128)S(1)}, s32[256,2]{0,1:T(2,128)}, u32[]{:S(2)}) copy-start(s32[256,2]{0,1:T(2,128)} %param.7) | copy-start | bytes 6148
  0.0 15.9 %copy-start.10 = (f32[2,256]{1,0:T(2,128)S(1)}, f32[2,256]{1,0:T(2,128)}, u32[]{:S(2)}) copy-start(f32[2,256]{1,0:T(2,128)} %param.8) | copy-start | bytes 6148
  2.2 63.2 %all-to-all-start = ((bf16[32,64,128]{2,1,0:T(8,128)(2,1)}), bf16[32,64,128]{2,1,0:T(8,128)(2,1)S(1)}, u32[]{:S(2)}, u32[]{:S(2)}) async-start(bf16[32,64,128]{2,1,0:T(8,128)(2,1)} %bitcast.7), calls=%async_computation | async-start | bytes 1048576 | tf_op jit(solution)/shard_map/all_to_all | solution.py:231
  50.0 4.2 %copy-start = (f32[16,4096]{1,0:T(8,128)S(1)}, f32[16,4096]{1,0:T(8,128)}, u32[]{:S(2)}) copy-start(f32[16,4096]{1,0:T(8,128)} %wave_ref.3) | copy-start | bytes 786436
  54.2 40.8 %copy-start.11 = (s32[2]{0:T(128)S(1)}, s32[2]{0:T(128)}, u32[]{:S(2)}) copy-start(s32[2]{0:T(128)} %param.11) | copy-start | bytes 28
  54.3 6.0 %collective-permute-start = (f32[8,4096]{1,0:T(8,128)S(1)}, f32[8,4096]{1,0:T(8,128)S(1)}, u32[]{:S(2)}, u32[]{:S(2)}) collective-permute-start(f32[8,4096]{1,0:T(8,128)S(1)} %get-tuple-element.16), channel_id=1, source_target_pairs={{0,1},{1,2},{2,3},{3,4},{4,5},{5,6},{6,7},{7,8},{8,9},{9,10},{10,1... | collective-permute-start | bytes 393224 | tf_op jit(solution)/shard_map/ppermute | solution.py:239
  58.3 6.3 %collective-permute-start.1 = (f32[8,4096]{1,0:T(8,128)S(1)}, f32[8,4096]{1,0:T(8,128)S(1)}, u32[]{:S(2)}, u32[]{:S(2)}) collective-permute-start(f32[8,4096]{1,0:T(8,128)S(1)} %get-tuple-element.17), channel_id=1, source_target_pairs={{1,0},{2,1},{3,2},{4,3},{5,4},{6,5},{7,6},{8,7},{9,8},{10,9},{11,1... | collective-permute-start | bytes 393224 | tf_op jit(solution)/shard_map/ppermute | solution.py:240
  60.3 57.6 %copy-start.3 = (f32[8,4096]{1,0:T(8,128)}, f32[8,4096]{1,0:T(8,128)S(1)}, u32[]{:S(2)}) copy-start(f32[8,4096]{1,0:T(8,128)S(1)} %collective-permute-done.wbelow_ref) | copy-start | bytes 393220
  64.6 53.3 %copy-start.4 = (f32[8,4096]{1,0:T(8,128)}, f32[8,4096]{1,0:T(8,128)S(1)}, u32[]{:S(2)}) copy-start(f32[8,4096]{1,0:T(8,128)S(1)} %collective-permute-done.1.wabove_ref) | copy-start | bytes 393220
  65.3 0.8 copy-start.1
  91.2 16.1 %all-to-all-start.1 = ((bf16[32,32,128]{2,1,0:T(8,128)(2,1)}), bf16[32,32,128]{2,1,0:T(8,128)(2,1)S(1)}, u32[]{:S(2)}, u32[]{:S(2)}) async-start(bf16[32,32,128]{2,1,0:T(8,128)(2,1)} %bitcast.9), calls=%async_computation.1 | async-start | bytes 524288 | tf_op jit(solution)/shard_map/all_to_all | solution.py:249
  97.6 20.3 %collective-permute-start.4 = (f32[1,2,8,4096]{3,2,1,0:T(8,128)}, f32[1,2,8,4096]{3,2,1,0:T(8,128)S(1)}, u32[]{:S(2)}, u32[]{:S(2)}) collective-permute-start(f32[1,2,8,4096]{3,2,1,0:T(8,128)} %get-tuple-element.24.hi_ref), channel_id=1, source_target_pairs={{0,1},{1,2},{2,3},{3,4},{4,5},{5,6},{6,7},{7,8},{8,9},{9,10},{10,1... | collective-permute-start | bytes 786440 | tf_op jit(solution)/shard_map/ppermute | solution.py:259
  102.0 15.9 %collective-permute-start.5 = (f32[1,2,8,4096]{3,2,1,0:T(8,128)}, f32[1,2,8,4096]{3,2,1,0:T(8,128)S(1)}, u32[]{:S(2)}, u32[]{:S(2)}) collective-permute-start(f32[1,2,8,4096]{3,2,1,0:T(8,128)} %get-tuple-element.23.lo_ref), channel_id=1, source_target_pairs={{1,0},{2,1},{3,2},{4,3},{5,4},{6,5},{7,6},{8,7},{9,8},{10,9},{11,1... | collective-permute-start | bytes 786440 | tf_op jit(solution)/shard_map/ppermute | solution.py:260
  107.3 0.7 copy-start.2
  109.9 17.4 %collective-permute-start.2 = (f32[1,2,8,4096]{3,2,1,0:T(8,128)}, f32[1,2,8,4096]{3,2,1,0:T(8,128)S(1)}, u32[]{:S(2)}, u32[]{:S(2)}) collective-permute-start(f32[1,2,8,4096]{3,2,1,0:T(8,128)} %get-tuple-element.20.hi_ref), channel_id=1, source_target_pairs={{0,1},{1,2},{2,3},{3,4},{4,5},{5,6},{6,7},{7,8},{8,9},{9,10},{10,1... | collective-permute-start | bytes 786440 | tf_op jit(solution)/shard_map/ppermute | solution.py:259
  115.8 11.6 %collective-permute-start.3 = (f32[1,2,8,4096]{3,2,1,0:T(8,128)}, f32[1,2,8,4096]{3,2,1,0:T(8,128)S(1)}, u32[]{:S(2)}, u32[]{:S(2)}) collective-permute-start(f32[1,2,8,4096]{3,2,1,0:T(8,128)} %get-tuple-element.19.lo_ref), channel_id=1, source_target_pairs={{1,0},{2,1},{3,2},{4,3},{5,4},{6,5},{7,6},{8,7},{9,8},{10,9},{11,1... | collective-permute-start | bytes 786440 | tf_op jit(solution)/shard_map/ppermute | solution.py:260
  117.9 0.7 copy-start.5
  118.6 0.7 copy-start.6
  127.3 0.7 copy-start.7
  128.1 0.7 copy-start.8

commit v7 on v5

--- a/solution.py
+++ b/solution.py
@@ -223,8 +223,15 @@
     recv = lax.all_to_all(send, "sta", 0, 0, tiled=True)
 
     big = build_resid(pair_list, pair_values, count)
-    big = big.reshape(2, count, 2, nsta, owned).transpose(1, 0, 3, 2, 4)
-    big = big.reshape(2 * count, 2 * count)
+    size = 2 * count
+    new = jnp.arange(size, dtype=jnp.int32)
+    old_row = (new % 2) * count + new // 2
+    src, rest = new // (2 * owned), new % (2 * owned)
+    old_col = (rest // owned) * count + src * owned + rest % owned
+    pick_rows = (old_row[:, None] == new[None, :]).astype(jnp.bfloat16)
+    pick_cols = (new[:, None] == old_col[None, :]).astype(jnp.bfloat16)
+    big = jnp.dot(pick_rows, big, preferred_element_type=jnp.float32).astype(jnp.bfloat16)
+    big = jnp.dot(big, pick_cols, preferred_element_type=jnp.float32).astype(jnp.bfloat16)
     big, wave_hi, wave_lo = lax.optimization_barrier(
         (big, wave_square[depth - HALO :], wave_square[:HALO])
     )

time: 94.6 us -> 92.1 us (0.974)
  local copies, waits for them, and re-layouts: 9.79 us -> 5.88 us
  waiting for transfers between devices: 30.8 us -> 34.3 us
  starting transfers between devices: 32.5 us -> 29.7 us
    all_to_all x1, waiting for transfers between devices: 1.48 us -> 5.21 us  [local(): recv = lax.all_to_all(send, 'sta', 0, 0, tiled=True)]
    all_to_all x1, starting transfers between devices: 8.3 us -> 4.64 us  [local(): lax.all_to_all(mixed.reshape(nsta, owned * parts * depth, lanes), 'sta',...]
    reshape x2 -> x0, local copies, waits for them, and re-layouts: 3.25 us -> none  [the longest x1 3.16 us: local(): big = big.reshape(2 * count, 2 * count)]
    unnamed x21, local copies, waits for them, and re-layouts: 3.56 us -> 4.86 us
    transpose x1 -> x0, local copies, waits for them, and re-layouts: 1.11 us -> none  [local(): big = big.reshape(2, count, 2, nsta, owned).transpose(1, 0, 3, 2, 4)]
  transfers between devices with their start and end apart: 6 -> 6, of which waited for: 6 -> 6; matrix products, arithmetic and copies ran while one was open for 8% -> 3% of each run, Pallas kernels for 0% -> 0%
where the time goes in v7:
time: 92.1 us; the launch traced here: 91.6 us
  waiting for transfers between devices  34.3 us (37%)
  starting transfers between devices  29.7 us (32%)
  Pallas kernels  18.4 us (20%)
  local copies, waits for them, and re-layouts  5.88 us (6%)
  matrix products  2.48 us (3%)
    all_to_all x1, waiting for transfers between devices, local(): lax.all_to_all(mixed.reshape(nsta, owned * parts * depth, lanes), 'sta',...  16.6 us
    pallas_call x1, Pallas kernels, sweeps(): pl.pallas_call(functools.partial(sweep_kernel, depth), out_shape=jax.Shap...  13.5 us
    all_to_all x1, starting transfers between devices, local(): recv = lax.all_to_all(send, 'sta', 0, 0, tiled=True)  13.3 us
    all_to_all x1, waiting for transfers between devices, local(): recv = lax.all_to_all(send, 'sta', 0, 0, tiled=True)  5.21 us
    ppermute x1, waiting for transfers between devices, local(): above = lax.ppermute(lo, 'slab', down_pairs)  5.07 us
    ppermute x1, waiting for transfers between devices, local(): below = lax.ppermute(hi, 'slab', up_pairs)  4.92 us
    unnamed x21, local copies, waits for them, and re-layouts  4.86 us
    ppermute x1, starting transfers between devices, local(): wabove = lax.ppermute(wave_lo, 'slab', down_pairs)  4.85 us
  transfers between devices with their start and end apart: 6, of which 6 were waited for; matrix products, arithmetic and copies ran while one was open for 3% of the time, Pallas kernels for 0%

profile of v7, /device:TPU:32, one launch (start us, length us, event | category | flops | bytes accessed | tf_op | source)
XLA Modules:
  0.0 91.6 jit_solution(16651241770529105358)
XLA Ops:
  0.0 1.1 %copy.8 = bf16[8,8,32,128]{3,2,1,0:T(8,128)(2,1)S(1)} copy(bf16[8,8,32,128]{3,1,2,0:T(8,128)(2,1)} %bitcast.18) | data formatting | bytes 1048576
  1.1 1.0 %copy.7 = bf16[32,2,2,16,128]{4,3,2,1,0:T(8,128)(2,1)} copy(bf16[32,2,2,16,128]{4,0,3,2,1:T(8,128)(2,1)S(1)} %bitcast.17) | data formatting | bytes 1048576 | tf_op jit(solution)/shard_map/transpose | solution.py:222
  2.1 13.3 %all-to-all-start = ((bf16[32,64,128]{2,1,0:T(8,128)(2,1)}), bf16[32,64,128]{2,1,0:T(8,128)(2,1)S(1)}, u32[]{:S(2)}, u32[]{:S(2)}) async-start(bf16[32,64,128]{2,1,0:T(8,128)(2,1)} %bitcast.6), calls=%async_computation | async-start | bytes 1048576 | tf_op jit(solution)/shard_map/all_to_all | solution.py:223
  15.5 0.7 copy-done.8
  17.7 0.9 %convolution_convert_fusion.big_ref = bf16[128,128]{1,0:T(8,128)(2,1)} fusion(bf16[64,64]{1,0:T(8,128)(2,1)S(1)} %fusion, bf16[64,64]{1,0:T(8,128)(2,1)S(1)} %get-tuple-element.28, bf16[64,64]{1,0:T(8,128)(2,1)S(1)} %get-tuple-element.27, s32[128]{0:T(128)S(1)} %get-tuple-element.30, s32[128]{0:T(128)S(1)} %get-tuple-element.29), kind=kOutput, calls=%fused_computation | convolution fusion | flops 8585216 | bytes 58368 | tf_op jit(solution)/shard_map/dot_general | solution.py:234
  18.7 1.9 %collective-permute-start = (f32[8,4096]{1,0:T(8,128)S(1)}, f32[8,4096]{1,0:T(8,128)S(1)}, u32[]{:S(2)}, u32[]{:S(2)}) collective-permute-start(f32[8,4096]{1,0:T(8,128)S(1)} %get-tuple-element.14), channel_id=1, source_target_pairs={{0,1},{1,2},{2,3},{3,4},{4,5},{5,6},{6,7},{7,8},{8,9},{9,10},{10,1... | collective-permute-start | bytes 393224 | tf_op jit(solution)/shard_map/ppermute | solution.py:238
  20.6 4.9 %collective-permute-start.1 = (f32[8,4096]{1,0:T(8,128)S(1)}, f32[8,4096]{1,0:T(8,128)S(1)}, u32[]{:S(2)}, u32[]{:S(2)}) collective-permute-start(f32[8,4096]{1,0:T(8,128)S(1)} %get-tuple-element.15), channel_id=1, source_target_pairs={{1,0},{2,1},{3,2},{4,3},{5,4},{6,5},{7,6},{8,7},{9,8},{10,9},{11,1... | collective-permute-start | bytes 393224 | tf_op jit(solution)/shard_map/ppermute | solution.py:239
  25.5 0.7 collective-permute-done.wbelow_ref
  26.2 1.8 %collective-permute-done.1.wabove_ref = f32[8,4096]{1,0:T(8,128)S(1)} collective-permute-done((f32[8,4096]{1,0:T(8,128)S(1)}, f32[8,4096]{1,0:T(8,128)S(1)}, u32[]{:S(2)}, u32[]{:S(2)}) %collective-permute-start.1) | collective-permute-done | bytes 131104 | tf_op jit(solution)/shard_map/ppermute | solution.py:239
  28.0 5.2 %all-to-all-done = bf16[32,64,128]{2,1,0:T(8,128)(2,1)S(1)} async-done(((bf16[32,64,128]{2,1,0:T(8,128)(2,1)}), bf16[32,64,128]{2,1,0:T(8,128)(2,1)S(1)}, u32[]{:S(2)}, u32[]{:S(2)}) %all-to-all-start) | async-done | bytes 524320 | tf_op jit(solution)/shard_map/all_to_all | solution.py:223
  33.2 0.8 copy-done
  34.0 2.7 %shard_map.64 = bf16[2048,128]{1,0:T(8,128)(2,1)} custom-call(bf16[128,128]{1,0:T(8,128)(2,1)} %convolution_convert_fusion.big_ref, bf16[2048,128]{1,0:T(8,128)(2,1)} %bitcast.15), custom_call_target="tpu_custom_call" | custom-call | flops 67108864 | bytes 1048576 | tf_op jit(solution)/shard_map/pallas_call | solution.py:55
  36.7 4.6 %all-to-all-start.1 = ((bf16[32,64,128]{2,1,0:T(8,128)(2,1)}), bf16[32,64,128]{2,1,0:T(8,128)(2,1)S(1)}, u32[]{:S(2)}, u32[]{:S(2)}) async-start(bf16[32,64,128]{2,1,0:T(8,128)(2,1)} %bitcast.16), calls=%async_computation.1 | async-start | bytes 1048576 | tf_op jit(solution)/shard_map/all_to_all | solution.py:242
  41.4 0.6 copy-done.9
  42.0 0.7 pad_add_fusion.meta_ref
  42.7 16.6 %all-to-all-done.1.recv_ref = bf16[32,64,128]{2,1,0:T(8,128)(2,1)S(1)} async-done(((bf16[32,64,128]{2,1,0:T(8,128)(2,1)}), bf16[32,64,128]{2,1,0:T(8,128)(2,1)S(1)}, u32[]{:S(2)}, u32[]{:S(2)}) %all-to-all-start.1) | async-done | bytes 524320 | tf_op jit(solution)/shard_map/all_to_all | solution.py:242
  59.3 0.8 copy-done.1
  60.1 2.3 %shard_map.65 = (f32[2,2,8,4096]{3,2,1,0:T(8,128)}, f32[2,2,8,4096]{3,2,1,0:T(8,128)}) custom-call(s32[4]{0:T(128)} %pad_add_fusion.meta_ref, bf16[32,64,128]{2,1,0:T(8,128)(2,1)} %copy-done.1, f32[16,4096]{1,0:T(8,128)} %noise_ref.1), custom_call_target="tpu_custom_call" | custom-call | tf_op jit(solution)/shard_map/pallas_call | solution.py:248
  62.3 3.0 %collective-permute-start.3 = (f32[2,2,8,4096]{3,2,1,0:T(8,128)}, f32[2,2,8,4096]{3,2,1,0:T(8,128)S(1)}, u32[]{:S(2)}, u32[]{:S(2)}) collective-permute-start(f32[2,2,8,4096]{3,2,1,0:T(8,128)} %get-tuple-element.17.lo_ref), channel_id=1, source_target_pairs={{1,0},{2,1},{3,2},{4,3},{5,4},{6,5},{7,6},{8,7},{9,8},{10,9},{11,1... | collective-permute-start | bytes 1572872 | tf_op jit(solution)/shard_map/ppermute | solution.py:258
  65.4 1.9 %collective-permute-start.2 = (f32[2,2,8,4096]{3,2,1,0:T(8,128)}, f32[2,2,8,4096]{3,2,1,0:T(8,128)S(1)}, u32[]{:S(2)}, u32[]{:S(2)}) collective-permute-start(f32[2,2,8,4096]{3,2,1,0:T(8,128)} %get-tuple-element.18.hi_ref), channel_id=1, source_target_pairs={{0,1},{1,2},{2,3},{3,4},{4,5},{5,6},{6,7},{7,8},{8,9},{9,10},{10,1... | collective-permute-start | bytes 1572872 | tf_op jit(solution)/shard_map/ppermute | solution.py:257
  67.3 5.1 %collective-permute-done.3.above_ref = f32[2,2,8,4096]{3,2,1,0:T(8,128)S(1)} collective-permute-done((f32[2,2,8,4096]{3,2,1,0:T(8,128)}, f32[2,2,8,4096]{3,2,1,0:T(8,128)S(1)}, u32[]{:S(2)}, u32[]{:S(2)}) %collective-permute-start.3) | collective-permute-done | bytes 524320 | tf_op jit(solution)/shard_map/ppermute | solution.py:258
  72.4 4.9 %collective-permute-done.2.below_ref = f32[2,2,8,4096]{3,2,1,0:T(8,128)S(1)} collective-permute-done((f32[2,2,8,4096]{3,2,1,0:T(8,128)}, f32[2,2,8,4096]{3,2,1,0:T(8,128)S(1)}, u32[]{:S(2)}, u32[]{:S(2)}) %collective-permute-start.2) | collective-permute-done | bytes 524320 | tf_op jit(solution)/shard_map/ppermute | solution.py:257
  77.3 0.8 copy-done.4
  78.1 13.5 %shard_map.66 = f32[2,2,16,4096]{3,2,1,0:T(8,128)} custom-call(s32[4]{0:T(128)} %pad_add_fusion.meta_ref, f32[2,2,8,4096]{3,2,1,0:T(8,128)} %get-tuple-element.17.lo_ref, f32[2,2,8,4096]{3,2,1,0:T(8,128)} %get-tuple-element.18.hi_ref, f32[2,2,8,4096]{3,2,1,0:T(8,128)} %copy-done.4, f32[2,2,8,4096]{3,2,1,0:T(8,128)} %copy-done.3, f32[16,4096]{1,0:T(8,128)} %wave_ref.1, ...), custom_call_target="tpu_custom_call" | custom-call | flops 94371840 | bytes 3145728 | tf_op jit(solution)/shard_map/pallas_call | solution.py:198
  (23 shorter events, 1.6 us)
Async XLA Ops:
  2.1 13.3 %copy-start.7 = (s32[256,2]{0,1:T(2,128)S(1)}, s32[256,2]{0,1:T(2,128)}, u32[]{:S(2)}) copy-start(s32[256,2]{0,1:T(2,128)} %param.7) | copy-start | bytes 6148
  2.1 31.1 %all-to-all-start = ((bf16[32,64,128]{2,1,0:T(8,128)(2,1)}), bf16[32,64,128]{2,1,0:T(8,128)(2,1)S(1)}, u32[]{:S(2)}, u32[]{:S(2)}) async-start(bf16[32,64,128]{2,1,0:T(8,128)(2,1)} %bitcast.6), calls=%async_computation | async-start | bytes 1048576 | tf_op jit(solution)/shard_map/all_to_all | solution.py:223
  15.5 0.7 copy-start.8
  17.0 1.7 %copy-start.2 = (f32[16,4096]{1,0:T(8,128)S(1)}, f32[16,4096]{1,0:T(8,128)}, u32[]{:S(2)}) copy-start(f32[16,4096]{1,0:T(8,128)} %wave_ref.1) | copy-start | bytes 786436
  18.7 7.5 %collective-permute-start = (f32[8,4096]{1,0:T(8,128)S(1)}, f32[8,4096]{1,0:T(8,128)S(1)}, u32[]{:S(2)}, u32[]{:S(2)}) collective-permute-start(f32[8,4096]{1,0:T(8,128)S(1)} %get-tuple-element.14), channel_id=1, source_target_pairs={{0,1},{1,2},{2,3},{3,4},{4,5},{5,6},{6,7},{7,8},{8,9},{9,10},{10,1... | collective-permute-start | bytes 393224 | tf_op jit(solution)/shard_map/ppermute | solution.py:238
  20.6 7.4 %collective-permute-start.1 = (f32[8,4096]{1,0:T(8,128)S(1)}, f32[8,4096]{1,0:T(8,128)S(1)}, u32[]{:S(2)}, u32[]{:S(2)}) collective-permute-start(f32[8,4096]{1,0:T(8,128)S(1)} %get-tuple-element.15), channel_id=1, source_target_pairs={{1,0},{2,1},{3,2},{4,3},{5,4},{6,5},{7,6},{8,7},{9,8},{10,9},{11,1... | collective-permute-start | bytes 393224 | tf_op jit(solution)/shard_map/ppermute | solution.py:239
  26.2 10.5 %copy-start.5 = (f32[8,4096]{1,0:T(8,128)}, f32[8,4096]{1,0:T(8,128)S(1)}, u32[]{:S(2)}) copy-start(f32[8,4096]{1,0:T(8,128)S(1)} %collective-permute-done.wbelow_ref) | copy-start | bytes 393220
  28.0 8.7 %copy-start.6 = (f32[8,4096]{1,0:T(8,128)}, f32[8,4096]{1,0:T(8,128)S(1)}, u32[]{:S(2)}) copy-start(f32[8,4096]{1,0:T(8,128)S(1)} %collective-permute-done.1.wabove_ref) | copy-start | bytes 393220
  33.2 0.8 copy-start
  36.7 22.5 %all-to-all-start.1 = ((bf16[32,64,128]{2,1,0:T(8,128)(2,1)}), bf16[32,64,128]{2,1,0:T(8,128)(2,1)S(1)}, u32[]{:S(2)}, u32[]{:S(2)}) async-start(bf16[32,64,128]{2,1,0:T(8,128)(2,1)} %bitcast.16), calls=%async_computation.1 | async-start | bytes 1048576 | tf_op jit(solution)/shard_map/all_to_all | solution.py:242
  41.4 0.7 copy-start.9
  59.3 0.8 copy-start.1
  62.3 10.0 %collective-permute-start.3 = (f32[2,2,8,4096]{3,2,1,0:T(8,128)}, f32[2,2,8,4096]{3,2,1,0:T(8,128)S(1)}, u32[]{:S(2)}, u32[]{:S(2)}) collective-permute-start(f32[2,2,8,4096]{3,2,1,0:T(8,128)} %get-tuple-element.17.lo_ref), channel_id=1, source_target_pairs={{1,0},{2,1},{3,2},{4,3},{5,4},{6,5},{7,6},{8,7},{9,8},{10,9},{11,1... | collective-permute-start | bytes 1572872 | tf_op jit(solution)/shard_map/ppermute | solution.py:258
  65.4 11.9 %collective-permute-start.2 = (f32[2,2,8,4096]{3,2,1,0:T(8,128)}, f32[2,2,8,4096]{3,2,1,0:T(8,128)S(1)}, u32[]{:S(2)}, u32[]{:S(2)}) collective-permute-start(f32[2,2,8,4096]{3,2,1,0:T(8,128)} %get-tuple-element.18.hi_ref), channel_id=1, source_target_pairs={{0,1},{1,2},{2,3},{3,4},{4,5},{5,6},{6,7},{7,8},{8,9},{9,10},{10,1... | collective-permute-start | bytes 1572872 | tf_op jit(solution)/shard_map/ppermute | solution.py:257
  72.4 4.9 %copy-start.3 = (f32[2,2,8,4096]{3,2,1,0:T(8,128)}, f32[2,2,8,4096]{3,2,1,0:T(8,128)S(1)}, u32[]{:S(2)}) copy-start(f32[2,2,8,4096]{3,2,1,0:T(8,128)S(1)} %collective-permute-done.3.above_ref) | copy-start | bytes 1572868
  77.3 0.8 copy-start.4

commit v8 on v7

--- a/solution.py
+++ b/solution.py
@@ -36,6 +36,16 @@
     upper = jnp.concatenate([resid_real, -resid_imag], axis=1)
     lower = jnp.concatenate([resid_imag, resid_real], axis=1)
     return jnp.concatenate([upper, lower], axis=0)
+
+
+def pack_kernel(green_ref, send_ref):
+    parts, owned, depth, cells = green_ref.shape
+    pieces, _, lanes = send_ref.shape
+    for part in range(parts):
+        for b in range(owned):
+            start = (part * owned + b) * depth
+            for ct in range(pieces):
+                send_ref[ct, start : start + depth, :] = green_ref[part, b, :, ct * lanes : (ct + 1) * lanes]
 
 
 def mix_kernel(depth, big_ref, recv_ref, out_ref, wide_ref, acc_ref):
@@ -218,8 +228,10 @@
     down_pairs = [(i + 1, i) for i in range(nslab - 1)]
     half = depth // 2
 
-    send = green_fields.reshape(parts, owned, depth, nsta, lanes)
-    send = send.transpose(3, 0, 1, 2, 4).reshape(nsta, parts * owned * depth, lanes)
+    send = pl.pallas_call(
+        pack_kernel,
+        out_shape=jax.ShapeDtypeStruct((nsta, parts * owned * depth, lanes), green_fields.dtype),
+    )(green_fields)
     recv = lax.all_to_all(send, "sta", 0, 0, tiled=True)
 
     big = build_resid(pair_list, pair_values, count)

time: 92.1 us -> 91.9 us (level)
  local copies, waits for them, and re-layouts: 5.88 us -> 3.75 us
  Pallas kernels: 18.4 us -> 20.4 us
    pallas_call x0 -> x1, Pallas kernels: none -> 1.92 us  [local(): pl.pallas_call(pack_kernel, out_shape=jax.ShapeDtypeStruct((nsta, parts *...]
    unnamed x21 -> x20, local copies, waits for them, and re-layouts: 4.86 us -> 3.72 us
    transpose x1 -> x0, local copies, waits for them, and re-layouts: 1 us -> none  [local(): send.transpose(3, 0, 1, 2, 4).reshape(nsta, parts * owned * depth, lanes)]
where the time goes in v8:
time: 91.9 us; the launch traced here: 91.3 us
  waiting for transfers between devices  34.3 us (37%)
  starting transfers between devices  29.7 us (32%)
  Pallas kernels  20.4 us (22%)
  local copies, waits for them, and re-layouts  3.75 us (4%)
  matrix products  2.48 us (3%)
    all_to_all x1, waiting for transfers between devices, local(): lax.all_to_all(mixed.reshape(nsta, owned * parts * depth, lanes), 'sta',...  16.6 us
    pallas_call x1, Pallas kernels, sweeps(): pl.pallas_call(functools.partial(sweep_kernel, depth), out_shape=jax.Shap...  13.5 us
    all_to_all x1, starting transfers between devices, local(): recv = lax.all_to_all(send, 'sta', 0, 0, tiled=True)  13.3 us
    all_to_all x1, waiting for transfers between devices, local(): recv = lax.all_to_all(send, 'sta', 0, 0, tiled=True)  5.21 us
    ppermute x1, waiting for transfers between devices, local(): above = lax.ppermute(lo, 'slab', down_pairs)  5.07 us
    ppermute x1, waiting for transfers between devices, local(): below = lax.ppermute(hi, 'slab', up_pairs)  4.92 us
    ppermute x1, starting transfers between devices, local(): wabove = lax.ppermute(wave_lo, 'slab', down_pairs)  4.85 us
    all_to_all x1, starting transfers between devices, local(): lax.all_to_all(mixed.reshape(nsta, owned * parts * depth, lanes), 'sta',...  4.64 us
  transfers between devices with their start and end apart: 6, of which 6 were waited for; matrix products, arithmetic and copies ran while one was open for 3% of the time, Pallas kernels for 0%

profile of v8, /device:TPU:32, one launch (start us, length us, event | category | flops | bytes accessed | tf_op | source)
XLA Modules:
  0.0 91.3 jit_solution(3013120176212767148)
XLA Ops:
  0.0 1.9 %shard_map.64 = bf16[32,64,128]{2,1,0:T(8,128)(2,1)} custom-call(bf16[2,2,16,4096]{3,2,1,0:T(8,128)(2,1)} %green_ref.1), custom_call_target="tpu_custom_call" | custom-call | tf_op jit(solution)/shard_map/pallas_call | solution.py:231
  1.9 13.3 %all-to-all-start = ((bf16[32,64,128]{2,1,0:T(8,128)(2,1)}), bf16[32,64,128]{2,1,0:T(8,128)(2,1)S(1)}, u32[]{:S(2)}, u32[]{:S(2)}) async-start(bf16[32,64,128]{2,1,0:T(8,128)(2,1)} %shard_map.64), calls=%async_computation | async-start | bytes 1048576 | tf_op jit(solution)/shard_map/all_to_all | solution.py:235
  15.3 0.7 copy-done.8
  17.1 0.4 fusion.55
  17.5 0.9 %convolution_convert_fusion.big_ref = bf16[128,128]{1,0:T(8,128)(2,1)} fusion(bf16[64,64]{1,0:T(8,128)(2,1)S(1)} %fusion, bf16[64,64]{1,0:T(8,128)(2,1)S(1)} %get-tuple-element.28, bf16[64,64]{1,0:T(8,128)(2,1)S(1)} %get-tuple-element.27, s32[128]{0:T(128)S(1)} %get-tuple-element.30, s32[128]{0:T(128)S(1)} %get-tuple-element.29), kind=kOutput, calls=%fused_computation | convolution fusion | flops 8585216 | bytes 58368 | tf_op jit(solution)/shard_map/dot_general | solution.py:246
  18.5 1.9 %collective-permute-start = (f32[8,4096]{1,0:T(8,128)S(1)}, f32[8,4096]{1,0:T(8,128)S(1)}, u32[]{:S(2)}, u32[]{:S(2)}) collective-permute-start(f32[8,4096]{1,0:T(8,128)S(1)} %get-tuple-element.14), channel_id=1, source_target_pairs={{0,1},{1,2},{2,3},{3,4},{4,5},{5,6},{6,7},{7,8},{8,9},{9,10},{10,1... | collective-permute-start | bytes 393224 | tf_op jit(solution)/shard_map/ppermute | solution.py:250
  20.4 4.9 %collective-permute-start.1 = (f32[8,4096]{1,0:T(8,128)S(1)}, f32[8,4096]{1,0:T(8,128)S(1)}, u32[]{:S(2)}, u32[]{:S(2)}) collective-permute-start(f32[8,4096]{1,0:T(8,128)S(1)} %get-tuple-element.15), channel_id=1, source_target_pairs={{1,0},{2,1},{3,2},{4,3},{5,4},{6,5},{7,6},{8,7},{9,8},{10,9},{11,1... | collective-permute-start | bytes 393224 | tf_op jit(solution)/shard_map/ppermute | solution.py:251
  25.3 0.7 collective-permute-done.wbelow_ref
  26.0 1.8 %collective-permute-done.1.wabove_ref = f32[8,4096]{1,0:T(8,128)S(1)} collective-permute-done((f32[8,4096]{1,0:T(8,128)S(1)}, f32[8,4096]{1,0:T(8,128)S(1)}, u32[]{:S(2)}, u32[]{:S(2)}) %collective-permute-start.1) | collective-permute-done | bytes 131104 | tf_op jit(solution)/shard_map/ppermute | solution.py:251
  27.8 5.2 %all-to-all-done = bf16[32,64,128]{2,1,0:T(8,128)(2,1)S(1)} async-done(((bf16[32,64,128]{2,1,0:T(8,128)(2,1)}), bf16[32,64,128]{2,1,0:T(8,128)(2,1)S(1)}, u32[]{:S(2)}, u32[]{:S(2)}) %all-to-all-start) | async-done | bytes 524320 | tf_op jit(solution)/shard_map/all_to_all | solution.py:235
  33.0 0.8 copy-done
  33.8 2.7 %shard_map.65 = bf16[2048,128]{1,0:T(8,128)(2,1)} custom-call(bf16[128,128]{1,0:T(8,128)(2,1)} %convolution_convert_fusion.big_ref, bf16[2048,128]{1,0:T(8,128)(2,1)} %bitcast.7), custom_call_target="tpu_custom_call" | custom-call | flops 67108864 | bytes 1048576 | tf_op jit(solution)/shard_map/pallas_call | solution.py:65
  36.5 4.6 %all-to-all-start.1 = ((bf16[32,64,128]{2,1,0:T(8,128)(2,1)}), bf16[32,64,128]{2,1,0:T(8,128)(2,1)S(1)}, u32[]{:S(2)}, u32[]{:S(2)}) async-start(bf16[32,64,128]{2,1,0:T(8,128)(2,1)} %bitcast.8), calls=%async_computation.1 | async-start | bytes 1048576 | tf_op jit(solution)/shard_map/all_to_all | solution.py:254
  41.2 0.6 copy-done.9
  41.8 0.7 pad_add_fusion.meta_ref
  42.5 16.6 %all-to-all-done.1.recv_ref = bf16[32,64,128]{2,1,0:T(8,128)(2,1)S(1)} async-done(((bf16[32,64,128]{2,1,0:T(8,128)(2,1)}), bf16[32,64,128]{2,1,0:T(8,128)(2,1)S(1)}, u32[]{:S(2)}, u32[]{:S(2)}) %all-to-all-start.1) | async-done | bytes 524320 | tf_op jit(solution)/shard_map/all_to_all | solution.py:254
  59.1 0.8 copy-done.1
  59.8 2.3 %shard_map.66 = (f32[2,2,8,4096]{3,2,1,0:T(8,128)}, f32[2,2,8,4096]{3,2,1,0:T(8,128)}) custom-call(s32[4]{0:T(128)} %pad_add_fusion.meta_ref, bf16[32,64,128]{2,1,0:T(8,128)(2,1)} %copy-done.1, f32[16,4096]{1,0:T(8,128)} %noise_ref.1), custom_call_target="tpu_custom_call" | custom-call | tf_op jit(solution)/shard_map/pallas_call | solution.py:260
  62.1 3.0 %collective-permute-start.3 = (f32[2,2,8,4096]{3,2,1,0:T(8,128)}, f32[2,2,8,4096]{3,2,1,0:T(8,128)S(1)}, u32[]{:S(2)}, u32[]{:S(2)}) collective-permute-start(f32[2,2,8,4096]{3,2,1,0:T(8,128)} %get-tuple-element.17.lo_ref), channel_id=1, source_target_pairs={{1,0},{2,1},{3,2},{4,3},{5,4},{6,5},{7,6},{8,7},{9,8},{10,9},{11,1... | collective-permute-start | bytes 1572872 | tf_op jit(solution)/shard_map/ppermute | solution.py:270
  65.1 1.9 %collective-permute-start.2 = (f32[2,2,8,4096]{3,2,1,0:T(8,128)}, f32[2,2,8,4096]{3,2,1,0:T(8,128)S(1)}, u32[]{:S(2)}, u32[]{:S(2)}) collective-permute-start(f32[2,2,8,4096]{3,2,1,0:T(8,128)} %get-tuple-element.18.hi_ref), channel_id=1, source_target_pairs={{0,1},{1,2},{2,3},{3,4},{4,5},{5,6},{6,7},{7,8},{8,9},{9,10},{10,1... | collective-permute-start | bytes 1572872 | tf_op jit(solution)/shard_map/ppermute | solution.py:269
  67.1 5.1 %collective-permute-done.3.above_ref = f32[2,2,8,4096]{3,2,1,0:T(8,128)S(1)} collective-permute-done((f32[2,2,8,4096]{3,2,1,0:T(8,128)}, f32[2,2,8,4096]{3,2,1,0:T(8,128)S(1)}, u32[]{:S(2)}, u32[]{:S(2)}) %collective-permute-start.3) | collective-permute-done | bytes 524320 | tf_op jit(solution)/shard_map/ppermute | solution.py:270
  72.1 4.9 %collective-permute-done.2.below_ref = f32[2,2,8,4096]{3,2,1,0:T(8,128)S(1)} collective-permute-done((f32[2,2,8,4096]{3,2,1,0:T(8,128)}, f32[2,2,8,4096]{3,2,1,0:T(8,128)S(1)}, u32[]{:S(2)}, u32[]{:S(2)}) %collective-permute-start.2) | collective-permute-done | bytes 524320 | tf_op jit(solution)/shard_map/ppermute | solution.py:269
  77.1 0.8 copy-done.4
  77.9 13.5 %shard_map.67 = f32[2,2,16,4096]{3,2,1,0:T(8,128)} custom-call(s32[4]{0:T(128)} %pad_add_fusion.meta_ref, f32[2,2,8,4096]{3,2,1,0:T(8,128)} %get-tuple-element.17.lo_ref, f32[2,2,8,4096]{3,2,1,0:T(8,128)} %get-tuple-element.18.hi_ref, f32[2,2,8,4096]{3,2,1,0:T(8,128)} %copy-done.4, f32[2,2,8,4096]{3,2,1,0:T(8,128)} %copy-done.3, f32[16,4096]{1,0:T(8,128)} %wave_ref.1, ...), custom_call_target="tpu_custom_call" | custom-call | flops 94371840 | bytes 3145728 | tf_op jit(solution)/shard_map/pallas_call | solution.py:208
  (22 shorter events, 1.2 us)
Async XLA Ops:
  1.9 13.3 %copy-start.7 = (s32[256,2]{0,1:T(2,128)S(1)}, s32[256,2]{0,1:T(2,128)}, u32[]{:S(2)}) copy-start(s32[256,2]{0,1:T(2,128)} %param.7) | copy-start | bytes 6148
  1.9 31.1 %all-to-all-start = ((bf16[32,64,128]{2,1,0:T(8,128)(2,1)}), bf16[32,64,128]{2,1,0:T(8,128)(2,1)S(1)}, u32[]{:S(2)}, u32[]{:S(2)}) async-start(bf16[32,64,128]{2,1,0:T(8,128)(2,1)} %shard_map.64), calls=%async_computation | async-start | bytes 1048576 | tf_op jit(solution)/shard_map/all_to_all | solution.py:235
  15.3 0.7 copy-start.8
  16.7 1.7 %copy-start.2 = (f32[16,4096]{1,0:T(8,128)S(1)}, f32[16,4096]{1,0:T(8,128)}, u32[]{:S(2)}) copy-start(f32[16,4096]{1,0:T(8,128)} %wave_ref.1) | copy-start | bytes 786436
  18.5 7.5 %collective-permute-start = (f32[8,4096]{1,0:T(8,128)S(1)}, f32[8,4096]{1,0:T(8,128)S(1)}, u32[]{:S(2)}, u32[]{:S(2)}) collective-permute-start(f32[8,4096]{1,0:T(8,128)S(1)} %get-tuple-element.14), channel_id=1, source_target_pairs={{0,1},{1,2},{2,3},{3,4},{4,5},{5,6},{6,7},{7,8},{8,9},{9,10},{10,1... | collective-permute-start | bytes 393224 | tf_op jit(solution)/shard_map/ppermute | solution.py:250
  20.4 7.4 %collective-permute-start.1 = (f32[8,4096]{1,0:T(8,128)S(1)}, f32[8,4096]{1,0:T(8,128)S(1)}, u32[]{:S(2)}, u32[]{:S(2)}) collective-permute-start(f32[8,4096]{1,0:T(8,128)S(1)} %get-tuple-element.15), channel_id=1, source_target_pairs={{1,0},{2,1},{3,2},{4,3},{5,4},{6,5},{7,6},{8,7},{9,8},{10,9},{11,1... | collective-permute-start | bytes 393224 | tf_op jit(solution)/shard_map/ppermute | solution.py:251
  26.0 10.5 %copy-start.5 = (f32[8,4096]{1,0:T(8,128)}, f32[8,4096]{1,0:T(8,128)S(1)}, u32[]{:S(2)}) copy-start(f32[8,4096]{1,0:T(8,128)S(1)} %collective-permute-done.wbelow_ref) | copy-start | bytes 393220
  27.8 8.7 %copy-start.6 = (f32[8,4096]{1,0:T(8,128)}, f32[8,4096]{1,0:T(8,128)S(1)}, u32[]{:S(2)}) copy-start(f32[8,4096]{1,0:T(8,128)S(1)} %collective-permute-done.1.wabove_ref) | copy-start | bytes 393220
  33.0 0.8 copy-start
  36.5 22.5 %all-to-all-start.1 = ((bf16[32,64,128]{2,1,0:T(8,128)(2,1)}), bf16[32,64,128]{2,1,0:T(8,128)(2,1)S(1)}, u32[]{:S(2)}, u32[]{:S(2)}) async-start(bf16[32,64,128]{2,1,0:T(8,128)(2,1)} %bitcast.8), calls=%async_computation.1 | async-start | bytes 1048576 | tf_op jit(solution)/shard_map/all_to_all | solution.py:254
  41.2 0.7 copy-start.9
  59.1 0.8 copy-start.1
  62.1 10.0 %collective-permute-start.3 = (f32[2,2,8,4096]{3,2,1,0:T(8,128)}, f32[2,2,8,4096]{3,2,1,0:T(8,128)S(1)}, u32[]{:S(2)}, u32[]{:S(2)}) collective-permute-start(f32[2,2,8,4096]{3,2,1,0:T(8,128)} %get-tuple-element.17.lo_ref), channel_id=1, source_target_pairs={{1,0},{2,1},{3,2},{4,3},{5,4},{6,5},{7,6},{8,7},{9,8},{10,9},{11,1... | collective-permute-start | bytes 1572872 | tf_op jit(solution)/shard_map/ppermute | solution.py:270
  65.1 11.9 %collective-permute-start.2 = (f32[2,2,8,4096]{3,2,1,0:T(8,128)}, f32[2,2,8,4096]{3,2,1,0:T(8,128)S(1)}, u32[]{:S(2)}, u32[]{:S(2)}) collective-permute-start(f32[2,2,8,4096]{3,2,1,0:T(8,128)} %get-tuple-element.18.hi_ref), channel_id=1, source_target_pairs={{0,1},{1,2},{2,3},{3,4},{4,5},{5,6},{6,7},{7,8},{8,9},{9,10},{10,1... | collective-permute-start | bytes 1572872 | tf_op jit(solution)/shard_map/ppermute | solution.py:269
  72.1 4.9 %copy-start.3 = (f32[2,2,8,4096]{3,2,1,0:T(8,128)}, f32[2,2,8,4096]{3,2,1,0:T(8,128)S(1)}, u32[]{:S(2)}) copy-start(f32[2,2,8,4096]{3,2,1,0:T(8,128)S(1)} %collective-permute-done.3.above_ref) | copy-start | bytes 1572868
  77.1 0.8 copy-start.4

commit v9 on v8

--- a/solution.py
+++ b/solution.py
@@ -249,10 +249,10 @@
     )
     wbelow = lax.ppermute(wave_hi, "slab", up_pairs)
     wabove = lax.ppermute(wave_lo, "slab", down_pairs)
-    big, wbelow, wabove = lax.optimization_barrier((big, wbelow, wabove))
     mixed = mix(big, recv.reshape(nsta * parts * owned * depth, lanes), depth)
     back = lax.all_to_all(mixed.reshape(nsta, owned * parts * depth, lanes), "sta", 0, 0,
                           tiled=True)
+    back, wbelow, wabove = lax.optimization_barrier((back, wbelow, wabove))
 
     meta = jnp.concatenate(
         [jnp.stack([slab, jnp.int32(nslab)]).astype(jnp.int32), station_cell.astype(jnp.int32)]

time: 91.9 us -> 89.8 us (0.977)
  waiting for transfers between devices: 34.3 us -> 32.9 us
    all_to_all x1, waiting for transfers between devices: 5.21 us -> 14.5 us  [local(): recv = lax.all_to_all(send, 'sta', 0, 0, tiled=True)]
    all_to_all x1, waiting for transfers between devices: 16.6 us -> 7.71 us  [local(): lax.all_to_all(mixed.reshape(nsta, owned * parts * depth, lanes), 'sta',...]
    ppermute x1, starting transfers between devices: 3.03 us -> 1.91 us  [local(): above = lax.ppermute(lo, 'slab', down_pairs)]
  transfers between devices with their start and end apart: 6 -> 6, of which waited for: 6 -> 5; matrix products, arithmetic and copies ran while one was open for 3% -> 4% of each run, Pallas kernels for 0% -> 0%
where the time goes in v9:
time: 89.8 us; the launch traced here: 89.3 us
  waiting for transfers between devices  32.9 us (37%)
  starting transfers between devices  29 us (32%)
  Pallas kernels  20.4 us (23%)
  local copies, waits for them, and re-layouts  3.75 us (4%)
  matrix products  2.48 us (3%)
    all_to_all x1, waiting for transfers between devices, local(): recv = lax.all_to_all(send, 'sta', 0, 0, tiled=True)  14.5 us
    pallas_call x1, Pallas kernels, sweeps(): pl.pallas_call(functools.partial(sweep_kernel, depth), out_shape=jax.Shap...  13.5 us
    all_to_all x1, starting transfers between devices, local(): recv = lax.all_to_all(send, 'sta', 0, 0, tiled=True)  13.3 us
    all_to_all x1, waiting for transfers between devices, local(): lax.all_to_all(mixed.reshape(nsta, owned * parts * depth, lanes), 'sta',...  7.71 us
    ppermute x1, waiting for transfers between devices, local(): below = lax.ppermute(hi, 'slab', up_pairs)  4.92 us
    ppermute x1, starting transfers between devices, local(): wabove = lax.ppermute(wave_lo, 'slab', down_pairs)  4.85 us
    all_to_all x1, starting transfers between devices, local(): lax.all_to_all(mixed.reshape(nsta, owned * parts * depth, lanes), 'sta',...  4.64 us
    ppermute x1, waiting for transfers between devices, local(): above = lax.ppermute(lo, 'slab', down_pairs)  4.58 us
  transfers between devices with their start and end apart: 6, of which 5 were waited for; matrix products, arithmetic and copies ran while one was open for 4% of the time, Pallas kernels for 0%

profile of v9, /device:TPU:32, one launch (start us, length us, event | category | flops | bytes accessed | tf_op | source)
XLA Modules:
  0.0 89.3 jit_solution(17102924681847153273)
XLA Ops:
  0.0 1.9 %shard_map.64 = bf16[32,64,128]{2,1,0:T(8,128)(2,1)} custom-call(bf16[2,2,16,4096]{3,2,1,0:T(8,128)(2,1)} %green_ref.1), custom_call_target="tpu_custom_call" | custom-call | tf_op jit(solution)/shard_map/pallas_call | solution.py:231
  1.9 13.3 %all-to-all-start = ((bf16[32,64,128]{2,1,0:T(8,128)(2,1)}), bf16[32,64,128]{2,1,0:T(8,128)(2,1)S(1)}, u32[]{:S(2)}, u32[]{:S(2)}) async-start(bf16[32,64,128]{2,1,0:T(8,128)(2,1)} %shard_map.64), calls=%async_computation | async-start | bytes 1048576 | tf_op jit(solution)/shard_map/all_to_all | solution.py:235
  15.3 0.7 copy-done.8
  16.3 0.4 fusion
  17.1 0.4 fusion.55
  17.5 0.9 %convolution_convert_fusion.big_ref = bf16[128,128]{1,0:T(8,128)(2,1)} fusion(bf16[64,64]{1,0:T(8,128)(2,1)S(1)} %fusion, bf16[64,64]{1,0:T(8,128)(2,1)S(1)} %get-tuple-element.28, bf16[64,64]{1,0:T(8,128)(2,1)S(1)} %get-tuple-element.27, s32[128]{0:T(128)S(1)} %get-tuple-element.30, s32[128]{0:T(128)S(1)} %get-tuple-element.29), kind=kOutput, calls=%fused_computation | convolution fusion | flops 8585216 | bytes 58368 | tf_op jit(solution)/shard_map/dot_general | solution.py:246
  18.5 14.5 %all-to-all-done = bf16[32,64,128]{2,1,0:T(8,128)(2,1)S(1)} async-done(((bf16[32,64,128]{2,1,0:T(8,128)(2,1)}), bf16[32,64,128]{2,1,0:T(8,128)(2,1)S(1)}, u32[]{:S(2)}, u32[]{:S(2)}) %all-to-all-start) | async-done | bytes 524320 | tf_op jit(solution)/shard_map/all_to_all | solution.py:235
  33.0 0.8 copy-done
  33.8 2.7 %shard_map.65 = bf16[2048,128]{1,0:T(8,128)(2,1)} custom-call(bf16[128,128]{1,0:T(8,128)(2,1)} %convolution_convert_fusion.big_ref, bf16[2048,128]{1,0:T(8,128)(2,1)} %bitcast.7), custom_call_target="tpu_custom_call" | custom-call | flops 67108864 | bytes 1048576 | tf_op jit(solution)/shard_map/pallas_call | solution.py:65
  36.5 4.6 %all-to-all-start.1 = ((bf16[32,64,128]{2,1,0:T(8,128)(2,1)}), bf16[32,64,128]{2,1,0:T(8,128)(2,1)S(1)}, u32[]{:S(2)}, u32[]{:S(2)}) async-start(bf16[32,64,128]{2,1,0:T(8,128)(2,1)} %bitcast.8), calls=%async_computation.1 | async-start | bytes 1048576 | tf_op jit(solution)/shard_map/all_to_all | solution.py:253
  41.1 1.9 %collective-permute-start = (f32[8,4096]{1,0:T(8,128)S(1)}, f32[8,4096]{1,0:T(8,128)S(1)}, u32[]{:S(2)}, u32[]{:S(2)}) collective-permute-start(f32[8,4096]{1,0:T(8,128)S(1)} %get-tuple-element.14), channel_id=1, source_target_pairs={{0,1},{1,2},{2,3},{3,4},{4,5},{5,6},{6,7},{7,8},{8,9},{9,10},{10,1... | collective-permute-start | bytes 393224 | tf_op jit(solution)/shard_map/ppermute | solution.py:250
  43.1 4.9 %collective-permute-start.1 = (f32[8,4096]{1,0:T(8,128)S(1)}, f32[8,4096]{1,0:T(8,128)S(1)}, u32[]{:S(2)}, u32[]{:S(2)}) collective-permute-start(f32[8,4096]{1,0:T(8,128)S(1)} %get-tuple-element.15), channel_id=1, source_target_pairs={{1,0},{2,1},{3,2},{4,3},{5,4},{6,5},{7,6},{8,7},{9,8},{10,9},{11,1... | collective-permute-start | bytes 393224 | tf_op jit(solution)/shard_map/ppermute | solution.py:251
  48.0 0.6 copy-done.9
  48.6 0.7 pad_add_fusion.meta_ref
  49.3 1.2 %collective-permute-done.1.wabove_ref = f32[8,4096]{1,0:T(8,128)S(1)} collective-permute-done((f32[8,4096]{1,0:T(8,128)S(1)}, f32[8,4096]{1,0:T(8,128)S(1)}, u32[]{:S(2)}, u32[]{:S(2)}) %collective-permute-start.1) | collective-permute-done | bytes 131104 | tf_op jit(solution)/shard_map/ppermute | solution.py:251
  50.4 7.7 %all-to-all-done.1.recv_ref = bf16[32,64,128]{2,1,0:T(8,128)(2,1)S(1)} async-done(((bf16[32,64,128]{2,1,0:T(8,128)(2,1)}), bf16[32,64,128]{2,1,0:T(8,128)(2,1)S(1)}, u32[]{:S(2)}, u32[]{:S(2)}) %all-to-all-start.1) | async-done | bytes 524320 | tf_op jit(solution)/shard_map/all_to_all | solution.py:253
  58.1 0.8 copy-done.1
  58.9 2.3 %shard_map.66 = (f32[2,2,8,4096]{3,2,1,0:T(8,128)}, f32[2,2,8,4096]{3,2,1,0:T(8,128)}) custom-call(s32[4]{0:T(128)} %pad_add_fusion.meta_ref, bf16[32,64,128]{2,1,0:T(8,128)(2,1)} %copy-done.1, f32[16,4096]{1,0:T(8,128)} %noise_ref.1), custom_call_target="tpu_custom_call" | custom-call | tf_op jit(solution)/shard_map/pallas_call | solution.py:260
  61.2 1.9 %collective-permute-start.3 = (f32[2,2,8,4096]{3,2,1,0:T(8,128)}, f32[2,2,8,4096]{3,2,1,0:T(8,128)S(1)}, u32[]{:S(2)}, u32[]{:S(2)}) collective-permute-start(f32[2,2,8,4096]{3,2,1,0:T(8,128)} %get-tuple-element.17.lo_ref), channel_id=1, source_target_pairs={{1,0},{2,1},{3,2},{4,3},{5,4},{6,5},{7,6},{8,7},{9,8},{10,9},{11,1... | collective-permute-start | bytes 1572872 | tf_op jit(solution)/shard_map/ppermute | solution.py:270
  63.1 2.4 %collective-permute-start.2 = (f32[2,2,8,4096]{3,2,1,0:T(8,128)}, f32[2,2,8,4096]{3,2,1,0:T(8,128)S(1)}, u32[]{:S(2)}, u32[]{:S(2)}) collective-permute-start(f32[2,2,8,4096]{3,2,1,0:T(8,128)} %get-tuple-element.18.hi_ref), channel_id=1, source_target_pairs={{0,1},{1,2},{2,3},{3,4},{4,5},{5,6},{6,7},{7,8},{8,9},{9,10},{10,1... | collective-permute-start | bytes 1572872 | tf_op jit(solution)/shard_map/ppermute | solution.py:269
  65.5 4.6 %collective-permute-done.3.above_ref = f32[2,2,8,4096]{3,2,1,0:T(8,128)S(1)} collective-permute-done((f32[2,2,8,4096]{3,2,1,0:T(8,128)}, f32[2,2,8,4096]{3,2,1,0:T(8,128)S(1)}, u32[]{:S(2)}, u32[]{:S(2)}) %collective-permute-start.3) | collective-permute-done | bytes 524320 | tf_op jit(solution)/shard_map/ppermute | solution.py:270
  70.1 4.9 %collective-permute-done.2.below_ref = f32[2,2,8,4096]{3,2,1,0:T(8,128)S(1)} collective-permute-done((f32[2,2,8,4096]{3,2,1,0:T(8,128)}, f32[2,2,8,4096]{3,2,1,0:T(8,128)S(1)}, u32[]{:S(2)}, u32[]{:S(2)}) %collective-permute-start.2) | collective-permute-done | bytes 524320 | tf_op jit(solution)/shard_map/ppermute | solution.py:269
  75.0 0.8 copy-done.4
  75.8 13.5 %shard_map.67 = f32[2,2,16,4096]{3,2,1,0:T(8,128)} custom-call(s32[4]{0:T(128)} %pad_add_fusion.meta_ref, f32[2,2,8,4096]{3,2,1,0:T(8,128)} %get-tuple-element.17.lo_ref, f32[2,2,8,4096]{3,2,1,0:T(8,128)} %get-tuple-element.18.hi_ref, f32[2,2,8,4096]{3,2,1,0:T(8,128)} %copy-done.4, f32[2,2,8,4096]{3,2,1,0:T(8,128)} %copy-done.3, f32[16,4096]{1,0:T(8,128)} %wave_ref.1, ...), custom_call_target="tpu_custom_call" | custom-call | flops 94371840 | bytes 3145728 | tf_op jit(solution)/shard_map/pallas_call | solution.py:208
  (22 shorter events, 0.8 us)
Async XLA Ops:
  1.9 13.3 %copy-start.7 = (s32[256,2]{0,1:T(2,128)S(1)}, s32[256,2]{0,1:T(2,128)}, u32[]{:S(2)}) copy-start(s32[256,2]{0,1:T(2,128)} %param.7) | copy-start | bytes 6148
  1.9 31.1 %all-to-all-start = ((bf16[32,64,128]{2,1,0:T(8,128)(2,1)}), bf16[32,64,128]{2,1,0:T(8,128)(2,1)S(1)}, u32[]{:S(2)}, u32[]{:S(2)}) async-start(bf16[32,64,128]{2,1,0:T(8,128)(2,1)} %shard_map.64), calls=%async_computation | async-start | bytes 1048576 | tf_op jit(solution)/shard_map/all_to_all | solution.py:235
  15.3 0.7 copy-start.8
  16.7 1.7 %copy-start.2 = (f32[16,4096]{1,0:T(8,128)S(1)}, f32[16,4096]{1,0:T(8,128)}, u32[]{:S(2)}) copy-start(f32[16,4096]{1,0:T(8,128)} %wave_ref.1) | copy-start | bytes 786436
  33.0 0.8 copy-start
  36.5 21.6 %all-to-all-start.1 = ((bf16[32,64,128]{2,1,0:T(8,128)(2,1)}), bf16[32,64,128]{2,1,0:T(8,128)(2,1)S(1)}, u32[]{:S(2)}, u32[]{:S(2)}) async-start(bf16[32,64,128]{2,1,0:T(8,128)(2,1)} %bitcast.8), calls=%async_computation.1 | async-start | bytes 1048576 | tf_op jit(solution)/shard_map/all_to_all | solution.py:253
  41.1 8.1 %collective-permute-start = (f32[8,4096]{1,0:T(8,128)S(1)}, f32[8,4096]{1,0:T(8,128)S(1)}, u32[]{:S(2)}, u32[]{:S(2)}) collective-permute-start(f32[8,4096]{1,0:T(8,128)S(1)} %get-tuple-element.14), channel_id=1, source_target_pairs={{0,1},{1,2},{2,3},{3,4},{4,5},{5,6},{6,7},{7,8},{8,9},{9,10},{10,1... | collective-permute-start | bytes 393224 | tf_op jit(solution)/shard_map/ppermute | solution.py:250
  43.1 7.4 %collective-permute-start.1 = (f32[8,4096]{1,0:T(8,128)S(1)}, f32[8,4096]{1,0:T(8,128)S(1)}, u32[]{:S(2)}, u32[]{:S(2)}) collective-permute-start(f32[8,4096]{1,0:T(8,128)S(1)} %get-tuple-element.15), channel_id=1, source_target_pairs={{1,0},{2,1},{3,2},{4,3},{5,4},{6,5},{7,6},{8,7},{9,8},{10,9},{11,1... | collective-permute-start | bytes 393224 | tf_op jit(solution)/shard_map/ppermute | solution.py:251
  47.9 0.7 copy-start.9
  49.3 11.9 %copy-start.5 = (f32[8,4096]{1,0:T(8,128)}, f32[8,4096]{1,0:T(8,128)S(1)}, u32[]{:S(2)}) copy-start(f32[8,4096]{1,0:T(8,128)S(1)} %collective-permute-done.wbelow_ref) | copy-start | bytes 393220
  50.4 10.8 %copy-start.6 = (f32[8,4096]{1,0:T(8,128)}, f32[8,4096]{1,0:T(8,128)S(1)}, u32[]{:S(2)}) copy-start(f32[8,4096]{1,0:T(8,128)S(1)} %collective-permute-done.1.wabove_ref) | copy-start | bytes 393220
  58.1 0.8 copy-start.1
  61.2 8.9 %collective-permute-start.3 = (f32[2,2,8,4096]{3,2,1,0:T(8,128)}, f32[2,2,8,4096]{3,2,1,0:T(8,128)S(1)}, u32[]{:S(2)}, u32[]{:S(2)}) collective-permute-start(f32[2,2,8,4096]{3,2,1,0:T(8,128)} %get-tuple-element.17.lo_ref), channel_id=1, source_target_pairs={{1,0},{2,1},{3,2},{4,3},{5,4},{6,5},{7,6},{8,7},{9,8},{10,9},{11,1... | collective-permute-start | bytes 1572872 | tf_op jit(solution)/shard_map/ppermute | solution.py:270
  63.1 11.9 %collective-permute-start.2 = (f32[2,2,8,4096]{3,2,1,0:T(8,128)}, f32[2,2,8,4096]{3,2,1,0:T(8,128)S(1)}, u32[]{:S(2)}, u32[]{:S(2)}) collective-permute-start(f32[2,2,8,4096]{3,2,1,0:T(8,128)} %get-tuple-element.18.hi_ref), channel_id=1, source_target_pairs={{0,1},{1,2},{2,3},{3,4},{4,5},{5,6},{6,7},{7,8},{8,9},{9,10},{10,1... | collective-permute-start | bytes 1572872 | tf_op jit(solution)/shard_map/ppermute | solution.py:269
  70.1 4.9 %copy-start.3 = (f32[2,2,8,4096]{3,2,1,0:T(8,128)}, f32[2,2,8,4096]{3,2,1,0:T(8,128)S(1)}, u32[]{:S(2)}) copy-start(f32[2,2,8,4096]{3,2,1,0:T(8,128)S(1)} %collective-permute-done.3.above_ref) | copy-start | bytes 1572868
  75.0 0.8 copy-start.4

commit v10 on v9

--- a/solution.py
+++ b/solution.py
@@ -143,7 +143,7 @@
         aim_ref[:, out] = sr * src_im + si * src_re
         return carry
 
-    lax.fori_loop(0, chunks, first, 0)
+    lax.fori_loop(0, chunks, first, 0, unroll=True)
 
     keep = 1.0 - relaxation
     lane = lax.broadcasted_iota(jnp.int32, (rows, width), 1)

time: 89.8 us -> 88.8 us (0.989)
  Pallas kernels: 20.4 us -> 19.4 us
    pallas_call x1, Pallas kernels: 13.5 us -> 12.5 us  [sweeps(): pl.pallas_call(functools.partial(sweep_kernel, depth), out_shape=jax.Shap...]
where the time goes in v10:
time: 88.8 us; the launch traced here: 88.3 us
  waiting for transfers between devices  32.9 us (37%)
  starting transfers between devices  29 us (33%)
  Pallas kernels  19.4 us (22%)
  local copies, waits for them, and re-layouts  3.75 us (4%)
  matrix products  2.48 us (3%)
    all_to_all x1, waiting for transfers between devices, local(): recv = lax.all_to_all(send, 'sta', 0, 0, tiled=True)  14.5 us
    all_to_all x1, starting transfers between devices, local(): recv = lax.all_to_all(send, 'sta', 0, 0, tiled=True)  13.3 us
    pallas_call x1, Pallas kernels, sweeps(): pl.pallas_call(functools.partial(sweep_kernel, depth), out_shape=jax.Shap...  12.5 us
    all_to_all x1, waiting for transfers between devices, local(): lax.all_to_all(mixed.reshape(nsta, owned * parts * depth, lanes), 'sta',...  7.71 us
    ppermute x1, waiting for transfers between devices, local(): below = lax.ppermute(hi, 'slab', up_pairs)  4.92 us
    ppermute x1, starting transfers between devices, local(): wabove = lax.ppermute(wave_lo, 'slab', down_pairs)  4.85 us
    all_to_all x1, starting transfers between devices, local(): lax.all_to_all(mixed.reshape(nsta, owned * parts * depth, lanes), 'sta',...  4.64 us
    ppermute x1, waiting for transfers between devices, local(): above = lax.ppermute(lo, 'slab', down_pairs)  4.58 us
  transfers between devices with their start and end apart: 6, of which 5 were waited for; matrix products, arithmetic and copies ran while one was open for 4% of the time, Pallas kernels for 0%

profile of v10, /device:TPU:32, one launch (start us, length us, event | category | flops | bytes accessed | tf_op | source)
XLA Modules:
  0.0 88.3 jit_solution(1735995388088844859)
XLA Ops:
  0.0 1.9 %shard_map.64 = bf16[32,64,128]{2,1,0:T(8,128)(2,1)} custom-call(bf16[2,2,16,4096]{3,2,1,0:T(8,128)(2,1)} %green_ref.1), custom_call_target="tpu_custom_call" | custom-call | tf_op jit(solution)/shard_map/pallas_call | solution.py:231
  1.9 13.3 %all-to-all-start = ((bf16[32,64,128]{2,1,0:T(8,128)(2,1)}), bf16[32,64,128]{2,1,0:T(8,128)(2,1)S(1)}, u32[]{:S(2)}, u32[]{:S(2)}) async-start(bf16[32,64,128]{2,1,0:T(8,128)(2,1)} %shard_map.64), calls=%async_computation | async-start | bytes 1048576 | tf_op jit(solution)/shard_map/all_to_all | solution.py:235
  15.3 0.7 copy-done.8
  16.3 0.4 fusion
  17.1 0.4 fusion.55
  17.5 0.9 %convolution_convert_fusion.big_ref = bf16[128,128]{1,0:T(8,128)(2,1)} fusion(bf16[64,64]{1,0:T(8,128)(2,1)S(1)} %fusion, bf16[64,64]{1,0:T(8,128)(2,1)S(1)} %get-tuple-element.28, bf16[64,64]{1,0:T(8,128)(2,1)S(1)} %get-tuple-element.27, s32[128]{0:T(128)S(1)} %get-tuple-element.30, s32[128]{0:T(128)S(1)} %get-tuple-element.29), kind=kOutput, calls=%fused_computation | convolution fusion | flops 8585216 | bytes 58368 | tf_op jit(solution)/shard_map/dot_general | solution.py:246
  18.5 14.5 %all-to-all-done = bf16[32,64,128]{2,1,0:T(8,128)(2,1)S(1)} async-done(((bf16[32,64,128]{2,1,0:T(8,128)(2,1)}), bf16[32,64,128]{2,1,0:T(8,128)(2,1)S(1)}, u32[]{:S(2)}, u32[]{:S(2)}) %all-to-all-start) | async-done | bytes 524320 | tf_op jit(solution)/shard_map/all_to_all | solution.py:235
  33.0 0.8 copy-done
  33.8 2.7 %shard_map.65 = bf16[2048,128]{1,0:T(8,128)(2,1)} custom-call(bf16[128,128]{1,0:T(8,128)(2,1)} %convolution_convert_fusion.big_ref, bf16[2048,128]{1,0:T(8,128)(2,1)} %bitcast.7), custom_call_target="tpu_custom_call" | custom-call | flops 67108864 | bytes 1048576 | tf_op jit(solution)/shard_map/pallas_call | solution.py:65
  36.5 4.6 %all-to-all-start.1 = ((bf16[32,64,128]{2,1,0:T(8,128)(2,1)}), bf16[32,64,128]{2,1,0:T(8,128)(2,1)S(1)}, u32[]{:S(2)}, u32[]{:S(2)}) async-start(bf16[32,64,128]{2,1,0:T(8,128)(2,1)} %bitcast.8), calls=%async_computation.1 | async-start | bytes 1048576 | tf_op jit(solution)/shard_map/all_to_all | solution.py:253
  41.1 1.9 %collective-permute-start = (f32[8,4096]{1,0:T(8,128)S(1)}, f32[8,4096]{1,0:T(8,128)S(1)}, u32[]{:S(2)}, u32[]{:S(2)}) collective-permute-start(f32[8,4096]{1,0:T(8,128)S(1)} %get-tuple-element.14), channel_id=1, source_target_pairs={{0,1},{1,2},{2,3},{3,4},{4,5},{5,6},{6,7},{7,8},{8,9},{9,10},{10,1... | collective-permute-start | bytes 393224 | tf_op jit(solution)/shard_map/ppermute | solution.py:250
  43.1 4.9 %collective-permute-start.1 = (f32[8,4096]{1,0:T(8,128)S(1)}, f32[8,4096]{1,0:T(8,128)S(1)}, u32[]{:S(2)}, u32[]{:S(2)}) collective-permute-start(f32[8,4096]{1,0:T(8,128)S(1)} %get-tuple-element.15), channel_id=1, source_target_pairs={{1,0},{2,1},{3,2},{4,3},{5,4},{6,5},{7,6},{8,7},{9,8},{10,9},{11,1... | collective-permute-start | bytes 393224 | tf_op jit(solution)/shard_map/ppermute | solution.py:251
  48.0 0.6 copy-done.9
  48.6 0.7 pad_add_fusion.meta_ref
  49.3 1.2 %collective-permute-done.1.wabove_ref = f32[8,4096]{1,0:T(8,128)S(1)} collective-permute-done((f32[8,4096]{1,0:T(8,128)S(1)}, f32[8,4096]{1,0:T(8,128)S(1)}, u32[]{:S(2)}, u32[]{:S(2)}) %collective-permute-start.1) | collective-permute-done | bytes 131104 | tf_op jit(solution)/shard_map/ppermute | solution.py:251
  50.4 7.7 %all-to-all-done.1.recv_ref = bf16[32,64,128]{2,1,0:T(8,128)(2,1)S(1)} async-done(((bf16[32,64,128]{2,1,0:T(8,128)(2,1)}), bf16[32,64,128]{2,1,0:T(8,128)(2,1)S(1)}, u32[]{:S(2)}, u32[]{:S(2)}) %all-to-all-start.1) | async-done | bytes 524320 | tf_op jit(solution)/shard_map/all_to_all | solution.py:253
  58.1 0.8 copy-done.1
  58.9 2.3 %shard_map.66 = (f32[2,2,8,4096]{3,2,1,0:T(8,128)}, f32[2,2,8,4096]{3,2,1,0:T(8,128)}) custom-call(s32[4]{0:T(128)} %pad_add_fusion.meta_ref, bf16[32,64,128]{2,1,0:T(8,128)(2,1)} %copy-done.1, f32[16,4096]{1,0:T(8,128)} %noise_ref.1), custom_call_target="tpu_custom_call" | custom-call | tf_op jit(solution)/shard_map/pallas_call | solution.py:260
  61.2 1.9 %collective-permute-start.3 = (f32[2,2,8,4096]{3,2,1,0:T(8,128)}, f32[2,2,8,4096]{3,2,1,0:T(8,128)S(1)}, u32[]{:S(2)}, u32[]{:S(2)}) collective-permute-start(f32[2,2,8,4096]{3,2,1,0:T(8,128)} %get-tuple-element.17.lo_ref), channel_id=1, source_target_pairs={{1,0},{2,1},{3,2},{4,3},{5,4},{6,5},{7,6},{8,7},{9,8},{10,9},{11,1... | collective-permute-start | bytes 1572872 | tf_op jit(solution)/shard_map/ppermute | solution.py:270
  63.1 2.4 %collective-permute-start.2 = (f32[2,2,8,4096]{3,2,1,0:T(8,128)}, f32[2,2,8,4096]{3,2,1,0:T(8,128)S(1)}, u32[]{:S(2)}, u32[]{:S(2)}) collective-permute-start(f32[2,2,8,4096]{3,2,1,0:T(8,128)} %get-tuple-element.18.hi_ref), channel_id=1, source_target_pairs={{0,1},{1,2},{2,3},{3,4},{4,5},{5,6},{6,7},{7,8},{8,9},{9,10},{10,1... | collective-permute-start | bytes 1572872 | tf_op jit(solution)/shard_map/ppermute | solution.py:269
  65.5 4.6 %collective-permute-done.3.above_ref = f32[2,2,8,4096]{3,2,1,0:T(8,128)S(1)} collective-permute-done((f32[2,2,8,4096]{3,2,1,0:T(8,128)}, f32[2,2,8,4096]{3,2,1,0:T(8,128)S(1)}, u32[]{:S(2)}, u32[]{:S(2)}) %collective-permute-start.3) | collective-permute-done | bytes 524320 | tf_op jit(solution)/shard_map/ppermute | solution.py:270
  70.1 4.9 %collective-permute-done.2.below_ref = f32[2,2,8,4096]{3,2,1,0:T(8,128)S(1)} collective-permute-done((f32[2,2,8,4096]{3,2,1,0:T(8,128)}, f32[2,2,8,4096]{3,2,1,0:T(8,128)S(1)}, u32[]{:S(2)}, u32[]{:S(2)}) %collective-permute-start.2) | collective-permute-done | bytes 524320 | tf_op jit(solution)/shard_map/ppermute | solution.py:269
  75.0 0.8 copy-done.4
  75.8 12.5 %shard_map.67 = f32[2,2,16,4096]{3,2,1,0:T(8,128)} custom-call(s32[4]{0:T(128)} %pad_add_fusion.meta_ref, f32[2,2,8,4096]{3,2,1,0:T(8,128)} %get-tuple-element.17.lo_ref, f32[2,2,8,4096]{3,2,1,0:T(8,128)} %get-tuple-element.18.hi_ref, f32[2,2,8,4096]{3,2,1,0:T(8,128)} %copy-done.4, f32[2,2,8,4096]{3,2,1,0:T(8,128)} %copy-done.3, f32[16,4096]{1,0:T(8,128)} %wave_ref.1, ...), custom_call_target="tpu_custom_call" | custom-call | flops 94371840 | bytes 3145728 | tf_op jit(solution)/shard_map/pallas_call | solution.py:208
  (22 shorter events, 0.8 us)
Async XLA Ops:
  1.9 13.3 %copy-start.7 = (s32[256,2]{0,1:T(2,128)S(1)}, s32[256,2]{0,1:T(2,128)}, u32[]{:S(2)}) copy-start(s32[256,2]{0,1:T(2,128)} %param.7) | copy-start | bytes 6148
  1.9 31.1 %all-to-all-start = ((bf16[32,64,128]{2,1,0:T(8,128)(2,1)}), bf16[32,64,128]{2,1,0:T(8,128)(2,1)S(1)}, u32[]{:S(2)}, u32[]{:S(2)}) async-start(bf16[32,64,128]{2,1,0:T(8,128)(2,1)} %shard_map.64), calls=%async_computation | async-start | bytes 1048576 | tf_op jit(solution)/shard_map/all_to_all | solution.py:235
  15.3 0.7 copy-start.8
  16.7 1.7 %copy-start.2 = (f32[16,4096]{1,0:T(8,128)S(1)}, f32[16,4096]{1,0:T(8,128)}, u32[]{:S(2)}) copy-start(f32[16,4096]{1,0:T(8,128)} %wave_ref.1) | copy-start | bytes 786436
  33.0 0.8 copy-start
  36.5 21.6 %all-to-all-start.1 = ((bf16[32,64,128]{2,1,0:T(8,128)(2,1)}), bf16[32,64,128]{2,1,0:T(8,128)(2,1)S(1)}, u32[]{:S(2)}, u32[]{:S(2)}) async-start(bf16[32,64,128]{2,1,0:T(8,128)(2,1)} %bitcast.8), calls=%async_computation.1 | async-start | bytes 1048576 | tf_op jit(solution)/shard_map/all_to_all | solution.py:253
  41.1 8.1 %collective-permute-start = (f32[8,4096]{1,0:T(8,128)S(1)}, f32[8,4096]{1,0:T(8,128)S(1)}, u32[]{:S(2)}, u32[]{:S(2)}) collective-permute-start(f32[8,4096]{1,0:T(8,128)S(1)} %get-tuple-element.14), channel_id=1, source_target_pairs={{0,1},{1,2},{2,3},{3,4},{4,5},{5,6},{6,7},{7,8},{8,9},{9,10},{10,1... | collective-permute-start | bytes 393224 | tf_op jit(solution)/shard_map/ppermute | solution.py:250
  43.1 7.4 %collective-permute-start.1 = (f32[8,4096]{1,0:T(8,128)S(1)}, f32[8,4096]{1,0:T(8,128)S(1)}, u32[]{:S(2)}, u32[]{:S(2)}) collective-permute-start(f32[8,4096]{1,0:T(8,128)S(1)} %get-tuple-element.15), channel_id=1, source_target_pairs={{1,0},{2,1},{3,2},{4,3},{5,4},{6,5},{7,6},{8,7},{9,8},{10,9},{11,1... | collective-permute-start | bytes 393224 | tf_op jit(solution)/shard_map/ppermute | solution.py:251
  47.9 0.7 copy-start.9
  49.3 11.9 %copy-start.5 = (f32[8,4096]{1,0:T(8,128)}, f32[8,4096]{1,0:T(8,128)S(1)}, u32[]{:S(2)}) copy-start(f32[8,4096]{1,0:T(8,128)S(1)} %collective-permute-done.wbelow_ref) | copy-start | bytes 393220
  50.4 10.8 %copy-start.6 = (f32[8,4096]{1,0:T(8,128)}, f32[8,4096]{1,0:T(8,128)S(1)}, u32[]{:S(2)}) copy-start(f32[8,4096]{1,0:T(8,128)S(1)} %collective-permute-done.1.wabove_ref) | copy-start | bytes 393220
  58.1 0.8 copy-start.1
  61.2 8.9 %collective-permute-start.3 = (f32[2,2,8,4096]{3,2,1,0:T(8,128)}, f32[2,2,8,4096]{3,2,1,0:T(8,128)S(1)}, u32[]{:S(2)}, u32[]{:S(2)}) collective-permute-start(f32[2,2,8,4096]{3,2,1,0:T(8,128)} %get-tuple-element.17.lo_ref), channel_id=1, source_target_pairs={{1,0},{2,1},{3,2},{4,3},{5,4},{6,5},{7,6},{8,7},{9,8},{10,9},{11,1... | collective-permute-start | bytes 1572872 | tf_op jit(solution)/shard_map/ppermute | solution.py:270
  63.1 11.9 %collective-permute-start.2 = (f32[2,2,8,4096]{3,2,1,0:T(8,128)}, f32[2,2,8,4096]{3,2,1,0:T(8,128)S(1)}, u32[]{:S(2)}, u32[]{:S(2)}) collective-permute-start(f32[2,2,8,4096]{3,2,1,0:T(8,128)} %get-tuple-element.18.hi_ref), channel_id=1, source_target_pairs={{0,1},{1,2},{2,3},{3,4},{4,5},{5,6},{6,7},{7,8},{8,9},{9,10},{10,1... | collective-permute-start | bytes 1572872 | tf_op jit(solution)/shard_map/ppermute | solution.py:269
  70.1 4.9 %copy-start.3 = (f32[2,2,8,4096]{3,2,1,0:T(8,128)}, f32[2,2,8,4096]{3,2,1,0:T(8,128)S(1)}, u32[]{:S(2)}) copy-start(f32[2,2,8,4096]{3,2,1,0:T(8,128)S(1)} %collective-permute-done.3.above_ref) | copy-start | bytes 1572868
  75.0 0.8 copy-start.4

commit v11 on v10

--- a/solution.py
+++ b/solution.py
@@ -10,6 +10,7 @@
 GY = 64
 SWEEPS = 6
 HALO = 8
+REACH = SWEEPS - 1
 LANES = 512
 PAD = 128
 
@@ -77,7 +78,7 @@
     )(big, recv)
 
 
-def source_kernel(owned, depth, meta_ref, recv_ref, noise_ref, lo_ref, hi_ref):
+def source_kernel(owned, depth, meta_ref, recv_ref, noise_ref, lo_ref, hi_ref, dn_ref, up_ref):
     pieces, _, lanes = recv_ref.shape
     half = depth // 2
     slab = meta_ref[0]
@@ -97,6 +98,9 @@
                     value = value + jnp.where(hit, point_size, 0.0)
                 lo_ref[b, part, :, cols] = value[:half]
                 hi_ref[b, part, :, cols] = value[half:]
+                at = (b * 2 + part) * REACH
+                dn_ref[at : at + REACH, cols] = value[:REACH]
+                up_ref[at : at + REACH, cols] = value[depth - REACH :]
 
 
 def sweep_kernel(depth, meta_ref, lo_ref, hi_ref, below_ref, above_ref, wave_ref, wbelow_ref,
@@ -111,11 +115,22 @@
     w_ref[0:HALO] = wbelow_ref[...]
     w_ref[HALO : HALO + depth] = wave_ref[...]
     w_ref[HALO + depth :] = wabove_ref[...]
+    spare = jnp.zeros((HALO - REACH, cells), jnp.float32)
     for part, dst in ((0, sre_ref), (1, sim_ref)):
-        dst[0:HALO] = below_ref[0, part]
+        dst[0 : HALO - REACH] = spare
         dst[HALO : HALO + half] = lo_ref[0, part]
         dst[HALO + half : HALO + depth] = hi_ref[0, part]
-        dst[HALO + depth :] = above_ref[0, part]
+        dst[HALO + depth + REACH :] = spare
+    owned = below_ref.shape[0] // (2 * REACH)
+    for bb in range(owned):
+
+        @pl.when(pl.program_id(0) == bb)
+        def _():
+            for part, dst in ((0, sre_ref), (1, sim_ref)):
+                at = (bb * 2 + part) * REACH
+                dst[HALO - REACH : HALO] = below_ref[at : at + REACH]
+                dst[HALO + depth : HALO + depth + REACH] = above_ref[at : at + REACH]
+
     zeros = jnp.zeros((rows, PAD), jnp.float32)
     for ref in (are_ref, aim_ref, bre_ref, bim_ref):
         ref[:, 0:PAD] = zeros
@@ -194,7 +209,7 @@
     depth = 2 * half
     rows = depth + 2 * HALO
     piece = pl.BlockSpec((1, 2, half, cells), lambda b, *_: (b, 0, 0, 0))
-    halo = pl.BlockSpec((1, 2, HALO, cells), lambda b, *_: (b, 0, 0, 0))
+    halo = pl.BlockSpec((owned * 2 * REACH, cells), lambda b, *_: (0, 0))
     whole = lambda shape: pl.BlockSpec(shape, lambda b, *_: (0,) * len(shape))
     grid_spec = pltpu.PrefetchScalarGridSpec(
         num_scalar_prefetch=1,
@@ -257,17 +272,18 @@
     meta = jnp.concatenate(
         [jnp.stack([slab, jnp.int32(nslab)]).astype(jnp.int32), station_cell.astype(jnp.int32)]
     )
-    lo, hi = pl.pallas_call(
+    lo, hi, edge_dn, edge_up = pl.pallas_call(
         functools.partial(source_kernel, owned, depth),
-        out_shape=[jax.ShapeDtypeStruct((owned, 2, half, cells), jnp.float32)] * 2,
+        out_shape=[jax.ShapeDtypeStruct((owned, 2, half, cells), jnp.float32)] * 2
+        + [jax.ShapeDtypeStruct((owned * 2 * REACH, cells), jnp.float32)] * 2,
         in_specs=[
             pl.BlockSpec(memory_space=pltpu.SMEM),
             pl.BlockSpec(memory_space=pltpu.VMEM),
             pl.BlockSpec(memory_space=pltpu.VMEM),
         ],
     )(meta, back, noise_map)
-    below = lax.ppermute(hi, "slab", up_pairs)
-    above = lax.ppermute(lo, "slab", down_pairs)
+    below = lax.ppermute(edge_up, "slab", up_pairs)
+    above = lax.ppermute(edge_dn, "slab", down_pairs)
     return sweeps(meta, lo, hi, below, above, wave_square, wbelow, wabove)
 
 

time: 88.8 us -> 90.9 us (1.024)
  the two profiles are of different devices: /device:TPU:32 before, /device:TPU:25 now
where the time goes in v11:
time: 90.9 us; the launch traced here: 90.4 us
  starting transfers between devices  36.1 us (40%)
  waiting for transfers between devices  27.5 us (30%)
  Pallas kernels  19.9 us (22%)
  local copies, waits for them, and re-layouts  3.69 us (4%)
  matrix products  2.48 us (3%)
    all_to_all x1, waiting for transfers between devices, local(): recv = lax.all_to_all(send, 'sta', 0, 0, tiled=True)  13 us
    all_to_all x1, starting transfers between devices, local(): recv = lax.all_to_all(send, 'sta', 0, 0, tiled=True)  13 us
    pallas_call x1, Pallas kernels, sweeps(): pl.pallas_call(functools.partial(sweep_kernel, depth), out_shape=jax.Shap...  12.8 us
    ppermute x1, starting transfers between devices, local(): below = lax.ppermute(edge_up, 'slab', up_pairs)  7.87 us
    ppermute x1, starting transfers between devices, local(): wbelow = lax.ppermute(wave_hi, 'slab', up_pairs)  6.11 us
    ppermute x1, waiting for transfers between devices, local(): above = lax.ppermute(edge_dn, 'slab', down_pairs)  5.5 us
    all_to_all x1, starting transfers between devices, local(): lax.all_to_all(mixed.reshape(nsta, owned * parts * depth, lanes), 'sta',...  5.25 us
    ppermute x1, waiting for transfers between devices, local(): wabove = lax.ppermute(wave_lo, 'slab', down_pairs)  4.56 us
  transfers between devices with their start and end apart: 6, of which 5 were waited for; matrix products, arithmetic and copies ran while one was open for 3% of the time, Pallas kernels for 0%

profile of v11, /device:TPU:25, one launch (start us, length us, event | category | flops | bytes accessed | tf_op | source)
XLA Modules:
  0.0 90.4 jit_solution(17860613124528725940)
XLA Ops:
  0.0 1.9 %shard_map.64 = bf16[32,64,128]{2,1,0:T(8,128)(2,1)} custom-call(bf16[2,2,16,4096]{3,2,1,0:T(8,128)(2,1)} %green_ref.1), custom_call_target="tpu_custom_call" | custom-call | tf_op jit(solution)/shard_map/pallas_call | solution.py:246
  1.9 13.0 %all-to-all-start = ((bf16[32,64,128]{2,1,0:T(8,128)(2,1)}), bf16[32,64,128]{2,1,0:T(8,128)(2,1)S(1)}, u32[]{:S(2)}, u32[]{:S(2)}) async-start(bf16[32,64,128]{2,1,0:T(8,128)(2,1)} %shard_map.64), calls=%async_computation | async-start | bytes 1048576 | tf_op jit(solution)/shard_map/all_to_all | solution.py:250
  15.0 0.7 copy-done.8
  16.1 0.4 fusion
  16.9 0.4 fusion.55
  17.2 0.9 %convolution_convert_fusion.big_ref = bf16[128,128]{1,0:T(8,128)(2,1)} fusion(bf16[64,64]{1,0:T(8,128)(2,1)S(1)} %fusion, bf16[64,64]{1,0:T(8,128)(2,1)S(1)} %get-tuple-element.32, bf16[64,64]{1,0:T(8,128)(2,1)S(1)} %get-tuple-element.31, s32[128]{0:T(128)S(1)} %get-tuple-element.34, s32[128]{0:T(128)S(1)} %get-tuple-element.33), kind=kOutput, calls=%fused_computation | convolution fusion | flops 8585216 | bytes 58368 | tf_op jit(solution)/shard_map/dot_general | solution.py:261
  18.2 13.0 %all-to-all-done = bf16[32,64,128]{2,1,0:T(8,128)(2,1)S(1)} async-done(((bf16[32,64,128]{2,1,0:T(8,128)(2,1)}), bf16[32,64,128]{2,1,0:T(8,128)(2,1)S(1)}, u32[]{:S(2)}, u32[]{:S(2)}) %all-to-all-start) | async-done | bytes 524320 | tf_op jit(solution)/shard_map/all_to_all | solution.py:250
  31.2 0.8 copy-done
  32.0 2.7 %shard_map.65 = bf16[2048,128]{1,0:T(8,128)(2,1)} custom-call(bf16[128,128]{1,0:T(8,128)(2,1)} %convolution_convert_fusion.big_ref, bf16[2048,128]{1,0:T(8,128)(2,1)} %bitcast.7), custom_call_target="tpu_custom_call" | custom-call | flops 67108864 | bytes 1048576 | tf_op jit(solution)/shard_map/pallas_call | solution.py:66
  34.7 5.3 %all-to-all-start.1 = ((bf16[32,64,128]{2,1,0:T(8,128)(2,1)}), bf16[32,64,128]{2,1,0:T(8,128)(2,1)S(1)}, u32[]{:S(2)}, u32[]{:S(2)}) async-start(bf16[32,64,128]{2,1,0:T(8,128)(2,1)} %bitcast.8), calls=%async_computation.1 | async-start | bytes 1048576 | tf_op jit(solution)/shard_map/all_to_all | solution.py:268
  40.0 6.1 %collective-permute-start = (f32[8,4096]{1,0:T(8,128)S(1)}, f32[8,4096]{1,0:T(8,128)S(1)}, u32[]{:S(2)}, u32[]{:S(2)}) collective-permute-start(f32[8,4096]{1,0:T(8,128)S(1)} %get-tuple-element.16), channel_id=1, source_target_pairs={{0,1},{1,2},{2,3},{3,4},{4,5},{5,6},{6,7},{7,8},{8,9},{9,10},{10,1... | collective-permute-start | bytes 393224 | tf_op jit(solution)/shard_map/ppermute | solution.py:265
  46.1 1.9 %collective-permute-start.1 = (f32[8,4096]{1,0:T(8,128)S(1)}, f32[8,4096]{1,0:T(8,128)S(1)}, u32[]{:S(2)}, u32[]{:S(2)}) collective-permute-start(f32[8,4096]{1,0:T(8,128)S(1)} %get-tuple-element.17), channel_id=1, source_target_pairs={{1,0},{2,1},{3,2},{4,3},{5,4},{6,5},{7,6},{8,7},{9,8},{10,9},{11,1... | collective-permute-start | bytes 393224 | tf_op jit(solution)/shard_map/ppermute | solution.py:266
  48.1 0.6 copy-done.9
  48.7 0.6 pad_add_fusion.meta_ref
  49.4 4.6 %collective-permute-done.1.wabove_ref = f32[8,4096]{1,0:T(8,128)S(1)} collective-permute-done((f32[8,4096]{1,0:T(8,128)S(1)}, f32[8,4096]{1,0:T(8,128)S(1)}, u32[]{:S(2)}, u32[]{:S(2)}) %collective-permute-start.1) | collective-permute-done | bytes 131104 | tf_op jit(solution)/shard_map/ppermute | solution.py:266
  53.9 1.3 %all-to-all-done.1.recv_ref = bf16[32,64,128]{2,1,0:T(8,128)(2,1)S(1)} async-done(((bf16[32,64,128]{2,1,0:T(8,128)(2,1)}), bf16[32,64,128]{2,1,0:T(8,128)(2,1)S(1)}, u32[]{:S(2)}, u32[]{:S(2)}) %all-to-all-start.1) | async-done | bytes 524320 | tf_op jit(solution)/shard_map/all_to_all | solution.py:268
  55.3 0.8 copy-done.1
  56.0 2.5 %shard_map.66 = (f32[2,2,8,4096]{3,2,1,0:T(8,128)}, f32[2,2,8,4096]{3,2,1,0:T(8,128)}, f32[20,4096]{1,0:T(8,128)}, f32[20,4096]{1,0:T(8,128)}) custom-call(s32[4]{0:T(128)} %pad_add_fusion.meta_ref, bf16[32,64,128]{2,1,0:T(8,128)(2,1)} %copy-done.1, f32[16,4096]{1,0:T(8,128)} %noise_ref.1), custom_call_target="tpu_custom_call" | custom-call | tf_op jit(solution)/shard_map/pallas_call | solution.py:275
  58.5 7.9 %collective-permute-start.2 = (f32[20,4096]{1,0:T(8,128)}, f32[20,4096]{1,0:T(8,128)S(1)}, u32[]{:S(2)}, u32[]{:S(2)}) collective-permute-start(f32[20,4096]{1,0:T(8,128)} %get-tuple-element.21), channel_id=1, source_target_pairs={{0,1},{1,2},{2,3},{3,4},{4,5},{5,6},{6,7},{7,8},{8,9},{9,10},{10,1... | collective-permute-start | bytes 983048 | tf_op jit(solution)/shard_map/ppermute | solution.py:285
  66.4 1.9 %collective-permute-start.3 = (f32[20,4096]{1,0:T(8,128)}, f32[20,4096]{1,0:T(8,128)S(1)}, u32[]{:S(2)}, u32[]{:S(2)}) collective-permute-start(f32[20,4096]{1,0:T(8,128)} %get-tuple-element.22), channel_id=1, source_target_pairs={{1,0},{2,1},{3,2},{4,3},{5,4},{6,5},{7,6},{8,7},{9,8},{10,9},{11,1... | collective-permute-start | bytes 983048 | tf_op jit(solution)/shard_map/ppermute | solution.py:286
  68.3 3.1 %collective-permute-done.2.below_ref = f32[20,4096]{1,0:T(8,128)S(1)} collective-permute-done((f32[20,4096]{1,0:T(8,128)}, f32[20,4096]{1,0:T(8,128)S(1)}, u32[]{:S(2)}, u32[]{:S(2)}) %collective-permute-start.2) | collective-permute-done | bytes 327712 | tf_op jit(solution)/shard_map/ppermute | solution.py:285
  71.4 5.5 %collective-permute-done.3.above_ref = f32[20,4096]{1,0:T(8,128)S(1)} collective-permute-done((f32[20,4096]{1,0:T(8,128)}, f32[20,4096]{1,0:T(8,128)S(1)}, u32[]{:S(2)}, u32[]{:S(2)}) %collective-permute-start.3) | collective-permute-done | bytes 327712 | tf_op jit(solution)/shard_map/ppermute | solution.py:286
  76.9 0.7 copy-done.4
  77.7 12.8 %shard_map.67 = f32[2,2,16,4096]{3,2,1,0:T(8,128)} custom-call(s32[4]{0:T(128)} %pad_add_fusion.meta_ref, f32[2,2,8,4096]{3,2,1,0:T(8,128)} %get-tuple-element.19.lo_ref, f32[2,2,8,4096]{3,2,1,0:T(8,128)} %get-tuple-element.20.hi_ref, f32[20,4096]{1,0:T(8,128)} %copy-done.3, f32[20,4096]{1,0:T(8,128)} %copy-done.4, f32[16,4096]{1,0:T(8,128)} %wave_ref.1, ...), custom_call_target="tpu_custom_call" | custom-call | flops 94371840 | bytes 3145728 | tf_op jit(solution)/shard_map/pallas_call | solution.py:223
  (22 shorter events, 0.8 us)
Async XLA Ops:
  1.9 13.0 %copy-start.7 = (s32[256,2]{0,1:T(2,128)S(1)}, s32[256,2]{0,1:T(2,128)}, u32[]{:S(2)}) copy-start(s32[256,2]{0,1:T(2,128)} %param.7) | copy-start | bytes 6148
  1.9 29.3 %all-to-all-start = ((bf16[32,64,128]{2,1,0:T(8,128)(2,1)}), bf16[32,64,128]{2,1,0:T(8,128)(2,1)S(1)}, u32[]{:S(2)}, u32[]{:S(2)}) async-start(bf16[32,64,128]{2,1,0:T(8,128)(2,1)} %shard_map.64), calls=%async_computation | async-start | bytes 1048576 | tf_op jit(solution)/shard_map/all_to_all | solution.py:250
  15.0 0.7 copy-start.8
  16.4 1.7 %copy-start.2 = (f32[16,4096]{1,0:T(8,128)S(1)}, f32[16,4096]{1,0:T(8,128)}, u32[]{:S(2)}) copy-start(f32[16,4096]{1,0:T(8,128)} %wave_ref.1) | copy-start | bytes 786436
  31.2 0.8 copy-start
  34.7 20.5 %all-to-all-start.1 = ((bf16[32,64,128]{2,1,0:T(8,128)(2,1)}), bf16[32,64,128]{2,1,0:T(8,128)(2,1)S(1)}, u32[]{:S(2)}, u32[]{:S(2)}) async-start(bf16[32,64,128]{2,1,0:T(8,128)(2,1)} %bitcast.8), calls=%async_computation.1 | async-start | bytes 1048576 | tf_op jit(solution)/shard_map/all_to_all | solution.py:268
  40.0 9.4 %collective-permute-start = (f32[8,4096]{1,0:T(8,128)S(1)}, f32[8,4096]{1,0:T(8,128)S(1)}, u32[]{:S(2)}, u32[]{:S(2)}) collective-permute-start(f32[8,4096]{1,0:T(8,128)S(1)} %get-tuple-element.16), channel_id=1, source_target_pairs={{0,1},{1,2},{2,3},{3,4},{4,5},{5,6},{6,7},{7,8},{8,9},{9,10},{10,1... | collective-permute-start | bytes 393224 | tf_op jit(solution)/shard_map/ppermute | solution.py:265
  46.1 7.8 %collective-permute-start.1 = (f32[8,4096]{1,0:T(8,128)S(1)}, f32[8,4096]{1,0:T(8,128)S(1)}, u32[]{:S(2)}, u32[]{:S(2)}) collective-permute-start(f32[8,4096]{1,0:T(8,128)S(1)} %get-tuple-element.17), channel_id=1, source_target_pairs={{1,0},{2,1},{3,2},{4,3},{5,4},{6,5},{7,6},{8,7},{9,8},{10,9},{11,1... | collective-permute-start | bytes 393224 | tf_op jit(solution)/shard_map/ppermute | solution.py:266
  48.1 0.7 copy-start.9
  49.4 9.2 %copy-start.5 = (f32[8,4096]{1,0:T(8,128)}, f32[8,4096]{1,0:T(8,128)S(1)}, u32[]{:S(2)}) copy-start(f32[8,4096]{1,0:T(8,128)S(1)} %collective-permute-done.wbelow_ref) | copy-start | bytes 393220
  53.9 4.6 %copy-start.6 = (f32[8,4096]{1,0:T(8,128)}, f32[8,4096]{1,0:T(8,128)S(1)}, u32[]{:S(2)}) copy-start(f32[8,4096]{1,0:T(8,128)S(1)} %collective-permute-done.1.wabove_ref) | copy-start | bytes 393220
  55.2 0.8 copy-start.1
  58.5 12.9 %collective-permute-start.2 = (f32[20,4096]{1,0:T(8,128)}, f32[20,4096]{1,0:T(8,128)S(1)}, u32[]{:S(2)}, u32[]{:S(2)}) collective-permute-start(f32[20,4096]{1,0:T(8,128)} %get-tuple-element.21), channel_id=1, source_target_pairs={{0,1},{1,2},{2,3},{3,4},{4,5},{5,6},{6,7},{7,8},{8,9},{9,10},{10,1... | collective-permute-start | bytes 983048 | tf_op jit(solution)/shard_map/ppermute | solution.py:285
  66.4 10.5 %collective-permute-start.3 = (f32[20,4096]{1,0:T(8,128)}, f32[20,4096]{1,0:T(8,128)S(1)}, u32[]{:S(2)}, u32[]{:S(2)}) collective-permute-start(f32[20,4096]{1,0:T(8,128)} %get-tuple-element.22), channel_id=1, source_target_pairs={{1,0},{2,1},{3,2},{4,3},{5,4},{6,5},{7,6},{8,7},{9,8},{10,9},{11,1... | collective-permute-start | bytes 983048 | tf_op jit(solution)/shard_map/ppermute | solution.py:286
  71.4 5.5 %copy-start.3 = (f32[20,4096]{1,0:T(8,128)}, f32[20,4096]{1,0:T(8,128)S(1)}, u32[]{:S(2)}) copy-start(f32[20,4096]{1,0:T(8,128)S(1)} %collective-permute-done.2.below_ref) | copy-start | bytes 983044
  76.9 0.7 copy-start.4

commit v12 on v10

--- a/solution.py
+++ b/solution.py
@@ -48,12 +48,11 @@
                 send_ref[ct, start : start + depth, :] = green_ref[part, b, :, ct * lanes : (ct + 1) * lanes]
 
 
-def mix_kernel(depth, big_ref, recv_ref, out_ref, wide_ref, acc_ref):
-    wide_ref[...] = recv_ref[...].astype(jnp.float32)
+def mix_kernel(depth, big_ref, recv_ref, out_ref, acc_ref):
     big = big_ref[...]
     rows = big.shape[0]
     for r in range(depth):
-        rhs = wide_ref[pl.ds(r, rows, stride=depth), :].astype(jnp.bfloat16)
+        rhs = recv_ref[pl.ds(r, rows, stride=depth), :]
         acc_ref[pl.ds(r, rows, stride=depth), :] = jnp.dot(
             big, rhs, preferred_element_type=jnp.float32
         )
@@ -65,10 +64,7 @@
     return pl.pallas_call(
         functools.partial(mix_kernel, depth),
         out_shape=jax.ShapeDtypeStruct((total, lanes), jnp.bfloat16),
-        scratch_shapes=[
-            pltpu.VMEM((total, lanes), jnp.float32),
-            pltpu.VMEM((total, lanes), jnp.float32),
-        ],
+        scratch_shapes=[pltpu.VMEM((total, lanes), jnp.float32)],
         cost_estimate=pl.CostEstimate(
             flops=2 * big.shape[0] * big.shape[1] * depth * lanes,
             bytes_accessed=4 * total * lanes,

time: 88.8 us -> 88.6 us (level)
  no operation moved by 1% of the time
where the time goes in v12:
time: 88.6 us; the launch traced here: 88.1 us
  waiting for transfers between devices  32.9 us (37%)
  starting transfers between devices  29 us (33%)
  Pallas kernels  19.1 us (22%)
  local copies, waits for them, and re-layouts  3.75 us (4%)
  matrix products  2.48 us (3%)
    all_to_all x1, waiting for transfers between devices, local(): recv = lax.all_to_all(send, 'sta', 0, 0, tiled=True)  14.5 us
    all_to_all x1, starting transfers between devices, local(): recv = lax.all_to_all(send, 'sta', 0, 0, tiled=True)  13.3 us
    pallas_call x1, Pallas kernels, sweeps(): pl.pallas_call(functools.partial(sweep_kernel, depth), out_shape=jax.Shap...  12.5 us
    all_to_all x1, waiting for transfers between devices, local(): lax.all_to_all(mixed.reshape(nsta, owned * parts * depth, lanes), 'sta',...  7.71 us
    ppermute x1, waiting for transfers between devices, local(): below = lax.ppermute(hi, 'slab', up_pairs)  4.92 us
    ppermute x1, starting transfers between devices, local(): wabove = lax.ppermute(wave_lo, 'slab', down_pairs)  4.85 us
    all_to_all x1, starting transfers between devices, local(): lax.all_to_all(mixed.reshape(nsta, owned * parts * depth, lanes), 'sta',...  4.64 us
    ppermute x1, waiting for transfers between devices, local(): above = lax.ppermute(lo, 'slab', down_pairs)  4.58 us
  transfers between devices with their start and end apart: 6, of which 5 were waited for; matrix products, arithmetic and copies ran while one was open for 4% of the time, Pallas kernels for 0%

profile of v12, /device:TPU:32, one launch (start us, length us, event | category | flops | bytes accessed | tf_op | source)
XLA Modules:
  0.0 88.1 jit_solution(2275912795033541966)
XLA Ops:
  0.0 1.9 %shard_map.64 = bf16[32,64,128]{2,1,0:T(8,128)(2,1)} custom-call(bf16[2,2,16,4096]{3,2,1,0:T(8,128)(2,1)} %green_ref.1), custom_call_target="tpu_custom_call" | custom-call | tf_op jit(solution)/shard_map/pallas_call | solution.py:227
  1.9 13.3 %all-to-all-start = ((bf16[32,64,128]{2,1,0:T(8,128)(2,1)}), bf16[32,64,128]{2,1,0:T(8,128)(2,1)S(1)}, u32[]{:S(2)}, u32[]{:S(2)}) async-start(bf16[32,64,128]{2,1,0:T(8,128)(2,1)} %shard_map.64), calls=%async_computation | async-start | bytes 1048576 | tf_op jit(solution)/shard_map/all_to_all | solution.py:231
  15.3 0.7 copy-done.8
  16.3 0.4 fusion
  17.1 0.4 fusion.55
  17.5 0.9 %convolution_convert_fusion.big_ref = bf16[128,128]{1,0:T(8,128)(2,1)} fusion(bf16[64,64]{1,0:T(8,128)(2,1)S(1)} %fusion, bf16[64,64]{1,0:T(8,128)(2,1)S(1)} %get-tuple-element.28, bf16[64,64]{1,0:T(8,128)(2,1)S(1)} %get-tuple-element.27, s32[128]{0:T(128)S(1)} %get-tuple-element.30, s32[128]{0:T(128)S(1)} %get-tuple-element.29), kind=kOutput, calls=%fused_computation | convolution fusion | flops 8585216 | bytes 58368 | tf_op jit(solution)/shard_map/dot_general | solution.py:242
  18.5 14.5 %all-to-all-done = bf16[32,64,128]{2,1,0:T(8,128)(2,1)S(1)} async-done(((bf16[32,64,128]{2,1,0:T(8,128)(2,1)}), bf16[32,64,128]{2,1,0:T(8,128)(2,1)S(1)}, u32[]{:S(2)}, u32[]{:S(2)}) %all-to-all-start) | async-done | bytes 524320 | tf_op jit(solution)/shard_map/all_to_all | solution.py:231
  33.0 0.8 copy-done
  33.8 2.5 %shard_map.65 = bf16[2048,128]{1,0:T(8,128)(2,1)} custom-call(bf16[128,128]{1,0:T(8,128)(2,1)} %convolution_convert_fusion.big_ref, bf16[2048,128]{1,0:T(8,128)(2,1)} %bitcast.7), custom_call_target="tpu_custom_call" | custom-call | flops 67108864 | bytes 1048576 | tf_op jit(solution)/shard_map/pallas_call | solution.py:64
  36.3 4.6 %all-to-all-start.1 = ((bf16[32,64,128]{2,1,0:T(8,128)(2,1)}), bf16[32,64,128]{2,1,0:T(8,128)(2,1)S(1)}, u32[]{:S(2)}, u32[]{:S(2)}) async-start(bf16[32,64,128]{2,1,0:T(8,128)(2,1)} %bitcast.8), calls=%async_computation.1 | async-start | bytes 1048576 | tf_op jit(solution)/shard_map/all_to_all | solution.py:249
  40.9 1.9 %collective-permute-start = (f32[8,4096]{1,0:T(8,128)S(1)}, f32[8,4096]{1,0:T(8,128)S(1)}, u32[]{:S(2)}, u32[]{:S(2)}) collective-permute-start(f32[8,4096]{1,0:T(8,128)S(1)} %get-tuple-element.14), channel_id=1, source_target_pairs={{0,1},{1,2},{2,3},{3,4},{4,5},{5,6},{6,7},{7,8},{8,9},{9,10},{10,1... | collective-permute-start | bytes 393224 | tf_op jit(solution)/shard_map/ppermute | solution.py:246
  42.8 4.9 %collective-permute-start.1 = (f32[8,4096]{1,0:T(8,128)S(1)}, f32[8,4096]{1,0:T(8,128)S(1)}, u32[]{:S(2)}, u32[]{:S(2)}) collective-permute-start(f32[8,4096]{1,0:T(8,128)S(1)} %get-tuple-element.15), channel_id=1, source_target_pairs={{1,0},{2,1},{3,2},{4,3},{5,4},{6,5},{7,6},{8,7},{9,8},{10,9},{11,1... | collective-permute-start | bytes 393224 | tf_op jit(solution)/shard_map/ppermute | solution.py:247
  47.7 0.6 copy-done.9
  48.4 0.7 pad_add_fusion.meta_ref
  49.0 1.2 %collective-permute-done.1.wabove_ref = f32[8,4096]{1,0:T(8,128)S(1)} collective-permute-done((f32[8,4096]{1,0:T(8,128)S(1)}, f32[8,4096]{1,0:T(8,128)S(1)}, u32[]{:S(2)}, u32[]{:S(2)}) %collective-permute-start.1) | collective-permute-done | bytes 131104 | tf_op jit(solution)/shard_map/ppermute | solution.py:247
  50.2 7.7 %all-to-all-done.1.recv_ref = bf16[32,64,128]{2,1,0:T(8,128)(2,1)S(1)} async-done(((bf16[32,64,128]{2,1,0:T(8,128)(2,1)}), bf16[32,64,128]{2,1,0:T(8,128)(2,1)S(1)}, u32[]{:S(2)}, u32[]{:S(2)}) %all-to-all-start.1) | async-done | bytes 524320 | tf_op jit(solution)/shard_map/all_to_all | solution.py:249
  57.9 0.8 copy-done.1
  58.7 2.3 %shard_map.66 = (f32[2,2,8,4096]{3,2,1,0:T(8,128)}, f32[2,2,8,4096]{3,2,1,0:T(8,128)}) custom-call(s32[4]{0:T(128)} %pad_add_fusion.meta_ref, bf16[32,64,128]{2,1,0:T(8,128)(2,1)} %copy-done.1, f32[16,4096]{1,0:T(8,128)} %noise_ref.1), custom_call_target="tpu_custom_call" | custom-call | tf_op jit(solution)/shard_map/pallas_call | solution.py:256
  61.0 1.9 %collective-permute-start.3 = (f32[2,2,8,4096]{3,2,1,0:T(8,128)}, f32[2,2,8,4096]{3,2,1,0:T(8,128)S(1)}, u32[]{:S(2)}, u32[]{:S(2)}) collective-permute-start(f32[2,2,8,4096]{3,2,1,0:T(8,128)} %get-tuple-element.17.lo_ref), channel_id=1, source_target_pairs={{1,0},{2,1},{3,2},{4,3},{5,4},{6,5},{7,6},{8,7},{9,8},{10,9},{11,1... | collective-permute-start | bytes 1572872 | tf_op jit(solution)/shard_map/ppermute | solution.py:266
  62.9 2.4 %collective-permute-start.2 = (f32[2,2,8,4096]{3,2,1,0:T(8,128)}, f32[2,2,8,4096]{3,2,1,0:T(8,128)S(1)}, u32[]{:S(2)}, u32[]{:S(2)}) collective-permute-start(f32[2,2,8,4096]{3,2,1,0:T(8,128)} %get-tuple-element.18.hi_ref), channel_id=1, source_target_pairs={{0,1},{1,2},{2,3},{3,4},{4,5},{5,6},{6,7},{7,8},{8,9},{9,10},{10,1... | collective-permute-start | bytes 1572872 | tf_op jit(solution)/shard_map/ppermute | solution.py:265
  65.3 4.6 %collective-permute-done.3.above_ref = f32[2,2,8,4096]{3,2,1,0:T(8,128)S(1)} collective-permute-done((f32[2,2,8,4096]{3,2,1,0:T(8,128)}, f32[2,2,8,4096]{3,2,1,0:T(8,128)S(1)}, u32[]{:S(2)}, u32[]{:S(2)}) %collective-permute-start.3) | collective-permute-done | bytes 524320 | tf_op jit(solution)/shard_map/ppermute | solution.py:266
  69.9 4.9 %collective-permute-done.2.below_ref = f32[2,2,8,4096]{3,2,1,0:T(8,128)S(1)} collective-permute-done((f32[2,2,8,4096]{3,2,1,0:T(8,128)}, f32[2,2,8,4096]{3,2,1,0:T(8,128)S(1)}, u32[]{:S(2)}, u32[]{:S(2)}) %collective-permute-start.2) | collective-permute-done | bytes 524320 | tf_op jit(solution)/shard_map/ppermute | solution.py:265
  74.8 0.8 copy-done.4
  75.6 12.5 %shard_map.67 = f32[2,2,16,4096]{3,2,1,0:T(8,128)} custom-call(s32[4]{0:T(128)} %pad_add_fusion.meta_ref, f32[2,2,8,4096]{3,2,1,0:T(8,128)} %get-tuple-element.17.lo_ref, f32[2,2,8,4096]{3,2,1,0:T(8,128)} %get-tuple-element.18.hi_ref, f32[2,2,8,4096]{3,2,1,0:T(8,128)} %copy-done.4, f32[2,2,8,4096]{3,2,1,0:T(8,128)} %copy-done.3, f32[16,4096]{1,0:T(8,128)} %wave_ref.1, ...), custom_call_target="tpu_custom_call" | custom-call | flops 94371840 | bytes 3145728 | tf_op jit(solution)/shard_map/pallas_call | solution.py:204
  (22 shorter events, 0.8 us)
Async XLA Ops:
  1.9 13.3 %copy-start.7 = (s32[256,2]{0,1:T(2,128)S(1)}, s32[256,2]{0,1:T(2,128)}, u32[]{:S(2)}) copy-start(s32[256,2]{0,1:T(2,128)} %param.7) | copy-start | bytes 6148
  1.9 31.1 %all-to-all-start = ((bf16[32,64,128]{2,1,0:T(8,128)(2,1)}), bf16[32,64,128]{2,1,0:T(8,128)(2,1)S(1)}, u32[]{:S(2)}, u32[]{:S(2)}) async-start(bf16[32,64,128]{2,1,0:T(8,128)(2,1)} %shard_map.64), calls=%async_computation | async-start | bytes 1048576 | tf_op jit(solution)/shard_map/all_to_all | solution.py:231
  15.3 0.7 copy-start.8
  16.7 1.7 %copy-start.2 = (f32[16,4096]{1,0:T(8,128)S(1)}, f32[16,4096]{1,0:T(8,128)}, u32[]{:S(2)}) copy-start(f32[16,4096]{1,0:T(8,128)} %wave_ref.1) | copy-start | bytes 786436
  33.0 0.8 copy-start
  36.3 21.6 %all-to-all-start.1 = ((bf16[32,64,128]{2,1,0:T(8,128)(2,1)}), bf16[32,64,128]{2,1,0:T(8,128)(2,1)S(1)}, u32[]{:S(2)}, u32[]{:S(2)}) async-start(bf16[32,64,128]{2,1,0:T(8,128)(2,1)} %bitcast.8), calls=%async_computation.1 | async-start | bytes 1048576 | tf_op jit(solution)/shard_map/all_to_all | solution.py:249
  40.9 8.1 %collective-permute-start = (f32[8,4096]{1,0:T(8,128)S(1)}, f32[8,4096]{1,0:T(8,128)S(1)}, u32[]{:S(2)}, u32[]{:S(2)}) collective-permute-start(f32[8,4096]{1,0:T(8,128)S(1)} %get-tuple-element.14), channel_id=1, source_target_pairs={{0,1},{1,2},{2,3},{3,4},{4,5},{5,6},{6,7},{7,8},{8,9},{9,10},{10,1... | collective-permute-start | bytes 393224 | tf_op jit(solution)/shard_map/ppermute | solution.py:246
  42.8 7.4 %collective-permute-start.1 = (f32[8,4096]{1,0:T(8,128)S(1)}, f32[8,4096]{1,0:T(8,128)S(1)}, u32[]{:S(2)}, u32[]{:S(2)}) collective-permute-start(f32[8,4096]{1,0:T(8,128)S(1)} %get-tuple-element.15), channel_id=1, source_target_pairs={{1,0},{2,1},{3,2},{4,3},{5,4},{6,5},{7,6},{8,7},{9,8},{10,9},{11,1... | collective-permute-start | bytes 393224 | tf_op jit(solution)/shard_map/ppermute | solution.py:247
  47.7 0.7 copy-start.9
  49.0 11.9 %copy-start.5 = (f32[8,4096]{1,0:T(8,128)}, f32[8,4096]{1,0:T(8,128)S(1)}, u32[]{:S(2)}) copy-start(f32[8,4096]{1,0:T(8,128)S(1)} %collective-permute-done.wbelow_ref) | copy-start | bytes 393220
  50.2 10.8 %copy-start.6 = (f32[8,4096]{1,0:T(8,128)}, f32[8,4096]{1,0:T(8,128)S(1)}, u32[]{:S(2)}) copy-start(f32[8,4096]{1,0:T(8,128)S(1)} %collective-permute-done.1.wabove_ref) | copy-start | bytes 393220
  57.9 0.8 copy-start.1
  61.0 8.9 %collective-permute-start.3 = (f32[2,2,8,4096]{3,2,1,0:T(8,128)}, f32[2,2,8,4096]{3,2,1,0:T(8,128)S(1)}, u32[]{:S(2)}, u32[]{:S(2)}) collective-permute-start(f32[2,2,8,4096]{3,2,1,0:T(8,128)} %get-tuple-element.17.lo_ref), channel_id=1, source_target_pairs={{1,0},{2,1},{3,2},{4,3},{5,4},{6,5},{7,6},{8,7},{9,8},{10,9},{11,1... | collective-permute-start | bytes 1572872 | tf_op jit(solution)/shard_map/ppermute | solution.py:266
  62.9 11.9 %collective-permute-start.2 = (f32[2,2,8,4096]{3,2,1,0:T(8,128)}, f32[2,2,8,4096]{3,2,1,0:T(8,128)S(1)}, u32[]{:S(2)}, u32[]{:S(2)}) collective-permute-start(f32[2,2,8,4096]{3,2,1,0:T(8,128)} %get-tuple-element.18.hi_ref), channel_id=1, source_target_pairs={{0,1},{1,2},{2,3},{3,4},{4,5},{5,6},{6,7},{7,8},{8,9},{9,10},{10,1... | collective-permute-start | bytes 1572872 | tf_op jit(solution)/shard_map/ppermute | solution.py:265
  69.9 4.9 %copy-start.3 = (f32[2,2,8,4096]{3,2,1,0:T(8,128)}, f32[2,2,8,4096]{3,2,1,0:T(8,128)S(1)}, u32[]{:S(2)}) copy-start(f32[2,2,8,4096]{3,2,1,0:T(8,128)S(1)} %collective-permute-done.3.above_ref) | copy-start | bytes 1572868
  74.8 0.8 copy-start.4
